TPU v7x, 32 devices: a whole 2x2x4 slice. The times are simulated.
32 devices in a mesh: freq: 16 (over z, y, core), rows: 2 (over x).
Axes of the slice: x: 2, y: 2, z: 4, core: 2. Of those that a mesh axis runs over, the one named last changes fastest.
Arguments:
- image_cube: float32 [2048, 64, 128], P('freq', 'rows'), may hold values from 0.05 to 2
- data_grad: float32 [2048, 64, 128], P('freq', 'rows'), may hold values from -4 to 4
- space_duals: float32 [4, 2048, 64, 128], P(None, 'freq', 'rows'), may hold values from -0.5 to 0.5
- freq_duals: float32 [8192, 2048], P(('rows', 'freq')), may hold values from -1 to 1
Outputs:
- image_next: float32 [2048, 64, 128], P('freq', 'rows')
- space_next: float32 [4, 2048, 64, 128], P(None, 'freq', 'rows')
- freq_next: float32 [8192, 2048], P(('rows', 'freq'))
All inputs are finite; a program needn't handle non-finite values.
Results may differ from a plain program's by a relative error of at most 0.00008.
Values sent between devices are 32-bit elements; how exact they have to be, the bound alone decides.
No kernel may reach another device: no remote copies, remote signals or barrier semaphores. Data moves between devices by JAX's collectives and lax.ppermute only.
A program may use at most 128 MiB of HBM per device.

v0:
```python
import math

import jax
import jax.numpy as jnp
from jax import lax
from jax.sharding import PartitionSpec as P
from jax.experimental import pallas as pl
from jax.experimental.pallas import tpu as pltpu

SCALES = 4


TAPS = (0.0625, 0.25, 0.375, 0.25, 0.0625)
SIGMA = 0.5
TAU_STEP = 0.5
SPACE_BOUND = 0.5
FREQ_BOUND = 1.0
CHUNK = 8
GROUPS = 4


def padded_2(cells, sides, width):
    for axis, dim in sides:
        count = lax.axis_size(axis)
        ends = count - 1
        head = lax.slice_in_dim(cells, 0, width, axis=dim)
        tail = lax.slice_in_dim(cells, cells.shape[dim] - width, cells.shape[dim], axis=dim)
        cells = jnp.concatenate(
            [
                lax.ppermute(tail, axis, [(i, (i + 1) % count) for i in range(ends)]),
                cells,
                lax.ppermute(head, axis, [((i + 1) % count, i) for i in range(ends)]),
            ],
            axis=dim,
        )
    return cells


def blur_rows(padded, dilation, out_rows):
    running = TAPS[0] * padded[:, 0:out_rows, :]
    for tap_idx in range(1, 5):
        offset = tap_idx * dilation
        running = running + TAPS[tap_idx] * padded[:, offset : offset + out_rows, :]
    return running


def blur_cols(planar, dilation):
    columns = planar.shape[2]
    reach_cols = 2 * dilation
    padded = jnp.pad(planar, ((0, 0), (0, 0), (reach_cols, reach_cols)))
    running = TAPS[0] * padded[:, :, 0:columns]
    for tap_idx in range(1, 5):
        offset = tap_idx * dilation
        running = running + TAPS[tap_idx] * padded[:, :, offset : offset + columns]
    return running


def inside_rows(margin, local_rows):
    first_row = lax.axis_index("rows") * local_rows - margin
    positions = first_row + jnp.arange(local_rows + 2 * margin, dtype=jnp.int32)
    limit = local_rows * lax.axis_size("rows")
    return ((positions >= 0) & (positions < limit)).astype(jnp.float32)[None, :, None]


def analyse(image_cube):
    local_rows = image_cube.shape[1]
    details = []
    depth = 2 ** (SCALES + 1) - 2
    current = padded_2(image_cube, (("rows", 1),), depth)
    inside = inside_rows(depth, local_rows)
    margin = depth
    for level_idx in range(SCALES):
        dilation = 2**level_idx
        reach_rows = 2 * dilation
        new_margin = margin - reach_rows
        out_rows = local_rows + 2 * new_margin
        start_row = depth - new_margin
        smoothed = blur_cols(blur_rows(current, dilation, out_rows), dilation)
        smoothed = smoothed * inside[:, start_row : start_row + out_rows, :]
        kept = current[:, reach_rows : reach_rows + out_rows, :] - smoothed
        details.append(kept[:, new_margin : new_margin + local_rows, :])
        current = smoothed
        margin = new_margin
    return details


def synthesise(space_next):
    local_rows = space_next.shape[2]
    running = jnp.zeros_like(space_next[0])
    for level_idx in reversed(range(SCALES)):
        dilation = 2**level_idx
        operand = running - space_next[level_idx]
        padded = padded_2(operand, (("rows", 1),), 2 * dilation)
        running = (
            blur_cols(blur_rows(padded, dilation, local_rows), dilation) + space_next[level_idx]
        )
    return running


def dct_table(length):
    split = 64 if length % 64 == 0 else 1
    groups = length // split
    period = 4 * length
    coef_idx = jnp.arange(length, dtype=jnp.int32)
    scale = math.pi / (2 * length)
    outer_phase = (coef_idx[:, None] * (2 * split * jnp.arange(groups, dtype=jnp.int32))[None, :]) % period
    inner_phase = (coef_idx[:, None] * (2 * jnp.arange(split, dtype=jnp.int32) + 1)[None, :]) % period
    outer_angle = outer_phase.astype(jnp.float32) * scale
    inner_angle = inner_phase.astype(jnp.float32) * scale
    weights = jnp.where(
        coef_idx == 0, math.sqrt(1.0 / length), math.sqrt(2.0 / length)
    ).astype(jnp.float32)[:, None, None]
    table = (
        jnp.cos(outer_angle)[:, :, None] * jnp.cos(inner_angle)[:, None, :]
        - jnp.sin(outer_angle)[:, :, None] * jnp.sin(inner_angle)[:, None, :]
    ) * weights
    return table.reshape(length, length)


def spectral(pixel_cube, freq_duals):
    chans_all, pixel_count = pixel_cube.shape
    precision = lax.Precision.HIGH
    table = dct_table(chans_all)
    coeffs = lax.dot_general(
        pixel_cube,
        table,
        (((0,), (1,)), ((), ())),
        precision=precision,
        preferred_element_type=jnp.float32,
    )
    freq_next = jnp.clip(freq_duals + SIGMA * coeffs, -FREQ_BOUND, FREQ_BOUND)
    return table, freq_next


def spectral_back(table, freq_next):
    precision = lax.Precision.HIGH
    return lax.dot_general(
        table,
        freq_next,
        (((0,), (1,)), ((), ())),
        precision=precision,
        preferred_element_type=jnp.float32,
    )


def starlet_kernel(flags_ref, above_ref, own_ref, below_ref, duals_ref, *refs):
    sn_ref, send_ref, mid_ref, keep_ref, buf_a, buf_b = refs[-6:]
    block, local_rows, columns = own_ref.shape
    halo = send_ref.shape[0]
    extent = 2 * halo + local_rows
    pad = 2 ** SCALES
    row0 = flags_ref[0] - halo
    total_rows = flags_ref[1]
    lane = lax.broadcasted_iota(jnp.int32, (1, block, columns), 2)
    weights = {}
    for level_idx in range(SCALES):
        dilation = 2**level_idx
        weights[dilation] = tuple(
            jnp.where(keep, tap, 0.0).astype(jnp.float32)
            for step, tap in ((dilation, TAPS[1]), (2 * dilation, TAPS[0]))
            for keep in (lane >= step, lane < columns - step)
        )

    def smooth_rows(src, dst, dilation, lo, hi):
        near_w, far_w = weights[dilation][0:2], weights[dilation][2:4]
        for start in range(lo, hi, CHUNK):
            size = min(CHUNK, hi - start)
            at = start + pad

            def window(offset):
                return src[pl.ds(at + offset, size)]

            y = TAPS[0] * (window(-2 * dilation) + window(2 * dilation)) + TAPS[1] * (
                window(-dilation) + window(dilation)
            ) + TAPS[2] * window(0)
            z = (
                pltpu.roll(y, dilation, 2) * near_w[0]
                + pltpu.roll(y, columns - dilation, 2) * near_w[1]
                + pltpu.roll(y, 2 * dilation, 2) * far_w[0]
                + pltpu.roll(y, columns - 2 * dilation, 2) * far_w[1]
                + TAPS[2] * y
            )
            if start >= halo and start + size <= halo + local_rows:
                dst[pl.ds(at, size)] = z
            else:
                row = row0 + start + lax.broadcasted_iota(jnp.int32, (size, 1, 1), 0)
                dst[pl.ds(at, size)] = jnp.where((row >= 0) & (row < total_rows), z, 0.0)

    def rows_major(value):
        return jnp.swapaxes(value, 0, 1)

    buf_a[...] = jnp.zeros_like(buf_a)
    above = rows_major(above_ref[...])[local_rows - halo :]
    below = rows_major(below_ref[...])[:halo]
    buf_a[pl.ds(pad, halo)] = jnp.where(flags_ref[2] > 0, above, 0.0)
    buf_a[pl.ds(pad + halo, local_rows)] = rows_major(own_ref[...])
    buf_a[pl.ds(pad + halo + local_rows, halo)] = jnp.where(flags_ref[3] > 0, below, 0.0)
    bufs = (buf_a, buf_b)
    own = pl.ds(pad + halo, local_rows)
    fresh = []
    lo, hi = 0, extent
    for level_idx in range(SCALES):
        dilation = 2**level_idx
        src, dst = bufs[level_idx % 2], bufs[(level_idx + 1) % 2]
        lo, hi = lo + 2 * dilation, hi - 2 * dilation
        smooth_rows(src, dst, dilation, lo, hi)
        plane = jnp.clip(
            duals_ref[level_idx] + SIGMA * rows_major(src[own] - dst[own]), -SPACE_BOUND, SPACE_BOUND
        )
        sn_ref[level_idx] = plane

    buf_a[...] = jnp.zeros_like(buf_a)
    buf_b[...] = jnp.zeros_like(buf_b)
    lo, hi = halo, halo + local_rows
    for count, level_idx in enumerate(reversed(range(SCALES))):
        dilation = 2**level_idx
        src, dst = bufs[count % 2], bufs[(count + 1) % 2]
        plane = rows_major(sn_ref[level_idx])
        src[own] = src[own] - plane
        lo, hi = lo - 2 * dilation, hi + 2 * dilation
        smooth_rows(src, dst, dilation, max(lo, 0), min(hi, extent))
        dst[own] = dst[own] + plane
    top = dst[pl.ds(pad, halo)]
    bot = dst[pl.ds(pad + halo + local_rows, halo)]
    swap = flags_ref[4] > 0
    send_ref[...] = jnp.where(swap, bot, top)
    keep_ref[...] = jnp.where(swap, top, bot)
    mid_ref[...] = rows_major(dst[own])


def starlet(flags, above, own, below, duals, halo, group, groups, carry=(), interpret=False):
    chans, local_rows, columns = own.shape
    block = math.gcd(chans, 8)
    steps = chans // block // groups
    base = group * steps
    extent = 2 * halo + local_rows + 2 * 2**SCALES
    near_spec = pl.BlockSpec((block, local_rows, columns), lambda i: (i, 0, 0))
    own_spec = pl.BlockSpec((block, local_rows, columns), lambda i: (i + base, 0, 0))
    dual_spec = pl.BlockSpec((SCALES, block, local_rows, columns), lambda i: (0, i + base, 0, 0))
    edge_spec = pl.BlockSpec((halo, block, columns), lambda i: (0, i, 0))
    edge_shape = jax.ShapeDtypeStruct((halo, chans // groups, columns), jnp.float32)
    carry_specs = [pl.BlockSpec(memory_space=pl.ANY)] * len(carry)
    return pl.pallas_call(
        starlet_kernel,
        grid=(steps,),
        in_specs=[pl.BlockSpec(memory_space=pltpu.SMEM), near_spec, own_spec, near_spec, dual_spec] + carry_specs,
        out_specs=[dual_spec, edge_spec, own_spec, edge_spec],
        out_shape=[
            jax.ShapeDtypeStruct(duals.shape, jnp.float32),
            edge_shape,
            jax.ShapeDtypeStruct(own.shape, jnp.float32),
            edge_shape,
        ],
        scratch_shapes=[pltpu.VMEM((extent, block, columns), jnp.float32)] * 2,
        input_output_aliases={5: 0, 6: 2} if carry else {},
        interpret=interpret,
    )(flags, above, own, below, duals, *carry)


def row_plan(chans, local_rows):
    halo = 2 ** (SCALES + 1) - 2
    assert local_rows >= halo
    block = math.gcd(chans, 8)
    groups = math.gcd(chans // block, GROUPS)
    return halo, groups, chans // groups


def exchange_halos(image_cube):
    chans, local_rows, columns = image_cube.shape
    halo, groups, width = row_plan(chans, local_rows)
    count = lax.axis_size("rows")
    down = [(i, i + 1) for i in range(count - 1)]
    up = [(i + 1, i) for i in range(count - 1)]
    halos = []
    for group in range(groups):
        part = image_cube[group * width : (group + 1) * width]
        if count == 2:
            got = lax.ppermute(part, "rows", down + up)
            halos.append((got, got))
        else:
            halos.append((lax.ppermute(part, "rows", down), lax.ppermute(part, "rows", up)))
    return halos


def spatial(halos, image_cube, space_duals):
    chans, local_rows, columns = image_cube.shape
    halo, groups, width = row_plan(chans, local_rows)
    count = lax.axis_size("rows")
    index = lax.axis_index("rows")
    down = [(i, i + 1) for i in range(count - 1)]
    up = [(i + 1, i) for i in range(count - 1)]
    paired = count == 2
    flags = jnp.stack(
        [index * local_rows, count * local_rows, index > 0, index < count - 1, paired & (index == 0)]
    ).astype(jnp.int32)
    carry = ()
    sends, keeps = [], []
    for group, (above, below) in enumerate(halos):
        space_next, send, mid, keep = starlet(flags, above, image_cube, below, space_duals, halo, group, groups, carry)
        carry = (space_next, mid)
        if paired:
            sends.append(lax.ppermute(send, "rows", down + up))
        else:
            sends.append(lax.ppermute(send, "rows", up))
            keeps.append(lax.ppermute(keep, "rows", down))
    got = jnp.concatenate(sends, axis=1)
    gap = local_rows - halo
    if paired:
        spill = jnp.where(
            index == 0,
            jnp.pad(got, ((gap, 0), (0, 0), (0, 0))),
            jnp.pad(got, ((0, gap), (0, 0), (0, 0))),
        )
    else:
        spill = jnp.pad(jnp.concatenate(keeps, axis=1), ((0, gap), (0, 0), (0, 0))) + jnp.pad(
            got, ((gap, 0), (0, 0), (0, 0))
        )
    return mid + jnp.transpose(spill, (1, 0, 2)), space_next


def local(image_cube, data_grad, space_duals, freq_duals):
    chans, local_rows, columns = image_cube.shape
    peers = lax.axis_size("freq")
    share = local_rows * columns // peers
    pieces = image_cube.reshape(chans, peers, share)
    halos = exchange_halos(image_cube)
    pixel_cube = lax.all_to_all(pieces, "freq", split_axis=1, concat_axis=0, tiled=True).reshape(
        chans * peers, share
    )
    pixel_cube, halos = lax.optimization_barrier((pixel_cube, halos))
    table, freq_next = spectral(pixel_cube, freq_duals)
    spectral_sum = spectral_back(table, freq_next)
    spectral_sum, halos = lax.optimization_barrier((spectral_sum, halos))
    returned = lax.all_to_all(
        spectral_sum.reshape(peers, chans, share),
        "freq",
        split_axis=0,
        concat_axis=2,
        tiled=True,
    )
    space_term, space_next = spatial(halos, image_cube, space_duals)
    spectral_term = returned.reshape(chans, local_rows, columns)
    image_next = jnp.maximum(image_cube - TAU_STEP * (data_grad + space_term + spectral_term), 0.0)
    return (image_next, space_next, freq_next)


def solution(mesh):
    in_specs = (
        P("freq", "rows", None),
        P("freq", "rows", None),
        P(None, "freq", "rows", None),
        P(("rows", "freq"), None),
    )
    out_specs = (P("freq", "rows", None), P(None, "freq", "rows", None), P(("rows", "freq"), None))
    return jax.shard_map(local, mesh=mesh, in_specs=in_specs, out_specs=out_specs, check_vma=False)
```

profile of v0, /device:TPU:13, one launch (start us, length us, event | category | flops | bytes accessed | tf_op | source)
XLA Modules:
  0.0 175.6 jit_solution(14847924339420970046)
XLA Ops:
  0.6 3.0 %copy.30 = f32[128,32,128]{0,2,1:T(8,128)} copy(f32[128,32,128]{2,1,0:T(8,128)} %own_ref.7) | data formatting | bytes 4194304 | tf_op args[0]
  3.6 6.7 %all-to-all-start = ((f32[128,16,256]{0,2,1:T(8,128)}), f32[128,16,256]{0,2,1:T(8,128)}, u32[]{:S(2)}, u32[]{:S(2)}) async-start(f32[128,16,256]{0,2,1:T(8,128)} %bitcast.34), calls=%async_computation | async-start | bytes 4194304 | tf_op jit(solution)/shard_map/all_to_all | solution.py:327
  10.3 1.4 fusion.24
  11.7 1.2 collective-permute-start
  12.9 0.3 collective-permute-start.1
  13.2 1.2 collective-permute-start.2
  14.3 0.3 collective-permute-start.3
  14.6 1.1 fusion.22
  15.7 2.1 %fusion.17 = (f32[2048,64]{0,1:T(8,128)S(1)}, f32[2048,64]{0,1:T(8,128)S(1)}) fusion(s32[64]{0:T(128)S(1)} %multiply_add_fusion), kind=kLoop, calls=%fused_computation.27 | loop fusion | flops 1835008 | bytes 1048832 | tf_op jit(solution)/shard_map/cos | solution.py:114
  17.8 8.2 %multiply_subtract_fusion = f32[2048,32,64]{0,2,1:T(8,128)} fusion(f32[2048,64]{0,1:T(8,128)S(1)} %get-tuple-element.70, f32[2048,32]{0,1:T(8,128)S(1)} %get-tuple-element.68, f32[2048,64]{0,1:T(8,128)S(1)} %get-tuple-element.69, f32[2048,32]{0,1:T(8,128)S(1)} %get-tuple-element.67), kind=kLoop, calls=%fused_computation.1 | loop fusion | flops 12582912 | bytes 18350080 | tf_op jit(solution)/shard_map/sub | solution.py:114
  26.1 11.9 %bitcast_multiply_fusion = f32[2048,2048]{0,1:T(8,128)} fusion(f32[2048,32,64]{0,2,1:T(8,128)} %multiply_subtract_fusion, f32[2048]{0:T(1024)S(1)} %fusion.23), kind=kLoop, calls=%fused_computation | loop fusion | flops 4194304 | bytes 33562624 | tf_op jit(solution)/shard_map/mul | solution.py:113
  37.9 20.1 %all-to-all-done = f32[128,16,256]{0,2,1:T(8,128)} async-done(((f32[128,16,256]{0,2,1:T(8,128)}), f32[128,16,256]{0,2,1:T(8,128)}, u32[]{:S(2)}, u32[]{:S(2)}) %all-to-all-start) | async-done | bytes 2097184 | tf_op jit(solution)/shard_map/all_to_all | solution.py:327
  58.0 1.9 %copy.31 = f32[16,128,1,256]{3,1,0,2:T(8,128)S(1)} copy(f32[16,128,1,256]{1,3,0,2:T(8,128)} %bitcast.7) | data formatting | bytes 4194304 | tf_op jit(solution)/shard_map/all_to_all | solution.py:327
  59.9 0.0 collective-permute-done.above_ref.below_ref
  59.9 0.0 collective-permute-done.1.above_ref.below_ref
  59.9 0.0 collective-permute-done.2.above_ref.below_ref
  60.0 0.0 collective-permute-done.3.above_ref.below_ref
  60.0 13.4 %fusion.1 = f32[256,2048]{1,0:T(8,128)S(1)} fusion(f32[256,2048]{1,0:T(8,128)} %param.7, f32[2048,256]{1,0:T(8,128)S(1)} %bitcast.35, f32[2048,2048]{0,1:T(8,128)} %bitcast_multiply_fusion), kind=kOutput, calls=%fused_computation.4 | convolution fusion | flops 6444023808 | bytes 23068672 | tf_op jit(solution)/shard_map/dot_general | solution.py:124
  73.5 0.0 copy-done
  73.5 0.0 copy-start.3
  73.5 8.5 %fusion.25 = f32[2048,256]{1,0:T(8,128)} fusion(f32[2048,2048]{0,1:T(8,128)S(1)} %copy-done, f32[256,2048]{1,0:T(8,128)S(1)} %fusion.1), kind=kOutput, calls=%fused_computation.42 | convolution fusion | flops 6442450944 | bytes 20971520 | tf_op jit(solution)/shard_map/dot_general | solution.py:137
  82.0 5.6 %all-to-all-start.1 = ((f32[16,128,256]{2,1,0:T(8,128)}), f32[16,128,256]{2,1,0:T(8,128)S(1)}, u32[]{:S(2)}, u32[]{:S(2)}) async-start(f32[16,128,256]{2,1,0:T(8,128)} %bitcast.10), calls=%async_computation.1 | async-start | bytes 4194304 | tf_op jit(solution)/shard_map/all_to_all | solution.py:334
  87.6 0.7 stack.31.flags_ref
  88.3 13.1 %shard_map.67 = (f32[4,128,32,128]{3,2,1,0:T(8,128)}, f32[30,32,128]{2,1,0:T(8,128)}, f32[128,32,128]{2,1,0:T(8,128)}, f32[30,32,128]{2,1,0:T(8,128)}) custom-call(s32[5]{0:T(128)} %stack.31.flags_ref, f32[32,32,128]{2,1,0:T(8,128)} %collective-permute-done.above_ref.below_ref, f32[128,32,128]{2,1,0:T(8,128)} %own_ref.7, ...), custom_call_target="tpu_custom_call" | custom-call | tf_op jit(solution)/shard_map/pallas_call | solution.py:243
  101.3 1.3 copy.32
  102.7 1.3 collective-permute-start.4
  103.9 13.1 %shard_map.68 = (f32[4,128,32,128]{3,2,1,0:T(8,128)}, f32[30,32,128]{2,1,0:T(8,128)}, f32[128,32,128]{2,1,0:T(8,128)}, f32[30,32,128]{2,1,0:T(8,128)}) custom-call(s32[5]{0:T(128)} %stack.31.flags_ref, f32[32,32,128]{2,1,0:T(8,128)} %collective-permute-done.1.above_ref.below_ref, ...), custom_call_target="tpu_custom_call", output_to_operand_aliasing={{0}: (5, {}), {2}: (6, {})} | custom-call | tf_op jit(solution)/shard_map/pallas_call | solution.py:243
  117.1 2.1 %copy.33 = f32[30,32,128]{2,0,1:T(8,128)} copy(f32[30,32,128]{2,1,0:T(8,128)} %get-tuple-element.58) | data formatting | bytes 983040 | tf_op jit(solution)/shard_map/pallas_call | solution.py:243
  119.2 0.3 collective-permute-start.5
  119.4 13.1 %shard_map.69 = (f32[4,128,32,128]{3,2,1,0:T(8,128)}, f32[30,32,128]{2,1,0:T(8,128)}, f32[128,32,128]{2,1,0:T(8,128)}, f32[30,32,128]{2,1,0:T(8,128)}) custom-call(s32[5]{0:T(128)} %stack.31.flags_ref, f32[32,32,128]{2,1,0:T(8,128)} %copy-done.5, f32[128,32,128]{2,1,0:T(8,128)} %own_ref.7, ...), custom_call_target="tpu_custom_call", output_to_operand_aliasing={{0}: (5, {}), {2}: (6, {})} | custom-call | tf_op jit(solution)/shard_map/pallas_call | solution.py:243
  132.6 2.1 %copy.34 = f32[30,32,128]{2,0,1:T(8,128)} copy(f32[30,32,128]{2,1,0:T(8,128)} %get-tuple-element.59) | data formatting | bytes 983040 | tf_op jit(solution)/shard_map/pallas_call | solution.py:243
  134.7 1.2 collective-permute-start.6
  135.9 13.1 %shard_map.70 = (f32[4,128,32,128]{3,2,1,0:T(8,128)}, f32[30,32,128]{2,1,0:T(8,128)}, f32[128,32,128]{2,1,0:T(8,128)}, f32[30,32,128]{2,1,0:T(8,128)}) custom-call(s32[5]{0:T(128)} %stack.31.flags_ref, f32[32,32,128]{2,1,0:T(8,128)} %copy-done.4, f32[128,32,128]{2,1,0:T(8,128)} %own_ref.7, ...), custom_call_target="tpu_custom_call", output_to_operand_aliasing={{0}: (5, {}), {2}: (6, {})} | custom-call | tf_op jit(solution)/shard_map/pallas_call | solution.py:243
  149.0 1.3 copy.35
  150.3 0.5 collective-permute-start.7
  150.8 0.0 collective-permute-done.4
  150.8 0.8 constant_dynamic-update-slice_fusion.3
  151.6 0.0 collective-permute-done.5
  151.6 1.9 %constant_dynamic-update-slice_fusion.2 = f32[30,128,128]{2,0,1:T(8,128)} fusion(f32[30,128,128]{2,0,1:T(8,128)} %constant_dynamic-update-slice_fusion.3, f32[30,32,128]{2,0,1:T(8,128)} %collective-permute-done.5), kind=kLoop, calls=%fused_computation.35 | loop fusion | bytes 1048576
  153.5 0.0 collective-permute-done.6
  153.5 1.9 %constant_dynamic-update-slice_fusion.1 = f32[30,128,128]{2,0,1:T(8,128)} fusion(f32[30,128,128]{2,0,1:T(8,128)} %constant_dynamic-update-slice_fusion.2, f32[30,32,128]{2,0,1:T(8,128)} %collective-permute-done.6), kind=kLoop, calls=%fused_computation.34 | loop fusion | bytes 1048576
  155.4 7.2 %collective-permute-done.7 = f32[30,32,128]{2,0,1:T(8,128)S(1)} collective-permute-done((f32[30,32,128]{2,0,1:T(8,128)S(1)}, f32[30,32,128]{2,0,1:T(8,128)S(1)}, u32[]{:S(2)}, u32[]{:S(2)}) %collective-permute-start.7) | collective-permute-done | bytes 491552 | tf_op jit(solution)/shard_map/ppermute | solution.py:302
  162.6 0.8 constant_dynamic-update-slice_fusion
  163.4 0.0 all-to-all-done.1
  163.4 2.5 %copy.36 = f32[1,128,16,256]{3,2,1,0:T(8,128)} copy(f32[1,128,16,256]{3,1,2,0:T(8,128)S(1)} %bitcast.33) | data formatting | bytes 4194304 | tf_op jit(solution)/shard_map/all_to_all | solution.py:334
  166.0 2.8 %reshape.143 = f32[128,32,128]{2,1,0:T(8,128)} reshape(f32[1,128,16,256]{3,2,1,0:T(8,128)} %copy.36) | data formatting | bytes 4194304 | tf_op jit(solution)/shard_map/reshape | solution.py:342
  168.7 0.0 copy-done.2
  168.7 6.8 %fusion.6 = f32[128,32,128]{2,1,0:T(8,128)} fusion(f32[128,32,128]{2,1,0:T(8,128)S(1)} %copy-done.2, f32[128,32,128]{2,1,0:T(8,128)} %reshape.143, f32[128,32,128]{2,1,0:T(8,128)} %param.5, f32[128,32,128]{2,1,0:T(8,128)} %get-tuple-element.56, f32[30,128,128]{2,0,1:T(8,128)} %constant_dynamic-update-slice_fusion, pred[]{:T(512)S(6)} %eq.20), kind=kLoop, calls=%fused_computation.10 | loop fusion | flops 3670016 | bytes 12451841 | tf_op jit(solution)/shard_map/max | solution.py:343
  (12 shorter events, 0.0 us)
Async XLA Ops:
  3.6 6.7 %copy-start.1 = (f32[128,32,128]{2,1,0:T(8,128)S(1)}, f32[128,32,128]{2,1,0:T(8,128)}, u32[]{:S(2)}) copy-start(f32[128,32,128]{2,1,0:T(8,128)} %own_ref.7) | copy-start | bytes 6291460
  3.6 54.4 %all-to-all-start = ((f32[128,16,256]{0,2,1:T(8,128)}), f32[128,16,256]{0,2,1:T(8,128)}, u32[]{:S(2)}, u32[]{:S(2)}) async-start(f32[128,16,256]{0,2,1:T(8,128)} %bitcast.34), calls=%async_computation | async-start | bytes 4194304 | tf_op jit(solution)/shard_map/all_to_all | solution.py:327
  11.7 48.3 %collective-permute-start = (f32[32,32,128]{2,1,0:T(8,128)}, f32[32,32,128]{2,1,0:T(8,128)}, u32[]{:S(2)}, u32[]{:S(2)}) collective-permute-start(f32[32,32,128]{2,1,0:T(8,128)} %get-tuple-element.66), channel_id=1, source_target_pairs={{0,1},{1,0},{2,3},{3,2},{4,5},{5,4},{6,7},{7,6},{8,9},{9,8},{10,11... | collective-permute-start | bytes 1572872 | tf_op jit(solution)/shard_map/ppermute | solution.py:278
  12.9 47.1 %collective-permute-start.1 = (f32[32,32,128]{2,1,0:T(8,128)}, f32[32,32,128]{2,1,0:T(8,128)}, u32[]{:S(2)}, u32[]{:S(2)}) collective-permute-start(f32[32,32,128]{2,1,0:T(8,128)} %get-tuple-element.65), channel_id=1, source_target_pairs={{0,1},{1,0},{2,3},{3,2},{4,5},{5,4},{6,7},{7,6},{8,9},{9,8},{10,11... | collective-permute-start | bytes 1572872 | tf_op jit(solution)/shard_map/ppermute | solution.py:278
  13.2 46.8 %collective-permute-start.2 = (f32[32,32,128]{2,1,0:T(8,128)}, f32[32,32,128]{2,1,0:T(8,128)S(1)}, u32[]{:S(2)}, u32[]{:S(2)}) collective-permute-start(f32[32,32,128]{2,1,0:T(8,128)} %get-tuple-element.64), channel_id=1, source_target_pairs={{0,1},{1,0},{2,3},{3,2},{4,5},{5,4},{6,7},{7,6},{8,9},{9,8},{10,11... | collective-permute-start | bytes 1572872 | tf_op jit(solution)/shard_map/ppermute | solution.py:278
  14.3 45.6 %collective-permute-start.3 = (f32[32,32,128]{2,1,0:T(8,128)}, f32[32,32,128]{2,1,0:T(8,128)S(1)}, u32[]{:S(2)}, u32[]{:S(2)}) collective-permute-start(f32[32,32,128]{2,1,0:T(8,128)} %get-tuple-element.63), channel_id=1, source_target_pairs={{0,1},{1,0},{2,3},{3,2},{4,5},{5,4},{6,7},{7,6},{8,9},{9,8},{10,11... | collective-permute-start | bytes 1572872 | tf_op jit(solution)/shard_map/ppermute | solution.py:278
  60.0 13.5 %copy-start.5 = (f32[32,32,128]{2,1,0:T(8,128)}, f32[32,32,128]{2,1,0:T(8,128)S(1)}, u32[]{:S(2)}) copy-start(f32[32,32,128]{2,1,0:T(8,128)S(1)} %collective-permute-done.2.above_ref.below_ref) | copy-start | bytes 1572868
  60.0 13.5 %copy-start.4 = (f32[32,32,128]{2,1,0:T(8,128)}, f32[32,32,128]{2,1,0:T(8,128)S(1)}, u32[]{:S(2)}) copy-start(f32[32,32,128]{2,1,0:T(8,128)S(1)} %collective-permute-done.3.above_ref.below_ref) | copy-start | bytes 1572868
  60.0 13.5 %copy-start = (f32[2048,2048]{0,1:T(8,128)S(1)}, f32[2048,2048]{0,1:T(8,128)}, u32[]{:S(2)}) copy-start(f32[2048,2048]{0,1:T(8,128)} %bitcast_multiply_fusion) | copy-start | bytes 50331652
  73.5 8.6 %copy-start.3 = (f32[256,2048]{1,0:T(8,128)}, f32[256,2048]{1,0:T(8,128)S(1)}, u32[]{:S(2)}) copy-start(f32[256,2048]{1,0:T(8,128)S(1)} %fusion.1) | copy-start | bytes 6291460
  82.0 81.4 %all-to-all-start.1 = ((f32[16,128,256]{2,1,0:T(8,128)}), f32[16,128,256]{2,1,0:T(8,128)S(1)}, u32[]{:S(2)}, u32[]{:S(2)}) async-start(f32[16,128,256]{2,1,0:T(8,128)} %bitcast.10), calls=%async_computation.1 | async-start | bytes 4194304 | tf_op jit(solution)/shard_map/all_to_all | solution.py:334
  102.7 48.1 %collective-permute-start.4 = (f32[30,32,128]{2,0,1:T(8,128)S(1)}, f32[30,32,128]{2,0,1:T(8,128)S(1)}, u32[]{:S(2)}, u32[]{:S(2)}) collective-permute-start(f32[30,32,128]{2,0,1:T(8,128)S(1)} %copy.32), channel_id=1, source_target_pairs={{0,1},{1,0},{2,3},{3,2},{4,5},{5,4},{6,7},{7,6},{8,9},{9,8},{10,11... | collective-permute-start | bytes 1474568 | tf_op jit(solution)/shard_map/ppermute | solution.py:302
  119.2 32.4 %collective-permute-start.5 = (f32[30,32,128]{2,0,1:T(8,128)}, f32[30,32,128]{2,0,1:T(8,128)}, u32[]{:S(2)}, u32[]{:S(2)}) collective-permute-start(f32[30,32,128]{2,0,1:T(8,128)} %copy.33), channel_id=1, source_target_pairs={{0,1},{1,0},{2,3},{3,2},{4,5},{5,4},{6,7},{7,6},{8,9},{9,8},{10,11... | collective-permute-start | bytes 1474568 | tf_op jit(solution)/shard_map/ppermute | solution.py:302
  134.7 18.8 %collective-permute-start.6 = (f32[30,32,128]{2,0,1:T(8,128)}, f32[30,32,128]{2,0,1:T(8,128)}, u32[]{:S(2)}, u32[]{:S(2)}) collective-permute-start(f32[30,32,128]{2,0,1:T(8,128)} %copy.34), channel_id=1, source_target_pairs={{0,1},{1,0},{2,3},{3,2},{4,5},{5,4},{6,7},{7,6},{8,9},{9,8},{10,11... | collective-permute-start | bytes 1474568 | tf_op jit(solution)/shard_map/ppermute | solution.py:302
  150.3 12.3 %collective-permute-start.7 = (f32[30,32,128]{2,0,1:T(8,128)S(1)}, f32[30,32,128]{2,0,1:T(8,128)S(1)}, u32[]{:S(2)}, u32[]{:S(2)}) collective-permute-start(f32[30,32,128]{2,0,1:T(8,128)S(1)} %copy.35), channel_id=1, source_target_pairs={{0,1},{1,0},{2,3},{3,2},{4,5},{5,4},{6,7},{7,6},{8,9},{9,8},{10,11... | collective-permute-start | bytes 1474568 | tf_op jit(solution)/shard_map/ppermute | solution.py:302
  166.0 2.8 %copy-start.2 = (f32[128,32,128]{2,1,0:T(8,128)S(1)}, f32[128,32,128]{2,1,0:T(8,128)}, u32[]{:S(2)}) copy-start(f32[128,32,128]{2,1,0:T(8,128)} %own_ref.7) | copy-start | bytes 6291460
where the time goes:
time: 179 us; the launch traced here: 176 us
  Pallas kernels  52.4 us (29%)
  other arithmetic  30.1 us (17%)
  waiting for transfers between devices  27.3 us (15%)
  local copies, waits for them, and re-layouts  24.6 us (14%)
  matrix products  22 us (12%)
  starting transfers between devices  18.4 us (10%)
    pallas_call x4, Pallas kernels, starlet(): pl.pallas_call(starlet_kernel, grid=(steps,), in_specs=[pl.BlockSpec(memo...  52.4 us
    all_to_all x1, waiting for transfers between devices, local(): lax.all_to_all(pieces, 'freq', split_axis=1, concat_axis=0, tiled=True)  20.1 us
    dot_general x1, matrix products, spectral(): lax.dot_general(pixel_cube, table, (((0,), (1,)), ((), ())), precision=pr...  13.4 us
    mul x1, other arithmetic, dct_table(): (jnp.cos(outer_angle)[:, :, None] * jnp.cos(inner_angle)[:, None, :] - jn...  11.9 us
    dot_general x1, matrix products, spectral_back(): lax.dot_general(table, freq_next, (((0,), (1,)), ((), ())), precision=pre...  8.54 us
    sub x1, other arithmetic, dct_table(): jnp.cos(outer_angle)[:, :, None] * jnp.cos(inner_angle)[:, None, :]  8.24 us
    unnamed x16, local copies, waits for them, and re-layouts  7.58 us
    ppermute x4, waiting for transfers between devices, spatial(): sends.append(lax.ppermute(send, 'rows', down + up))  7.24 us
  transfers between devices with their start and end apart: 10, of which 2 were waited for; matrix products, arithmetic and copies ran while one was open for 23% of the time, Pallas kernels for 30%

commit v1 on v0

--- a/solution.py
+++ b/solution.py
@@ -97,11 +97,15 @@
     return running
 
 
-def dct_table(length):
-    split = 64 if length % 64 == 0 else 1
-    groups = length // split
+def dct_table(length, parity=None):
+    half = length if parity is None else length // 2
+    split = 64 if half % 64 == 0 else 1
+    groups = half // split
     period = 4 * length
-    coef_idx = jnp.arange(length, dtype=jnp.int32)
+    if parity is None:
+        coef_idx = jnp.arange(length, dtype=jnp.int32)
+    else:
+        coef_idx = 2 * jnp.arange(half, dtype=jnp.int32) + parity
     scale = math.pi / (2 * length)
     outer_phase = (coef_idx[:, None] * (2 * split * jnp.arange(groups, dtype=jnp.int32))[None, :]) % period
     inner_phase = (coef_idx[:, None] * (2 * jnp.arange(split, dtype=jnp.int32) + 1)[None, :]) % period
@@ -114,33 +118,53 @@
         jnp.cos(outer_angle)[:, :, None] * jnp.cos(inner_angle)[:, None, :]
         - jnp.sin(outer_angle)[:, :, None] * jnp.sin(inner_angle)[:, None, :]
     ) * weights
-    return table.reshape(length, length)
+    return table.reshape(coef_idx.shape[0], half)
+
+
+def forward_dot(samples, table):
+    return lax.dot_general(
+        samples,
+        table,
+        (((0,), (1,)), ((), ())),
+        precision=lax.Precision.HIGH,
+        preferred_element_type=jnp.float32,
+    )
 
 
 def spectral(pixel_cube, freq_duals):
     chans_all, pixel_count = pixel_cube.shape
-    precision = lax.Precision.HIGH
-    table = dct_table(chans_all)
-    coeffs = lax.dot_general(
-        pixel_cube,
-        table,
-        (((0,), (1,)), ((), ())),
-        precision=precision,
-        preferred_element_type=jnp.float32,
-    )
-    freq_next = jnp.clip(freq_duals + SIGMA * coeffs, -FREQ_BOUND, FREQ_BOUND)
-    return table, freq_next
-
-
-def spectral_back(table, freq_next):
-    precision = lax.Precision.HIGH
-    return lax.dot_general(
-        table,
-        freq_next,
-        (((0,), (1,)), ((), ())),
-        precision=precision,
-        preferred_element_type=jnp.float32,
-    )
+    if chans_all % 2:
+        table = dct_table(chans_all)
+        coeffs = forward_dot(pixel_cube, table)
+        freq_next = jnp.clip(freq_duals + SIGMA * coeffs, -FREQ_BOUND, FREQ_BOUND)
+        return (table,), freq_next, (freq_next,)
+    half = chans_all // 2
+    head = pixel_cube[:half]
+    tail = pixel_cube[half:][::-1]
+    tables = (dct_table(chans_all, 0), dct_table(chans_all, 1))
+    pairs = freq_duals.reshape(pixel_count, half, 2)
+    fresh = tuple(
+        jnp.clip(pairs[:, :, parity] + SIGMA * forward_dot(samples, tables[parity]), -FREQ_BOUND, FREQ_BOUND)
+        for parity, samples in ((0, head + tail), (1, head - tail))
+    )
+    freq_next = jnp.stack(fresh, axis=2).reshape(pixel_count, chans_all)
+    return tables, freq_next, fresh
+
+
+def spectral_back(tables, fresh):
+    parts = [
+        lax.dot_general(
+            table,
+            values,
+            (((0,), (1,)), ((), ())),
+            precision=lax.Precision.HIGH,
+            preferred_element_type=jnp.float32,
+        )
+        for table, values in zip(tables, fresh)
+    ]
+    if len(parts) == 1:
+        return parts[0]
+    return jnp.concatenate([parts[0] + parts[1], (parts[0] - parts[1])[::-1]], axis=0)
 
 
 def starlet_kernel(flags_ref, above_ref, own_ref, below_ref, duals_ref, *refs):
@@ -328,8 +352,8 @@
         chans * peers, share
     )
     pixel_cube, halos = lax.optimization_barrier((pixel_cube, halos))
-    table, freq_next = spectral(pixel_cube, freq_duals)
-    spectral_sum = spectral_back(table, freq_next)
+    tables, freq_next, fresh = spectral(pixel_cube, freq_duals)
+    spectral_sum = spectral_back(tables, fresh)
     spectral_sum, halos = lax.optimization_barrier((spectral_sum, halos))
     returned = lax.all_to_all(
         spectral_sum.reshape(peers, chans, share),

time: 179 us -> 184 us (1.028)
  local copies, waits for them, and re-layouts: 24.6 us -> 56.8 us
  matrix products: 22 us -> 11.8 us
  other arithmetic: 30.1 us -> 20 us
  waiting for transfers between devices: 27.3 us -> 20.4 us
    unnamed x16 -> x24, local copies, waits for them, and re-layouts: 7.58 us -> 20.4 us
    dot_general x2 -> x4, matrix products: 22 us -> 11.8 us  [the longest x2 7.11 us: forward_dot(): lax.dot_general(samples, table, (((0,), (1,)), ((), ())), precision=lax.P...]
    ppermute x4, waiting for transfers between devices: 7.24 us -> 0.01 us  [spatial(): sends.append(lax.ppermute(send, 'rows', down + up))]
    sub x1, other arithmetic: 8.24 us -> 1.36 us  [dct_table(): jnp.cos(outer_angle)[:, :, None] * jnp.cos(inner_angle)[:, None, :]]
    mul x1 -> x2, other arithmetic: 11.9 us -> 4.98 us  [dct_table(): (jnp.cos(outer_angle)[:, :, None] * jnp.cos(inner_angle)[:, None, :] - jn...]
    rev x0 -> x2, local copies, waits for them, and re-layouts: none -> 5.59 us  [the longest x1 5.15 us: spectral(): tail = pixel_cube[half:][::-1]]
    reshape x0 -> x2, local copies, waits for them, and re-layouts: none -> 4.94 us  [the longest x1 2.49 us: spectral(): pairs = freq_duals.reshape(pixel_count, half, 2)]
    another operation x0 -> x1, local copies, waits for them, and re-layouts: none -> 2.85 us  [spectral(): freq_next = jnp.stack(fresh, axis=2).reshape(pixel_count, chans_all)]
  transfers between devices with their start and end apart: 10 -> 10, of which waited for: 2 -> 1; matrix products, arithmetic and copies ran while one was open for 23% -> 28% of each run, Pallas kernels for 30% -> 29%
where the time goes in v1:
time: 184 us; the launch traced here: 181 us
  local copies, waits for them, and re-layouts  56.8 us (31%)
  Pallas kernels  52.7 us (29%)
  waiting for transfers between devices  20.4 us (11%)
  other arithmetic  20 us (11%)
  starting transfers between devices  18.3 us (10%)
  matrix products  11.8 us (6%)
    pallas_call x4, Pallas kernels, starlet(): pl.pallas_call(starlet_kernel, grid=(steps,), in_specs=[pl.BlockSpec(memo...  52.7 us
    unnamed x24, local copies, waits for them, and re-layouts  20.4 us
    all_to_all x1, waiting for transfers between devices, local(): lax.all_to_all(pieces, 'freq', split_axis=1, concat_axis=0, tiled=True)  20.3 us
    pallas_call x4, local copies, waits for them, and re-layouts, starlet(): pl.pallas_call(starlet_kernel, grid=(steps,), in_specs=[pl.BlockSpec(memo...  7.72 us
    dot_general x2, matrix products, forward_dot(): lax.dot_general(samples, table, (((0,), (1,)), ((), ())), precision=lax.P...  7.11 us
    max x1, other arithmetic, local(): jnp.maximum(image_cube - TAU_STEP * (data_grad + space_term + spectral_te...  6.82 us
    all_to_all x1, starting transfers between devices, local(): lax.all_to_all(pieces, 'freq', split_axis=1, concat_axis=0, tiled=True)  6.69 us
    all_to_all x1, starting transfers between devices, local(): lax.all_to_all(spectral_sum.reshape(peers, chans, share), 'freq', split_a...  5.61 us
  transfers between devices with their start and end apart: 10, of which 1 were waited for; matrix products, arithmetic and copies ran while one was open for 28% of the time, Pallas kernels for 29%

profile of v1, /device:TPU:13, one launch (start us, length us, event | category | flops | bytes accessed | tf_op | source)
XLA Modules:
  0.0 180.8 jit_solution(14991254108738755196)
XLA Ops:
  0.6 3.0 %copy.42 = f32[128,32,128]{0,2,1:T(8,128)} copy(f32[128,32,128]{2,1,0:T(8,128)} %own_ref.7) | data formatting | bytes 4194304 | tf_op args[0]
  3.6 6.7 %all-to-all-start = ((f32[128,16,256]{0,2,1:T(8,128)}), f32[128,16,256]{0,2,1:T(8,128)}, u32[]{:S(2)}, u32[]{:S(2)}) async-start(f32[128,16,256]{0,2,1:T(8,128)} %bitcast.52), calls=%async_computation | async-start | bytes 4194304 | tf_op jit(solution)/shard_map/all_to_all | solution.py:351
  10.3 1.4 fusion.36
  11.7 1.2 collective-permute-start.3
  13.2 1.2 collective-permute-start.1
  14.6 2.9 %copy.40 = f32[256,2048]{0,1:T(8,128)} copy(f32[256,2048]{1,0:T(8,128)} %param.7) | data formatting | bytes 4194304 | tf_op args[3]
  17.5 2.5 %reshape.325 = f32[256,1024,2]{0,2,1:T(2,128)S(1)} reshape(f32[256,2048]{0,1:T(8,128)} %copy.40) | data formatting | bytes 4194304 | tf_op jit(solution)/shard_map/reshape | solution.py:145
  20.0 2.6 %fusion.35 = (f32[256,1024,1]{0,2,1:T(1,128)}, f32[256,1024,1]{0,2,1:T(1,128)S(1)}) fusion(f32[256,1024,2]{0,2,1:T(2,128)S(1)} %reshape.325), kind=kLoop, calls=%fused_computation.73 | loop fusion | bytes 4194304 | tf_op jit(solution)/shard_map/slice | solution.py:147
  22.6 3.7 %copy.53 = f32[256,1024,1]{1,0,2:T(8,128)} copy(f32[256,1024,1]{0,2,1:T(1,128)} %get-tuple-element.74) | data formatting | bytes 2097152
  26.3 2.4 %copy.52 = f32[256,1024,1]{1,0,2:T(8,128)} copy(f32[256,1024,1]{0,2,1:T(1,128)S(1)} %get-tuple-element.75) | data formatting | bytes 2097152
  28.7 0.6 fusion.30
  29.3 2.1 %fusion.20 = (f32[1024,64]{0,1:T(8,128)S(1)}, f32[1024,64]{0,1:T(8,128)S(1)}, f32[1024,64]{0,1:T(8,128)S(1)}, f32[1024,64]{0,1:T(8,128)S(1)}) fusion(s32[64]{0:T(128)S(1)} %multiply_add_fusion, s32[1024]{0:T(1024)S(1)} %fusion.33, s32[1024]{0:T(1024)S(1)} %iota_multiply_fusion), kind=kLoop, calls=%fused_computation.39 | loop fusion | flops 1835008 | bytes 1057024 | tf_op jit(solution)/shard_map/cos | solution.py:118
  31.4 1.4 multiply_subtract_fusion
  32.8 2.5 %bitcast_multiply_fusion = f32[1024,1024]{0,1:T(8,128)} fusion(f32[1024,16,64]{0,2,1:T(8,128)S(1)} %get-tuple-element.93, f32[1024]{0:T(1024)S(1)} %compare_select_fusion), kind=kLoop, calls=%fused_computation | loop fusion | flops 1048576 | bytes 8392704 | tf_op jit(solution)/shard_map/mul | solution.py:117
  35.3 2.5 %bitcast_multiply_fusion.1 = f32[1024,1024]{0,1:T(8,128)} fusion(f32[1024,16,64]{0,2,1:T(8,128)S(1)} %get-tuple-element.94, f32[1024]{0:T(1024)S(1)} %compare_select_fusion.1), kind=kLoop, calls=%fused_computation.1 | loop fusion | flops 1048576 | bytes 8392704 | tf_op jit(solution)/shard_map/mul | solution.py:117
  37.8 20.3 %all-to-all-done = f32[128,16,256]{0,2,1:T(8,128)} async-done(((f32[128,16,256]{0,2,1:T(8,128)}), f32[128,16,256]{0,2,1:T(8,128)}, u32[]{:S(2)}, u32[]{:S(2)}) %all-to-all-start) | async-done | bytes 2097184 | tf_op jit(solution)/shard_map/all_to_all | solution.py:351
  58.1 1.9 %copy.43 = f32[16,128,1,256]{3,1,0,2:T(8,128)S(1)} copy(f32[16,128,1,256]{1,3,0,2:T(8,128)} %bitcast.8) | data formatting | bytes 4194304 | tf_op jit(solution)/shard_map/all_to_all | solution.py:351
  60.2 5.2 %rev.6 = f32[1024,256]{1,0:T(8,128)} reverse(f32[1024,256]{1,0:T(8,128)S(1)} %slice.30), dimensions={0} | reverse | bytes 2097152 | tf_op jit(solution)/shard_map/rev | solution.py:143
  65.3 4.9 %fusion.6 = f32[256,1024]{1,0:T(8,128)S(1)} fusion(f32[1024,1024]{0,1:T(8,128)} %bitcast_multiply_fusion, f32[256,1024,1]{1,0,2:T(8,128)} %copy.53, f32[1024,256]{1,0:T(8,128)} %rev.6, f32[2048,256]{1,0:T(8,128)S(1)} %bitcast.48), kind=kOutput, calls=%fused_computation.14 | convolution fusion | flops 1611661312 | bytes 8388608 | tf_op jit(solution)/shard_map/dot_general | solution.py:125
  70.3 1.8 %fusion.37 = f32[1024,256]{1,0:T(8,128)S(1)} fusion(f32[1024,1024]{0,1:T(8,128)S(1)} %copy-done.2, f32[256,1024]{1,0:T(8,128)S(1)} %fusion.6), kind=kOutput, calls=%fused_computation.75 | convolution fusion | flops 1610612736 | bytes 6291456 | tf_op jit(solution)/shard_map/dot_general | solution.py:156
  72.7 0.3 copy-done.7
  73.0 2.2 %fusion.8 = f32[256,1024]{1,0:T(8,128)S(1)} fusion(f32[1024,1024]{0,1:T(8,128)S(1)} %copy-done.3, f32[256,1024,1]{1,0,2:T(8,128)S(1)} %copy-done.7, f32[1024,256]{1,0:T(8,128)S(1)} %copy-done.4, f32[2048,256]{1,0:T(8,128)S(1)} %bitcast.49), kind=kOutput, calls=%fused_computation.17 | convolution fusion | flops 1611661312 | bytes 8388608 | tf_op jit(solution)/shard_map/dot_general | solution.py:125
  75.3 2.9 %fusion.34 = (f32[1024,256]{1,0:T(8,128)}, f32[1024,256]{1,0:T(8,128)S(1)}) fusion(f32[1024,256]{1,0:T(8,128)S(1)} %fusion.37, f32[1024,1024]{0,1:T(8,128)S(1)} %copy-done.3, f32[256,1024]{1,0:T(8,128)S(1)} %fusion.8), kind=kOutput, calls=%fused_computation.72 | convolution fusion | flops 1611137024 | bytes 8388608 | tf_op jit(solution)/shard_map/dot_general | solution.py:156
  78.1 0.4 rev.7
  78.6 2.7 %pad_maximum_fusion = f32[2048,256]{1,0:T(8,128)} fusion(f32[1024,256]{1,0:T(8,128)S(1)} %rev.7, f32[1024,256]{1,0:T(8,128)} %get-tuple-element.72), kind=kLoop, calls=%fused_computation.4 | loop fusion | flops 524288 | bytes 4194304 | tf_op jit(solution)/shard_map/concatenate | solution.py:167
  81.3 5.6 %all-to-all-start.1 = ((f32[16,128,256]{2,1,0:T(8,128)}), f32[16,128,256]{2,1,0:T(8,128)}, u32[]{:S(2)}, u32[]{:S(2)}) async-start(f32[16,128,256]{2,1,0:T(8,128)} %bitcast.13), calls=%async_computation.1 | async-start | bytes 4194304 | tf_op jit(solution)/shard_map/all_to_all | solution.py:358
  86.9 0.6 stack.40.flags_ref
  87.5 13.1 %shard_map.67 = (f32[4,128,32,128]{3,2,1,0:T(8,128)}, f32[30,32,128]{2,1,0:T(8,128)}, f32[128,32,128]{2,1,0:T(8,128)}, f32[30,32,128]{2,1,0:T(8,128)}) custom-call(s32[5]{0:T(128)} %stack.40.flags_ref, f32[32,32,128]{2,1,0:T(8,128)} %collective-permute-done.above_ref.below_ref, f32[128,32,128]{2,1,0:T(8,128)} %own_ref.7, ...), custom_call_target="tpu_custom_call" | custom-call | tf_op jit(solution)/shard_map/pallas_call | solution.py:267
  100.6 1.3 copy.45
  101.9 1.3 collective-permute-start.4
  103.2 13.1 %shard_map.68 = (f32[4,128,32,128]{3,2,1,0:T(8,128)}, f32[30,32,128]{2,1,0:T(8,128)}, f32[128,32,128]{2,1,0:T(8,128)}, f32[30,32,128]{2,1,0:T(8,128)}) custom-call(s32[5]{0:T(128)} %stack.40.flags_ref, f32[32,32,128]{2,1,0:T(8,128)} %collective-permute-done.1.above_ref.below_ref, ...), custom_call_target="tpu_custom_call", output_to_operand_aliasing={{0}: (5, {}), {2}: (6, {})} | custom-call | tf_op jit(solution)/shard_map/pallas_call | solution.py:267
  116.3 2.1 %copy.46 = f32[30,32,128]{2,0,1:T(8,128)} copy(f32[30,32,128]{2,1,0:T(8,128)} %get-tuple-element.58) | data formatting | bytes 983040 | tf_op jit(solution)/shard_map/pallas_call | solution.py:267
  118.6 13.1 %shard_map.69 = (f32[4,128,32,128]{3,2,1,0:T(8,128)}, f32[30,32,128]{2,1,0:T(8,128)}, f32[128,32,128]{2,1,0:T(8,128)}, f32[30,32,128]{2,1,0:T(8,128)}) custom-call(s32[5]{0:T(128)} %stack.40.flags_ref, f32[32,32,128]{2,1,0:T(8,128)} %collective-permute-done.2.above_ref.below_ref, ...), custom_call_target="tpu_custom_call", output_to_operand_aliasing={{0}: (5, {}), {2}: (6, {})} | custom-call | tf_op jit(solution)/shard_map/pallas_call | solution.py:267
  131.7 2.2 %copy.47 = f32[30,32,128]{2,0,1:T(8,128)} copy(f32[30,32,128]{2,1,0:T(8,128)} %get-tuple-element.59) | data formatting | bytes 983040 | tf_op jit(solution)/shard_map/pallas_call | solution.py:267
  133.9 1.2 collective-permute-start.6
  135.1 13.4 %shard_map.70 = (f32[4,128,32,128]{3,2,1,0:T(8,128)}, f32[30,32,128]{2,1,0:T(8,128)}, f32[128,32,128]{2,1,0:T(8,128)}, f32[30,32,128]{2,1,0:T(8,128)}) custom-call(s32[5]{0:T(128)} %stack.40.flags_ref, f32[32,32,128]{2,1,0:T(8,128)} %collective-permute-done.3.above_ref.below_ref, ...), custom_call_target="tpu_custom_call", output_to_operand_aliasing={{0}: (5, {}), {2}: (6, {})} | custom-call | tf_op jit(solution)/shard_map/pallas_call | solution.py:267
  148.5 2.1 %copy.48 = f32[30,32,128]{2,0,1:T(8,128)} copy(f32[30,32,128]{2,1,0:T(8,128)} %get-tuple-element.60) | data formatting | bytes 983040 | tf_op jit(solution)/shard_map/pallas_call | solution.py:267
  150.9 1.5 pad_maximum_fusion.1
  152.4 2.8 %copy.50 = f32[256,1024,2]{0,2,1:T(2,128)S(1)} copy(f32[256,1024,2]{1,0,2:T(8,128)} %pad_maximum_fusion.1) | data formatting | bytes 4194304 | tf_op jit(solution)/shard_map/stack | solution.py:150
  155.2 2.5 %reshape.330 = f32[256,2048]{0,1:T(8,128)} reshape(f32[256,1024,2]{0,2,1:T(2,128)S(1)} %copy.50) | data formatting | bytes 4194304 | tf_op jit(solution)/shard_map/reshape | solution.py:150
  157.7 2.9 %copy.51 = f32[256,2048]{1,0:T(8,128)} copy(f32[256,2048]{0,1:T(8,128)} %reshape.330) | data formatting | bytes 4194304
  160.6 0.8 constant_dynamic-update-slice_fusion.3
  161.4 1.9 %constant_dynamic-update-slice_fusion.2 = f32[30,128,128]{2,0,1:T(8,128)} fusion(f32[30,128,128]{2,0,1:T(8,128)} %constant_dynamic-update-slice_fusion.3, f32[30,32,128]{2,0,1:T(8,128)} %collective-permute-done.5), kind=kLoop, calls=%fused_computation.64 | loop fusion | bytes 1048576
  163.3 1.9 %constant_dynamic-update-slice_fusion.1 = f32[30,128,128]{2,0,1:T(8,128)} fusion(f32[30,128,128]{2,0,1:T(8,128)} %constant_dynamic-update-slice_fusion.2, f32[30,32,128]{2,0,1:T(8,128)} %collective-permute-done.6), kind=kLoop, calls=%fused_computation.63 | loop fusion | bytes 1048576
  165.2 1.9 %constant_dynamic-update-slice_fusion = f32[30,128,128]{2,0,1:T(8,128)} fusion(f32[30,128,128]{2,0,1:T(8,128)} %constant_dynamic-update-slice_fusion.1, f32[30,32,128]{2,0,1:T(8,128)} %collective-permute-done.7), kind=kLoop, calls=%fused_computation.62 | loop fusion | bytes 1048576 | tf_op jit(solution)/shard_map/concatenate | solution.py:330
  167.1 4.1 %copy.49 = f32[1,128,16,256]{3,2,1,0:T(8,128)} copy(f32[1,128,16,256]{3,1,2,0:T(8,128)} %bitcast.15) | data formatting | bytes 4194304 | tf_op jit(solution)/shard_map/all_to_all | solution.py:358
  171.2 2.8 %reshape.329 = f32[128,32,128]{2,1,0:T(8,128)} reshape(f32[1,128,16,256]{3,2,1,0:T(8,128)} %copy.49) | data formatting | bytes 4194304 | tf_op jit(solution)/shard_map/reshape | solution.py:366
  174.0 6.8 %fusion.4 = f32[128,32,128]{2,1,0:T(8,128)} fusion(f32[128,32,128]{2,1,0:T(8,128)S(1)} %copy-done.1, f32[128,32,128]{2,1,0:T(8,128)} %reshape.329, f32[128,32,128]{2,1,0:T(8,128)} %param.5, f32[128,32,128]{2,1,0:T(8,128)} %get-tuple-element.56, f32[30,128,128]{2,0,1:T(8,128)} %constant_dynamic-update-slice_fusion, pred[]{:T(512)S(6)} %eq.28), kind=kLoop, calls=%fused_computation.11 | loop fusion | flops 3670016 | bytes 12451841 | tf_op jit(solution)/shard_map/max | solution.py:367
  (35 shorter events, 1.8 us)
Async XLA Ops:
  3.6 6.7 %copy-start = (f32[128,32,128]{2,1,0:T(8,128)S(1)}, f32[128,32,128]{2,1,0:T(8,128)}, u32[]{:S(2)}) copy-start(f32[128,32,128]{2,1,0:T(8,128)} %own_ref.7) | copy-start | bytes 6291460
  3.6 54.5 %all-to-all-start = ((f32[128,16,256]{0,2,1:T(8,128)}), f32[128,16,256]{0,2,1:T(8,128)}, u32[]{:S(2)}, u32[]{:S(2)}) async-start(f32[128,16,256]{0,2,1:T(8,128)} %bitcast.52), calls=%async_computation | async-start | bytes 4194304 | tf_op jit(solution)/shard_map/all_to_all | solution.py:351
  11.7 48.4 %collective-permute-start.3 = (f32[32,32,128]{2,1,0:T(8,128)}, f32[32,32,128]{2,1,0:T(8,128)}, u32[]{:S(2)}, u32[]{:S(2)}) collective-permute-start(f32[32,32,128]{2,1,0:T(8,128)} %get-tuple-element.76), channel_id=1, source_target_pairs={{0,1},{1,0},{2,3},{3,2},{4,5},{5,4},{6,7},{7,6},{8,9},{9,8},{10,11... | collective-permute-start | bytes 1572872 | tf_op jit(solution)/shard_map/ppermute | solution.py:302
  12.9 47.2 %collective-permute-start.2 = (f32[32,32,128]{2,1,0:T(8,128)}, f32[32,32,128]{2,1,0:T(8,128)}, u32[]{:S(2)}, u32[]{:S(2)}) collective-permute-start(f32[32,32,128]{2,1,0:T(8,128)} %get-tuple-element.77), channel_id=1, source_target_pairs={{0,1},{1,0},{2,3},{3,2},{4,5},{5,4},{6,7},{7,6},{8,9},{9,8},{10,11... | collective-permute-start | bytes 1572872 | tf_op jit(solution)/shard_map/ppermute | solution.py:302
  13.2 46.9 %collective-permute-start.1 = (f32[32,32,128]{2,1,0:T(8,128)}, f32[32,32,128]{2,1,0:T(8,128)}, u32[]{:S(2)}, u32[]{:S(2)}) collective-permute-start(f32[32,32,128]{2,1,0:T(8,128)} %get-tuple-element.78), channel_id=1, source_target_pairs={{0,1},{1,0},{2,3},{3,2},{4,5},{5,4},{6,7},{7,6},{8,9},{9,8},{10,11... | collective-permute-start | bytes 1572872 | tf_op jit(solution)/shard_map/ppermute | solution.py:302
  14.4 45.7 %collective-permute-start = (f32[32,32,128]{2,1,0:T(8,128)}, f32[32,32,128]{2,1,0:T(8,128)}, u32[]{:S(2)}, u32[]{:S(2)}) collective-permute-start(f32[32,32,128]{2,1,0:T(8,128)} %get-tuple-element.79), channel_id=1, source_target_pairs={{0,1},{1,0},{2,3},{3,2},{4,5},{5,4},{6,7},{7,6},{8,9},{9,8},{10,11... | collective-permute-start | bytes 1572872 | tf_op jit(solution)/shard_map/ppermute | solution.py:302
  65.3 4.9 %copy-start.2 = (f32[1024,1024]{0,1:T(8,128)S(1)}, f32[1024,1024]{0,1:T(8,128)}, u32[]{:S(2)}) copy-start(f32[1024,1024]{0,1:T(8,128)} %bitcast_multiply_fusion) | copy-start | bytes 12582916
  70.2 2.2 %copy-start.3 = (f32[1024,1024]{0,1:T(8,128)S(1)}, f32[1024,1024]{0,1:T(8,128)}, u32[]{:S(2)}) copy-start(f32[1024,1024]{0,1:T(8,128)} %bitcast_multiply_fusion.1) | copy-start | bytes 12582916
  70.2 2.5 %copy-start.4 = (f32[1024,256]{1,0:T(8,128)S(1)}, f32[1024,256]{1,0:T(8,128)}, u32[]{:S(2)}) copy-start(f32[1024,256]{1,0:T(8,128)} %rev.6) | copy-start | bytes 3145732
  70.2 2.8 %copy-start.7 = (f32[256,1024,1]{1,0,2:T(8,128)S(1)}, f32[256,1024,1]{1,0,2:T(8,128)}, u32[]{:S(2)}) copy-start(f32[256,1024,1]{1,0,2:T(8,128)} %copy.52) | copy-start | bytes 3145732
  75.3 2.9 %copy-start.5 = (f32[256,1024]{1,0:T(8,128)}, f32[256,1024]{1,0:T(8,128)S(1)}, u32[]{:S(2)}) copy-start(f32[256,1024]{1,0:T(8,128)S(1)} %fusion.8) | copy-start | bytes 3145732
  81.3 85.8 %all-to-all-start.1 = ((f32[16,128,256]{2,1,0:T(8,128)}), f32[16,128,256]{2,1,0:T(8,128)}, u32[]{:S(2)}, u32[]{:S(2)}) async-start(f32[16,128,256]{2,1,0:T(8,128)} %bitcast.13), calls=%async_computation.1 | async-start | bytes 4194304 | tf_op jit(solution)/shard_map/all_to_all | solution.py:358
  101.9 58.7 %collective-permute-start.4 = (f32[30,32,128]{2,0,1:T(8,128)S(1)}, f32[30,32,128]{2,0,1:T(8,128)S(1)}, u32[]{:S(2)}, u32[]{:S(2)}) collective-permute-start(f32[30,32,128]{2,0,1:T(8,128)S(1)} %copy.45), channel_id=1, source_target_pairs={{0,1},{1,0},{2,3},{3,2},{4,5},{5,4},{6,7},{7,6},{8,9},{9,8},{10,11... | collective-permute-start | bytes 1474568 | tf_op jit(solution)/shard_map/ppermute | solution.py:326
  118.4 43.0 %collective-permute-start.5 = (f32[30,32,128]{2,0,1:T(8,128)}, f32[30,32,128]{2,0,1:T(8,128)}, u32[]{:S(2)}, u32[]{:S(2)}) collective-permute-start(f32[30,32,128]{2,0,1:T(8,128)} %copy.46), channel_id=1, source_target_pairs={{0,1},{1,0},{2,3},{3,2},{4,5},{5,4},{6,7},{7,6},{8,9},{9,8},{10,11... | collective-permute-start | bytes 1474568 | tf_op jit(solution)/shard_map/ppermute | solution.py:326
  133.9 29.4 %collective-permute-start.6 = (f32[30,32,128]{2,0,1:T(8,128)}, f32[30,32,128]{2,0,1:T(8,128)}, u32[]{:S(2)}, u32[]{:S(2)}) collective-permute-start(f32[30,32,128]{2,0,1:T(8,128)} %copy.47), channel_id=1, source_target_pairs={{0,1},{1,0},{2,3},{3,2},{4,5},{5,4},{6,7},{7,6},{8,9},{9,8},{10,11... | collective-permute-start | bytes 1474568 | tf_op jit(solution)/shard_map/ppermute | solution.py:326
  135.1 15.8 %copy-start.6 = (f32[256,1024]{1,0:T(8,128)S(1)}, f32[256,1024]{1,0:T(8,128)}, u32[]{:S(2)}) copy-start(f32[256,1024]{1,0:T(8,128)} %copy-done.5) | copy-start | bytes 3145732
  150.7 14.5 %collective-permute-start.7 = (f32[30,32,128]{2,0,1:T(8,128)}, f32[30,32,128]{2,0,1:T(8,128)}, u32[]{:S(2)}, u32[]{:S(2)}) collective-permute-start(f32[30,32,128]{2,0,1:T(8,128)} %copy.48), channel_id=1, source_target_pairs={{0,1},{1,0},{2,3},{3,2},{4,5},{5,4},{6,7},{7,6},{8,9},{9,8},{10,11... | collective-permute-start | bytes 1474568 | tf_op jit(solution)/shard_map/ppermute | solution.py:326
  171.2 2.8 %copy-start.1 = (f32[128,32,128]{2,1,0:T(8,128)S(1)}, f32[128,32,128]{2,1,0:T(8,128)}, u32[]{:S(2)}) copy-start(f32[128,32,128]{2,1,0:T(8,128)} %own_ref.7) | copy-start | bytes 6291460

commit v2 on v1

--- a/solution.py
+++ b/solution.py
@@ -298,6 +298,8 @@
     halos = []
     for group in range(groups):
         part = image_cube[group * width : (group + 1) * width]
+        if halos:
+            part, halos[-1] = lax.optimization_barrier((part, halos[-1]))
         if count == 2:
             got = lax.ppermute(part, "rows", down + up)
             halos.append((got, got))
@@ -306,40 +308,51 @@
     return halos
 
 
-def spatial(halos, image_cube, space_duals):
-    chans, local_rows, columns = image_cube.shape
-    halo, groups, width = row_plan(chans, local_rows)
-    count = lax.axis_size("rows")
-    index = lax.axis_index("rows")
-    down = [(i, i + 1) for i in range(count - 1)]
-    up = [(i + 1, i) for i in range(count - 1)]
-    paired = count == 2
-    flags = jnp.stack(
-        [index * local_rows, count * local_rows, index > 0, index < count - 1, paired & (index == 0)]
-    ).astype(jnp.int32)
-    carry = ()
-    sends, keeps = [], []
-    for group, (above, below) in enumerate(halos):
-        space_next, send, mid, keep = starlet(flags, above, image_cube, below, space_duals, halo, group, groups, carry)
-        carry = (space_next, mid)
-        if paired:
-            sends.append(lax.ppermute(send, "rows", down + up))
+class Spatial:
+    def __init__(self, image_cube, space_duals):
+        self.image_cube = image_cube
+        self.space_duals = space_duals
+        chans, local_rows, columns = image_cube.shape
+        self.halo, self.groups, self.width = row_plan(chans, local_rows)
+        count = lax.axis_size("rows")
+        self.index = lax.axis_index("rows")
+        self.down = [(i, i + 1) for i in range(count - 1)]
+        self.up = [(i + 1, i) for i in range(count - 1)]
+        self.paired = count == 2
+        index = self.index
+        self.flags = jnp.stack(
+            [index * local_rows, count * local_rows, index > 0, index < count - 1, self.paired & (index == 0)]
+        ).astype(jnp.int32)
+        self.sends, self.keeps = [], []
+
+    def run(self, group, halos, carry):
+        above, below = halos[group]
+        space_next, send, mid, keep = starlet(
+            self.flags, above, self.image_cube, below, self.space_duals, self.halo, group, self.groups, carry
+        )
+        if self.paired:
+            self.sends.append(lax.ppermute(send, "rows", self.down + self.up))
         else:
-            sends.append(lax.ppermute(send, "rows", up))
-            keeps.append(lax.ppermute(keep, "rows", down))
-    got = jnp.concatenate(sends, axis=1)
-    gap = local_rows - halo
-    if paired:
-        spill = jnp.where(
-            index == 0,
-            jnp.pad(got, ((gap, 0), (0, 0), (0, 0))),
-            jnp.pad(got, ((0, gap), (0, 0), (0, 0))),
-        )
-    else:
-        spill = jnp.pad(jnp.concatenate(keeps, axis=1), ((0, gap), (0, 0), (0, 0))) + jnp.pad(
-            got, ((gap, 0), (0, 0), (0, 0))
-        )
-    return mid + jnp.transpose(spill, (1, 0, 2)), space_next
+            self.sends.append(lax.ppermute(send, "rows", self.up))
+            self.keeps.append(lax.ppermute(keep, "rows", self.down))
+        return (space_next, mid)
+
+    def finish(self, carry):
+        space_next, mid = carry
+        local_rows = mid.shape[1]
+        got = jnp.concatenate(self.sends, axis=1)
+        gap = local_rows - self.halo
+        if self.paired:
+            spill = jnp.where(
+                self.index == 0,
+                jnp.pad(got, ((gap, 0), (0, 0), (0, 0))),
+                jnp.pad(got, ((0, gap), (0, 0), (0, 0))),
+            )
+        else:
+            spill = jnp.pad(jnp.concatenate(self.keeps, axis=1), ((0, gap), (0, 0), (0, 0))) + jnp.pad(
+                got, ((gap, 0), (0, 0), (0, 0))
+            )
+        return mid + jnp.transpose(spill, (1, 0, 2)), space_next
 
 
 def local(image_cube, data_grad, space_duals, freq_duals):
@@ -351,10 +364,18 @@
     pixel_cube = lax.all_to_all(pieces, "freq", split_axis=1, concat_axis=0, tiled=True).reshape(
         chans * peers, share
     )
-    pixel_cube, halos = lax.optimization_barrier((pixel_cube, halos))
+    work = Spatial(image_cube, space_duals)
+    early = work.groups // 2
+    carry = ()
+    for group in range(early):
+        carry = work.run(group, halos, carry)
+    pixel_cube, carry, later = lax.optimization_barrier((pixel_cube, carry, halos[early:]))
+    halos = halos[:early] + list(later)
     tables, freq_next, fresh = spectral(pixel_cube, freq_duals)
     spectral_sum = spectral_back(tables, fresh)
-    spectral_sum, halos = lax.optimization_barrier((spectral_sum, halos))
+    spectral_sum, carry, work.sends, work.keeps = lax.optimization_barrier(
+        (spectral_sum, carry, work.sends, work.keeps)
+    )
     returned = lax.all_to_all(
         spectral_sum.reshape(peers, chans, share),
         "freq",
@@ -362,7 +383,9 @@
         concat_axis=2,
         tiled=True,
     )
-    space_term, space_next = spatial(halos, image_cube, space_duals)
+    for group in range(early, work.groups):
+        carry = work.run(group, halos, carry)
+    space_term, space_next = work.finish(carry)
     spectral_term = returned.reshape(chans, local_rows, columns)
     image_next = jnp.maximum(image_cube - TAU_STEP * (data_grad + space_term + spectral_term), 0.0)
     return (image_next, space_next, freq_next)

time: 184 us -> 183 us (level)
  waiting for transfers between devices: 20.4 us -> 11.7 us
  starting transfers between devices: 18.3 us -> 23.9 us
    all_to_all x1, waiting for transfers between devices: 20.3 us -> 0.01 us  [local(): lax.all_to_all(pieces, 'freq', split_axis=1, concat_axis=0, tiled=True)]
    ppermute x4, waiting for transfers between devices: 0.01 us -> 11.6 us  [exchange_halos(): got = lax.ppermute(part, 'rows', down + up)]
    all_to_all x1, starting transfers between devices: 5.61 us -> 9.42 us  [local(): lax.all_to_all(spectral_sum.reshape(peers, chans, share), 'freq', split_a...]
    ppermute x4, starting transfers between devices: 2.96 us -> 4.84 us  [exchange_halos(): got = lax.ppermute(part, 'rows', down + up)]
    unnamed x24 -> x38, local copies, waits for them, and re-layouts: 20.4 us -> 21.9 us
  transfers between devices with their start and end apart: 10 -> 10, of which waited for: 1 -> 3; matrix products, arithmetic and copies ran while one was open for 28% -> 40% of each run, Pallas kernels for 29% -> 29%
where the time goes in v2:
time: 183 us; the launch traced here: 180 us
  local copies, waits for them, and re-layouts  58.4 us (32%)
  Pallas kernels  52.6 us (29%)
  starting transfers between devices  23.9 us (13%)
  other arithmetic  20.9 us (11%)
  matrix products  11.8 us (6%)
  waiting for transfers between devices  11.7 us (6%)
    pallas_call x4, Pallas kernels, starlet(): pl.pallas_call(starlet_kernel, grid=(steps,), in_specs=[pl.BlockSpec(memo...  52.6 us
    unnamed x38, local copies, waits for them, and re-layouts  21.9 us
    ppermute x4, waiting for transfers between devices, exchange_halos(): got = lax.ppermute(part, 'rows', down + up)  11.6 us
    all_to_all x1, starting transfers between devices, local(): lax.all_to_all(spectral_sum.reshape(peers, chans, share), 'freq', split_a...  9.42 us
    pallas_call x4, local copies, waits for them, and re-layouts, starlet(): pl.pallas_call(starlet_kernel, grid=(steps,), in_specs=[pl.BlockSpec(memo...  7.71 us
    dot_general x2, matrix products, forward_dot(): lax.dot_general(samples, table, (((0,), (1,)), ((), ())), precision=lax.P...  7.11 us
    max x1, other arithmetic, local(): jnp.maximum(image_cube - TAU_STEP * (data_grad + space_term + spectral_te...  6.82 us
    all_to_all x1, starting transfers between devices, local(): lax.all_to_all(pieces, 'freq', split_axis=1, concat_axis=0, tiled=True)  6.69 us
  transfers between devices with their start and end apart: 10, of which 3 were waited for; matrix products, arithmetic and copies ran while one was open for 40% of the time, Pallas kernels for 29%

profile of v2, /device:TPU:13, one launch (start us, length us, event | category | flops | bytes accessed | tf_op | source)
XLA Modules:
  0.0 180.1 jit_solution(10304077263232871970)
XLA Ops:
  0.6 3.0 %copy.40 = f32[128,32,128]{0,2,1:T(8,128)} copy(f32[128,32,128]{2,1,0:T(8,128)} %own_ref.7) | data formatting | bytes 4194304 | tf_op args[0]
  3.6 6.7 %all-to-all-start = ((f32[128,16,256]{0,2,1:T(8,128)}), f32[128,16,256]{0,2,1:T(8,128)}, u32[]{:S(2)}, u32[]{:S(2)}) async-start(f32[128,16,256]{0,2,1:T(8,128)} %bitcast.52), calls=%async_computation | async-start | bytes 4194304 | tf_op jit(solution)/shard_map/all_to_all | solution.py:364
  10.3 1.4 fusion.36
  11.7 1.2 collective-permute-start
  12.9 3.1 %fusion.20 = (f32[1024,64]{0,1:T(8,128)S(1)}, f32[1024,64]{0,1:T(8,128)}, f32[1024,64]{0,1:T(8,128)}, f32[1024,64]{0,1:T(8,128)}) fusion(s32[64]{0:T(128)S(1)} %multiply_add_fusion, s32[1024]{0:T(1024)S(1)} %fusion.33, s32[1024]{0:T(1024)S(1)} %iota_multiply_fusion), kind=kLoop, calls=%fused_computation.39 | loop fusion | flops 1835008 | bytes 1057024 | tf_op jit(solution)/shard_map/cos | solution.py:118
  16.0 2.9 %copy.42 = f32[256,2048]{0,1:T(8,128)} copy(f32[256,2048]{1,0:T(8,128)} %param.7) | data formatting | bytes 4194304 | tf_op args[3]
  18.9 2.5 %reshape.327 = f32[256,1024,2]{0,2,1:T(2,128)S(1)} reshape(f32[256,2048]{0,1:T(8,128)} %copy.42) | data formatting | bytes 4194304 | tf_op jit(solution)/shard_map/reshape | solution.py:145
  21.4 2.6 %fusion.35 = (f32[256,1024,1]{0,2,1:T(1,128)S(1)}, f32[256,1024,1]{0,2,1:T(1,128)}) fusion(f32[256,1024,2]{0,2,1:T(2,128)S(1)} %reshape.327), kind=kLoop, calls=%fused_computation.73 | loop fusion | bytes 4194304 | tf_op jit(solution)/shard_map/slice | solution.py:147
  24.0 1.2 collective-permute-done.above_ref.below_ref
  25.1 1.2 collective-permute-start.1
  27.0 3.7 %copy.52 = f32[256,1024,1]{1,0,2:T(8,128)} copy(f32[256,1024,1]{0,2,1:T(1,128)} %get-tuple-element.81) | data formatting | bytes 2097152
  30.7 2.4 %copy.53 = f32[256,1024,1]{1,0,2:T(8,128)} copy(f32[256,1024,1]{0,2,1:T(1,128)S(1)} %get-tuple-element.80) | data formatting | bytes 2097152
  33.7 1.3 multiply_subtract_fusion
  34.9 2.7 %collective-permute-done.1.above_ref.below_ref = f32[32,32,128]{2,1,0:T(8,128)S(1)} collective-permute-done((f32[32,32,128]{2,1,0:T(8,128)}, f32[32,32,128]{2,1,0:T(8,128)S(1)}, u32[]{:S(2)}, u32[]{:S(2)}) %collective-permute-start.1) | collective-permute-done | bytes 524320 | tf_op jit(solution)/shard_map/ppermute | solution.py:304
  37.7 1.2 collective-permute-start.2
  38.9 2.5 %bitcast_multiply_fusion.1 = f32[1024,1024]{0,1:T(8,128)} fusion(f32[1024,16,64]{0,2,1:T(8,128)S(1)} %get-tuple-element.100, f32[1024]{0:T(1024)S(1)} %compare_select_fusion.1), kind=kLoop, calls=%fused_computation.1 | loop fusion | flops 1048576 | bytes 8392704 | tf_op jit(solution)/shard_map/mul | solution.py:117
  41.3 7.7 %collective-permute-done.2.above_ref.below_ref = f32[32,32,128]{2,1,0:T(8,128)S(1)} collective-permute-done((f32[32,32,128]{2,1,0:T(8,128)S(1)}, f32[32,32,128]{2,1,0:T(8,128)S(1)}, u32[]{:S(2)}, u32[]{:S(2)}) %collective-permute-start.2) | collective-permute-done | bytes 524320 | tf_op jit(solution)/shard_map/ppermute | solution.py:304
  49.9 1.2 collective-permute-start.3
  51.1 2.5 %bitcast_multiply_fusion = f32[1024,1024]{0,1:T(8,128)} fusion(f32[1024,16,64]{0,2,1:T(8,128)S(1)} %get-tuple-element.99, f32[1024]{0:T(1024)S(1)} %compare_select_fusion), kind=kLoop, calls=%fused_computation | loop fusion | flops 1048576 | bytes 8392704 | tf_op jit(solution)/shard_map/mul | solution.py:117
  53.6 13.1 %shard_map.67 = (f32[4,128,32,128]{3,2,1,0:T(8,128)}, f32[30,32,128]{2,1,0:T(8,128)}, f32[128,32,128]{2,1,0:T(8,128)}, f32[30,32,128]{2,1,0:T(8,128)}) custom-call(s32[5]{0:T(128)} %stack.40.flags_ref, f32[32,32,128]{2,1,0:T(8,128)} %collective-permute-done.above_ref.below_ref, f32[128,32,128]{2,1,0:T(8,128)} %own_ref.7, ...), custom_call_target="tpu_custom_call" | custom-call | tf_op jit(solution)/shard_map/pallas_call | solution.py:267
  66.7 2.1 %copy.45 = f32[30,32,128]{2,0,1:T(8,128)} copy(f32[30,32,128]{2,1,0:T(8,128)} %get-tuple-element.56) | data formatting | bytes 983040 | tf_op jit(solution)/shard_map/pallas_call | solution.py:267
  69.1 13.2 %shard_map.68 = (f32[4,128,32,128]{3,2,1,0:T(8,128)}, f32[30,32,128]{2,1,0:T(8,128)}, f32[128,32,128]{2,1,0:T(8,128)}, f32[30,32,128]{2,1,0:T(8,128)}) custom-call(s32[5]{0:T(128)} %stack.40.flags_ref, f32[32,32,128]{2,1,0:T(8,128)} %copy-done.10, f32[128,32,128]{2,1,0:T(8,128)} %own_ref.7, ...), custom_call_target="tpu_custom_call", output_to_operand_aliasing={{0}: (5, {}), {2}: (6, {})} | custom-call | tf_op jit(solution)/shard_map/pallas_call | solution.py:267
  82.3 2.1 %copy.46 = f32[30,32,128]{2,0,1:T(8,128)} copy(f32[30,32,128]{2,1,0:T(8,128)} %get-tuple-element.57) | data formatting | bytes 983040 | tf_op jit(solution)/shard_map/pallas_call | solution.py:267
  84.4 1.2 collective-permute-start.5
  85.5 1.9 %copy.41 = f32[16,128,1,256]{3,1,0,2:T(8,128)S(1)} copy(f32[16,128,1,256]{1,3,0,2:T(8,128)} %bitcast.6) | data formatting | bytes 4194304 | tf_op jit(solution)/shard_map/all_to_all | solution.py:364
  88.3 5.2 %rev.6 = f32[1024,256]{1,0:T(8,128)} reverse(f32[1024,256]{1,0:T(8,128)S(1)} %slice.30), dimensions={0} | reverse | bytes 2097152 | tf_op jit(solution)/shard_map/rev | solution.py:143
  93.5 4.9 %fusion.6 = f32[256,1024]{1,0:T(8,128)S(1)} fusion(f32[1024,1024]{0,1:T(8,128)} %bitcast_multiply_fusion, f32[256,1024,1]{1,0,2:T(8,128)} %copy.53, f32[1024,256]{1,0:T(8,128)} %rev.6, f32[2048,256]{1,0:T(8,128)S(1)} %bitcast.48), kind=kOutput, calls=%fused_computation.14 | convolution fusion | flops 1611661312 | bytes 8388608 | tf_op jit(solution)/shard_map/dot_general | solution.py:125
  98.4 1.8 %fusion.37 = f32[1024,256]{1,0:T(8,128)S(1)} fusion(f32[1024,1024]{0,1:T(8,128)S(1)} %copy-done.2, f32[256,1024]{1,0:T(8,128)S(1)} %fusion.6), kind=kOutput, calls=%fused_computation.75 | convolution fusion | flops 1610612736 | bytes 6291456 | tf_op jit(solution)/shard_map/dot_general | solution.py:156
  101.2 2.2 %fusion.8 = f32[256,1024]{1,0:T(8,128)S(1)} fusion(f32[1024,1024]{0,1:T(8,128)S(1)} %copy-done.3, f32[256,1024,1]{1,0,2:T(8,128)S(1)} %copy-done.7, f32[1024,256]{1,0:T(8,128)S(1)} %copy-done.4, f32[2048,256]{1,0:T(8,128)S(1)} %bitcast.49), kind=kOutput, calls=%fused_computation.17 | convolution fusion | flops 1611661312 | bytes 8388608 | tf_op jit(solution)/shard_map/dot_general | solution.py:125
  103.4 2.9 %fusion.34 = (f32[1024,256]{1,0:T(8,128)}, f32[1024,256]{1,0:T(8,128)S(1)}) fusion(f32[1024,256]{1,0:T(8,128)S(1)} %fusion.37, f32[1024,1024]{0,1:T(8,128)S(1)} %copy-done.3, f32[256,1024]{1,0:T(8,128)S(1)} %fusion.8), kind=kOutput, calls=%fused_computation.72 | convolution fusion | flops 1611137024 | bytes 8388608 | tf_op jit(solution)/shard_map/dot_general | solution.py:156
  106.8 2.7 %pad_maximum_fusion = f32[2048,256]{1,0:T(8,128)} fusion(f32[1024,256]{1,0:T(8,128)S(1)} %rev.7, f32[1024,256]{1,0:T(8,128)} %get-tuple-element.78), kind=kLoop, calls=%fused_computation.4 | loop fusion | flops 524288 | bytes 4194304 | tf_op jit(solution)/shard_map/concatenate | solution.py:167
  109.5 9.4 %all-to-all-start.1 = ((f32[16,128,256]{2,1,0:T(8,128)}), f32[16,128,256]{2,1,0:T(8,128)}, u32[]{:S(2)}, u32[]{:S(2)}) async-start(f32[16,128,256]{2,1,0:T(8,128)} %bitcast.13), calls=%async_computation.1 | async-start | bytes 4194304 | tf_op jit(solution)/shard_map/all_to_all | solution.py:379
  118.9 13.2 %shard_map.69 = (f32[4,128,32,128]{3,2,1,0:T(8,128)}, f32[30,32,128]{2,1,0:T(8,128)}, f32[128,32,128]{2,1,0:T(8,128)}, f32[30,32,128]{2,1,0:T(8,128)}) custom-call(s32[5]{0:T(128)} %stack.40.flags_ref, f32[32,32,128]{2,1,0:T(8,128)} %copy-done.9, f32[128,32,128]{2,1,0:T(8,128)} %own_ref.7, ...), custom_call_target="tpu_custom_call", output_to_operand_aliasing={{0}: (5, {}), {2}: (6, {})} | custom-call | tf_op jit(solution)/shard_map/pallas_call | solution.py:267
  132.0 1.3 copy.47
  133.7 13.2 %shard_map.70 = (f32[4,128,32,128]{3,2,1,0:T(8,128)}, f32[30,32,128]{2,1,0:T(8,128)}, f32[128,32,128]{2,1,0:T(8,128)}, f32[30,32,128]{2,1,0:T(8,128)}) custom-call(s32[5]{0:T(128)} %stack.40.flags_ref, f32[32,32,128]{2,1,0:T(8,128)} %copy-done.8, f32[128,32,128]{2,1,0:T(8,128)} %own_ref.7, ...), custom_call_target="tpu_custom_call", output_to_operand_aliasing={{0}: (5, {}), {2}: (6, {})} | custom-call | tf_op jit(solution)/shard_map/pallas_call | solution.py:267
  146.9 2.2 %copy.48 = f32[30,32,128]{2,0,1:T(8,128)} copy(f32[30,32,128]{2,1,0:T(8,128)} %get-tuple-element.66) | data formatting | bytes 983040 | tf_op jit(solution)/shard_map/pallas_call | solution.py:267
  149.1 1.2 collective-permute-start.7
  150.3 1.5 pad_maximum_fusion.1
  151.7 2.8 %copy.50 = f32[256,1024,2]{0,2,1:T(2,128)S(1)} copy(f32[256,1024,2]{1,0,2:T(8,128)} %pad_maximum_fusion.1) | data formatting | bytes 4194304 | tf_op jit(solution)/shard_map/stack | solution.py:150
  154.6 2.4 %reshape.330 = f32[256,2048]{0,1:T(8,128)} reshape(f32[256,1024,2]{0,2,1:T(2,128)S(1)} %copy.50) | data formatting | bytes 4194304 | tf_op jit(solution)/shard_map/reshape | solution.py:150
  157.0 2.9 %copy.51 = f32[256,2048]{1,0:T(8,128)} copy(f32[256,2048]{0,1:T(8,128)} %reshape.330) | data formatting | bytes 4194304
  159.9 1.9 %constant_dynamic-update-slice_fusion.3 = f32[30,128,128]{2,0,1:T(8,128)} fusion(f32[30,32,128]{2,0,1:T(8,128)} %collective-permute-done.4), kind=kLoop, calls=%fused_computation.65 | loop fusion | bytes 1015808
  161.8 1.9 %constant_dynamic-update-slice_fusion.2 = f32[30,128,128]{2,0,1:T(8,128)} fusion(f32[30,128,128]{2,0,1:T(8,128)} %constant_dynamic-update-slice_fusion.3, f32[30,32,128]{2,0,1:T(8,128)} %collective-permute-done.5), kind=kLoop, calls=%fused_computation.64 | loop fusion | bytes 1048576
  163.6 0.8 constant_dynamic-update-slice_fusion.1
  164.5 1.9 %constant_dynamic-update-slice_fusion = f32[30,128,128]{2,0,1:T(8,128)} fusion(f32[30,128,128]{2,0,1:T(8,128)} %constant_dynamic-update-slice_fusion.1, f32[30,32,128]{2,0,1:T(8,128)} %collective-permute-done.7), kind=kLoop, calls=%fused_computation.62 | loop fusion | bytes 1048576 | tf_op jit(solution)/shard_map/concatenate | solution.py:343
  166.4 4.1 %copy.49 = f32[1,128,16,256]{3,2,1,0:T(8,128)} copy(f32[1,128,16,256]{3,1,2,0:T(8,128)} %bitcast.15) | data formatting | bytes 4194304 | tf_op jit(solution)/shard_map/all_to_all | solution.py:379
  170.5 2.8 %reshape.329 = f32[128,32,128]{2,1,0:T(8,128)} reshape(f32[1,128,16,256]{3,2,1,0:T(8,128)} %copy.49) | data formatting | bytes 4194304 | tf_op jit(solution)/shard_map/reshape | solution.py:389
  173.3 6.8 %fusion.4 = f32[128,32,128]{2,1,0:T(8,128)} fusion(f32[128,32,128]{2,1,0:T(8,128)S(1)} %copy-done.1, f32[128,32,128]{2,1,0:T(8,128)} %reshape.329, f32[128,32,128]{2,1,0:T(8,128)} %param.5, f32[128,32,128]{2,1,0:T(8,128)} %get-tuple-element.62, f32[30,128,128]{2,0,1:T(8,128)} %constant_dynamic-update-slice_fusion, pred[]{:T(512)S(6)} %eq.28), kind=kLoop, calls=%fused_computation.11 | loop fusion | flops 3670016 | bytes 12451841 | tf_op jit(solution)/shard_map/max | solution.py:390
  (49 shorter events, 4.9 us)
Async XLA Ops:
  3.6 6.7 %copy-start = (f32[128,32,128]{2,1,0:T(8,128)S(1)}, f32[128,32,128]{2,1,0:T(8,128)}, u32[]{:S(2)}) copy-start(f32[128,32,128]{2,1,0:T(8,128)} %own_ref.7) | copy-start | bytes 6291460
  3.6 81.9 %all-to-all-start = ((f32[128,16,256]{0,2,1:T(8,128)}), f32[128,16,256]{0,2,1:T(8,128)}, u32[]{:S(2)}, u32[]{:S(2)}) async-start(f32[128,16,256]{0,2,1:T(8,128)} %bitcast.52), calls=%async_computation | async-start | bytes 4194304 | tf_op jit(solution)/shard_map/all_to_all | solution.py:364
  11.7 13.5 %collective-permute-start = (f32[32,32,128]{2,1,0:T(8,128)}, f32[32,32,128]{2,1,0:T(8,128)}, u32[]{:S(2)}, u32[]{:S(2)}) collective-permute-start(f32[32,32,128]{2,1,0:T(8,128)} %get-tuple-element.83), channel_id=1, source_target_pairs={{0,1},{1,0},{2,3},{3,2},{4,5},{5,4},{6,7},{7,6},{8,9},{9,8},{10,11... | collective-permute-start | bytes 1572872 | tf_op jit(solution)/shard_map/ppermute | solution.py:304
  25.1 12.5 %collective-permute-start.1 = (f32[32,32,128]{2,1,0:T(8,128)}, f32[32,32,128]{2,1,0:T(8,128)S(1)}, u32[]{:S(2)}, u32[]{:S(2)}) collective-permute-start(f32[32,32,128]{2,1,0:T(8,128)} %get-tuple-element.36), channel_id=1, source_target_pairs={{0,1},{1,0},{2,3},{3,2},{4,5},{5,4},{6,7},{7,6},{8,9},{9,8},{10,11... | collective-permute-start | bytes 1572872 | tf_op jit(solution)/shard_map/ppermute | solution.py:304
  26.9 6.7 %copy-start.11 = (f32[1024,64]{0,1:T(8,128)S(1)}, f32[1024,64]{0,1:T(8,128)}, u32[]{:S(2)}) copy-start(f32[1024,64]{0,1:T(8,128)} %get-tuple-element.89) | copy-start | bytes 786436
  26.9 6.7 %copy-start.12 = (f32[1024,64]{0,1:T(8,128)S(1)}, f32[1024,64]{0,1:T(8,128)}, u32[]{:S(2)}) copy-start(f32[1024,64]{0,1:T(8,128)} %get-tuple-element.96) | copy-start | bytes 786436
  27.0 6.7 %copy-start.13 = (f32[1024,64]{0,1:T(8,128)S(1)}, f32[1024,64]{0,1:T(8,128)}, u32[]{:S(2)}) copy-start(f32[1024,64]{0,1:T(8,128)} %get-tuple-element.97) | copy-start | bytes 786436
  33.7 4.0 %copy-start.14 = (f32[32,32,128]{2,1,0:T(8,128)S(1)}, f32[32,32,128]{2,1,0:T(8,128)}, u32[]{:S(2)}) copy-start(f32[32,32,128]{2,1,0:T(8,128)} %get-tuple-element.45) | copy-start | bytes 1572868
  37.7 3.7 %copy-start.10 = (f32[32,32,128]{2,1,0:T(8,128)}, f32[32,32,128]{2,1,0:T(8,128)S(1)}, u32[]{:S(2)}) copy-start(f32[32,32,128]{2,1,0:T(8,128)S(1)} %collective-permute-done.1.above_ref.below_ref) | copy-start | bytes 1572868
  37.7 11.4 %collective-permute-start.2 = (f32[32,32,128]{2,1,0:T(8,128)S(1)}, f32[32,32,128]{2,1,0:T(8,128)S(1)}, u32[]{:S(2)}, u32[]{:S(2)}) collective-permute-start(f32[32,32,128]{2,1,0:T(8,128)S(1)} %copy-done.14), channel_id=1, source_target_pairs={{0,1},{1,0},{2,3},{3,2},{4,5},{5,4},{6,7},{7,6},{8,9},{9,8},{10,11... | collective-permute-start | bytes 1572872 | tf_op jit(solution)/shard_map/ppermute | solution.py:304
  49.1 0.8 copy-start.9
  49.9 37.6 %collective-permute-start.3 = (f32[32,32,128]{2,1,0:T(8,128)}, f32[32,32,128]{2,1,0:T(8,128)S(1)}, u32[]{:S(2)}, u32[]{:S(2)}) collective-permute-start(f32[32,32,128]{2,1,0:T(8,128)} %get-tuple-element.48), channel_id=1, source_target_pairs={{0,1},{1,0},{2,3},{3,2},{4,5},{5,4},{6,7},{7,6},{8,9},{9,8},{10,11... | collective-permute-start | bytes 1572872 | tf_op jit(solution)/shard_map/ppermute | solution.py:304
  68.8 40.6 %collective-permute-start.4 = (f32[30,32,128]{2,0,1:T(8,128)}, f32[30,32,128]{2,0,1:T(8,128)}, u32[]{:S(2)}, u32[]{:S(2)}) collective-permute-start(f32[30,32,128]{2,0,1:T(8,128)} %copy.45), channel_id=1, source_target_pairs={{0,1},{1,0},{2,3},{3,2},{4,5},{5,4},{6,7},{7,6},{8,9},{9,8},{10,11... | collective-permute-start | bytes 1474568 | tf_op jit(solution)/shard_map/ppermute | solution.py:334
  84.4 25.1 %collective-permute-start.5 = (f32[30,32,128]{2,0,1:T(8,128)}, f32[30,32,128]{2,0,1:T(8,128)}, u32[]{:S(2)}, u32[]{:S(2)}) collective-permute-start(f32[30,32,128]{2,0,1:T(8,128)} %copy.46), channel_id=1, source_target_pairs={{0,1},{1,0},{2,3},{3,2},{4,5},{5,4},{6,7},{7,6},{8,9},{9,8},{10,11... | collective-permute-start | bytes 1474568 | tf_op jit(solution)/shard_map/ppermute | solution.py:334
  87.5 0.8 copy-start.8
  93.5 4.9 %copy-start.2 = (f32[1024,1024]{0,1:T(8,128)S(1)}, f32[1024,1024]{0,1:T(8,128)}, u32[]{:S(2)}) copy-start(f32[1024,1024]{0,1:T(8,128)} %bitcast_multiply_fusion) | copy-start | bytes 12582916
  98.4 2.2 %copy-start.3 = (f32[1024,1024]{0,1:T(8,128)S(1)}, f32[1024,1024]{0,1:T(8,128)}, u32[]{:S(2)}) copy-start(f32[1024,1024]{0,1:T(8,128)} %bitcast_multiply_fusion.1) | copy-start | bytes 12582916
  98.4 2.5 %copy-start.4 = (f32[1024,256]{1,0:T(8,128)S(1)}, f32[1024,256]{1,0:T(8,128)}, u32[]{:S(2)}) copy-start(f32[1024,256]{1,0:T(8,128)} %rev.6) | copy-start | bytes 3145732
  98.4 2.8 %copy-start.7 = (f32[256,1024,1]{1,0,2:T(8,128)S(1)}, f32[256,1024,1]{1,0,2:T(8,128)}, u32[]{:S(2)}) copy-start(f32[256,1024,1]{1,0,2:T(8,128)} %copy.52) | copy-start | bytes 3145732
  103.4 2.9 %copy-start.5 = (f32[256,1024]{1,0:T(8,128)}, f32[256,1024]{1,0:T(8,128)S(1)}, u32[]{:S(2)}) copy-start(f32[256,1024]{1,0:T(8,128)S(1)} %fusion.8) | copy-start | bytes 3145732
  109.5 56.9 %all-to-all-start.1 = ((f32[16,128,256]{2,1,0:T(8,128)}), f32[16,128,256]{2,1,0:T(8,128)}, u32[]{:S(2)}, u32[]{:S(2)}) async-start(f32[16,128,256]{2,1,0:T(8,128)} %bitcast.13), calls=%async_computation.1 | async-start | bytes 4194304 | tf_op jit(solution)/shard_map/all_to_all | solution.py:379
  133.4 30.3 %collective-permute-start.6 = (f32[30,32,128]{2,0,1:T(8,128)S(1)}, f32[30,32,128]{2,0,1:T(8,128)S(1)}, u32[]{:S(2)}, u32[]{:S(2)}) collective-permute-start(f32[30,32,128]{2,0,1:T(8,128)S(1)} %copy.47), channel_id=1, source_target_pairs={{0,1},{1,0},{2,3},{3,2},{4,5},{5,4},{6,7},{7,6},{8,9},{9,8},{10,11... | collective-permute-start | bytes 1474568 | tf_op jit(solution)/shard_map/ppermute | solution.py:334
  133.7 16.6 %copy-start.6 = (f32[256,1024]{1,0:T(8,128)S(1)}, f32[256,1024]{1,0:T(8,128)}, u32[]{:S(2)}) copy-start(f32[256,1024]{1,0:T(8,128)} %copy-done.5) | copy-start | bytes 3145732
  149.1 15.4 %collective-permute-start.7 = (f32[30,32,128]{2,0,1:T(8,128)}, f32[30,32,128]{2,0,1:T(8,128)}, u32[]{:S(2)}, u32[]{:S(2)}) collective-permute-start(f32[30,32,128]{2,0,1:T(8,128)} %copy.48), channel_id=1, source_target_pairs={{0,1},{1,0},{2,3},{3,2},{4,5},{5,4},{6,7},{7,6},{8,9},{9,8},{10,11... | collective-permute-start | bytes 1474568 | tf_op jit(solution)/shard_map/ppermute | solution.py:334
  170.5 2.8 %copy-start.1 = (f32[128,32,128]{2,1,0:T(8,128)S(1)}, f32[128,32,128]{2,1,0:T(8,128)}, u32[]{:S(2)}) copy-start(f32[128,32,128]{2,1,0:T(8,128)} %own_ref.7) | copy-start | bytes 6291460

commit v3 on v2

--- a/solution.py
+++ b/solution.py
@@ -170,7 +170,7 @@
 def starlet_kernel(flags_ref, above_ref, own_ref, below_ref, duals_ref, *refs):
     sn_ref, send_ref, mid_ref, keep_ref, buf_a, buf_b = refs[-6:]
     block, local_rows, columns = own_ref.shape
-    halo = send_ref.shape[0]
+    halo = 2 ** (SCALES + 1) - 2
     extent = 2 * halo + local_rows
     pad = 2 ** SCALES
     row0 = flags_ref[0] - halo
@@ -244,11 +244,11 @@
         lo, hi = lo - 2 * dilation, hi + 2 * dilation
         smooth_rows(src, dst, dilation, max(lo, 0), min(hi, extent))
         dst[own] = dst[own] + plane
-    top = dst[pl.ds(pad, halo)]
-    bot = dst[pl.ds(pad + halo + local_rows, halo)]
+    top = dst[pl.ds(pad + halo - local_rows, local_rows)]
+    bot = dst[pl.ds(pad + halo + local_rows, local_rows)]
     swap = flags_ref[4] > 0
-    send_ref[...] = jnp.where(swap, bot, top)
-    keep_ref[...] = jnp.where(swap, top, bot)
+    send_ref[...] = rows_major(jnp.where(swap, bot, top))
+    keep_ref[...] = rows_major(jnp.where(swap, top, bot))
     mid_ref[...] = rows_major(dst[own])
 
 
@@ -261,8 +261,9 @@
     near_spec = pl.BlockSpec((block, local_rows, columns), lambda i: (i, 0, 0))
     own_spec = pl.BlockSpec((block, local_rows, columns), lambda i: (i + base, 0, 0))
     dual_spec = pl.BlockSpec((SCALES, block, local_rows, columns), lambda i: (0, i + base, 0, 0))
-    edge_spec = pl.BlockSpec((halo, block, columns), lambda i: (0, i, 0))
-    edge_shape = jax.ShapeDtypeStruct((halo, chans // groups, columns), jnp.float32)
+    assert local_rows - halo <= 2**SCALES <= halo
+    edge_spec = near_spec
+    edge_shape = jax.ShapeDtypeStruct((chans // groups, local_rows, columns), jnp.float32)
     carry_specs = [pl.BlockSpec(memory_space=pl.ANY)] * len(carry)
     return pl.pallas_call(
         starlet_kernel,
@@ -339,20 +340,10 @@
 
     def finish(self, carry):
         space_next, mid = carry
-        local_rows = mid.shape[1]
-        got = jnp.concatenate(self.sends, axis=1)
-        gap = local_rows - self.halo
-        if self.paired:
-            spill = jnp.where(
-                self.index == 0,
-                jnp.pad(got, ((gap, 0), (0, 0), (0, 0))),
-                jnp.pad(got, ((0, gap), (0, 0), (0, 0))),
-            )
-        else:
-            spill = jnp.pad(jnp.concatenate(self.keeps, axis=1), ((0, gap), (0, 0), (0, 0))) + jnp.pad(
-                got, ((gap, 0), (0, 0), (0, 0))
-            )
-        return mid + jnp.transpose(spill, (1, 0, 2)), space_next
+        space_term = mid + jnp.concatenate(self.sends, axis=0)
+        if not self.paired:
+            space_term = space_term + jnp.concatenate(self.keeps, axis=0)
+        return space_term, space_next
 
 
 def local(image_cube, data_grad, space_duals, freq_duals):

time: 183 us -> 176 us (0.962); the launches traced: 180 us -> 175 us
  local copies, waits for them, and re-layouts: 58.4 us -> 44.2 us
  waiting for transfers between devices: 11.7 us -> 21.6 us
    all_to_all x1, waiting for transfers between devices: 0.03 us -> 9.9 us  [local(): lax.all_to_all(spectral_sum.reshape(peers, chans, share), 'freq', split_a...]
    pallas_call x4 -> x0, local copies, waits for them, and re-layouts: 7.71 us -> none  [starlet(): pl.pallas_call(starlet_kernel, grid=(steps,), in_specs=[pl.BlockSpec(memo...]
    unnamed x38 -> x37, local copies, waits for them, and re-layouts: 21.9 us -> 17.4 us
    concatenate x1 -> x0, local copies, waits for them, and re-layouts: 1.89 us -> none  [finish(): got = jnp.concatenate(self.sends, axis=1)]
  transfers between devices with their start and end apart: 10 -> 10, of which waited for: 3 -> 4; matrix products, arithmetic and copies ran while one was open for 40% -> 37% of each run, Pallas kernels for 29% -> 30%
where the time goes in v3:
time: 176 us; the launch traced here: 175 us
  Pallas kernels  53.2 us (30%)
  local copies, waits for them, and re-layouts  44.2 us (25%)
  starting transfers between devices  23.9 us (14%)
  waiting for transfers between devices  21.6 us (12%)
  other arithmetic  19.8 us (11%)
  matrix products  11.8 us (7%)
    pallas_call x4, Pallas kernels, starlet(): pl.pallas_call(starlet_kernel, grid=(steps,), in_specs=[pl.BlockSpec(memo...  53.2 us
    unnamed x37, local copies, waits for them, and re-layouts  17.4 us
    ppermute x4, waiting for transfers between devices, exchange_halos(): got = lax.ppermute(part, 'rows', down + up)  11.6 us
    all_to_all x1, waiting for transfers between devices, local(): lax.all_to_all(spectral_sum.reshape(peers, chans, share), 'freq', split_a...  9.9 us
    all_to_all x1, starting transfers between devices, local(): lax.all_to_all(spectral_sum.reshape(peers, chans, share), 'freq', split_a...  9.44 us
    dot_general x2, matrix products, forward_dot(): lax.dot_general(samples, table, (((0,), (1,)), ((), ())), precision=lax.P...  7.11 us
    all_to_all x1, starting transfers between devices, local(): lax.all_to_all(pieces, 'freq', split_axis=1, concat_axis=0, tiled=True)  6.69 us
    max x1, other arithmetic, local(): jnp.maximum(image_cube - TAU_STEP * (data_grad + space_term + spectral_te...  5.68 us
  transfers between devices with their start and end apart: 10, of which 4 were waited for; matrix products, arithmetic and copies ran while one was open for 37% of the time, Pallas kernels for 30%

profile of v3, /device:TPU:13, one launch (start us, length us, event | category | flops | bytes accessed | tf_op | source)
XLA Modules:
  0.0 175.3 jit_solution(2543843245940968515)
XLA Ops:
  0.6 3.0 %copy.28 = f32[128,32,128]{0,2,1:T(8,128)} copy(f32[128,32,128]{2,1,0:T(8,128)} %own_ref.7) | data formatting | bytes 4194304 | tf_op args[0]
  3.6 6.7 %all-to-all-start = ((f32[128,16,256]{0,2,1:T(8,128)}), f32[128,16,256]{0,2,1:T(8,128)}, u32[]{:S(2)}, u32[]{:S(2)}) async-start(f32[128,16,256]{0,2,1:T(8,128)} %bitcast.40), calls=%async_computation | async-start | bytes 4194304 | tf_op jit(solution)/shard_map/all_to_all | solution.py:355
  10.3 1.3 fusion.36
  11.6 1.2 collective-permute-start
  12.9 3.1 %fusion.20 = (f32[1024,64]{0,1:T(8,128)S(1)}, f32[1024,64]{0,1:T(8,128)}, f32[1024,64]{0,1:T(8,128)}, f32[1024,64]{0,1:T(8,128)}) fusion(s32[64]{0:T(128)S(1)} %multiply_add_fusion, s32[1024]{0:T(1024)S(1)} %fusion.33, s32[1024]{0:T(1024)S(1)} %iota_multiply_fusion), kind=kLoop, calls=%fused_computation.39 | loop fusion | flops 1835008 | bytes 1057024 | tf_op jit(solution)/shard_map/cos | solution.py:118
  16.0 2.9 %copy.30 = f32[256,2048]{0,1:T(8,128)} copy(f32[256,2048]{1,0:T(8,128)} %param.7) | data formatting | bytes 4194304 | tf_op args[3]
  18.8 2.5 %reshape.327 = f32[256,1024,2]{0,2,1:T(2,128)S(1)} reshape(f32[256,2048]{0,1:T(8,128)} %copy.30) | data formatting | bytes 4194304 | tf_op jit(solution)/shard_map/reshape | solution.py:145
  21.4 2.6 %fusion.35 = (f32[256,1024,1]{0,2,1:T(1,128)S(1)}, f32[256,1024,1]{0,2,1:T(1,128)}) fusion(f32[256,1024,2]{0,2,1:T(2,128)S(1)} %reshape.327), kind=kLoop, calls=%fused_computation.69 | loop fusion | bytes 4194304 | tf_op jit(solution)/shard_map/slice | solution.py:147
  23.9 1.2 collective-permute-done.above_ref.below_ref
  25.1 1.2 collective-permute-start.1
  26.3 0.6 fusion.30
  27.0 3.7 %copy.36 = f32[256,1024,1]{1,0,2:T(8,128)} copy(f32[256,1024,1]{0,2,1:T(1,128)} %get-tuple-element.81) | data formatting | bytes 2097152
  30.6 2.4 %copy.37 = f32[256,1024,1]{1,0,2:T(8,128)} copy(f32[256,1024,1]{0,2,1:T(1,128)S(1)} %get-tuple-element.80) | data formatting | bytes 2097152
  33.0 0.6 stack.40.flags_ref
  33.6 1.3 multiply_subtract_fusion
  34.9 2.8 %collective-permute-done.1.above_ref.below_ref = f32[32,32,128]{2,1,0:T(8,128)S(1)} collective-permute-done((f32[32,32,128]{2,1,0:T(8,128)}, f32[32,32,128]{2,1,0:T(8,128)S(1)}, u32[]{:S(2)}, u32[]{:S(2)}) %collective-permute-start.1) | collective-permute-done | bytes 524320 | tf_op jit(solution)/shard_map/ppermute | solution.py:305
  37.7 1.2 collective-permute-start.2
  38.9 2.5 %bitcast_multiply_fusion.1 = f32[1024,1024]{0,1:T(8,128)} fusion(f32[1024,16,64]{0,2,1:T(8,128)S(1)} %get-tuple-element.100, f32[1024]{0:T(1024)S(1)} %compare_select_fusion.1), kind=kLoop, calls=%fused_computation.1 | loop fusion | flops 1048576 | bytes 8392704 | tf_op jit(solution)/shard_map/mul | solution.py:117
  41.4 7.7 %collective-permute-done.2.above_ref.below_ref = f32[32,32,128]{2,1,0:T(8,128)S(1)} collective-permute-done((f32[32,32,128]{2,1,0:T(8,128)S(1)}, f32[32,32,128]{2,1,0:T(8,128)S(1)}, u32[]{:S(2)}, u32[]{:S(2)}) %collective-permute-start.2) | collective-permute-done | bytes 524320 | tf_op jit(solution)/shard_map/ppermute | solution.py:305
  49.1 0.8 copy-done.9
  49.9 1.2 collective-permute-start.3
  51.1 2.5 %bitcast_multiply_fusion = f32[1024,1024]{0,1:T(8,128)} fusion(f32[1024,16,64]{0,2,1:T(8,128)S(1)} %get-tuple-element.99, f32[1024]{0:T(1024)S(1)} %compare_select_fusion), kind=kLoop, calls=%fused_computation | loop fusion | flops 1048576 | bytes 8392704 | tf_op jit(solution)/shard_map/mul | solution.py:117
  53.6 13.2 %shard_map.67 = (f32[4,128,32,128]{3,2,1,0:T(8,128)}, f32[32,32,128]{2,1,0:T(8,128)}, f32[128,32,128]{2,1,0:T(8,128)}, f32[32,32,128]{2,1,0:T(8,128)}) custom-call(s32[5]{0:T(128)} %stack.40.flags_ref, f32[32,32,128]{2,1,0:T(8,128)} %collective-permute-done.above_ref.below_ref, f32[128,32,128]{2,1,0:T(8,128)} %own_ref.7, ...), custom_call_target="tpu_custom_call" | custom-call | tf_op jit(solution)/shard_map/pallas_call | solution.py:268
  67.1 13.3 %shard_map.68 = (f32[4,128,32,128]{3,2,1,0:T(8,128)}, f32[32,32,128]{2,1,0:T(8,128)}, f32[128,32,128]{2,1,0:T(8,128)}, f32[32,32,128]{2,1,0:T(8,128)}) custom-call(s32[5]{0:T(128)} %stack.40.flags_ref, f32[32,32,128]{2,1,0:T(8,128)} %copy-done.8, f32[128,32,128]{2,1,0:T(8,128)} %own_ref.7, ...), custom_call_target="tpu_custom_call", output_to_operand_aliasing={{0}: (5, {}), {2}: (6, {})} | custom-call | tf_op jit(solution)/shard_map/pallas_call | solution.py:268
  80.4 1.2 collective-permute-start.5
  81.6 1.9 %copy.29 = f32[16,128,1,256]{3,1,0,2:T(8,128)S(1)} copy(f32[16,128,1,256]{1,3,0,2:T(8,128)} %bitcast.6) | data formatting | bytes 4194304 | tf_op jit(solution)/shard_map/all_to_all | solution.py:355
  83.6 0.8 copy-done.10
  84.5 5.2 %rev.6 = f32[1024,256]{1,0:T(8,128)} reverse(f32[1024,256]{1,0:T(8,128)S(1)} %slice.30), dimensions={0} | reverse | bytes 2097152 | tf_op jit(solution)/shard_map/rev | solution.py:143
  89.6 4.9 %fusion.6 = f32[256,1024]{1,0:T(8,128)S(1)} fusion(f32[1024,1024]{0,1:T(8,128)} %bitcast_multiply_fusion, f32[256,1024,1]{1,0,2:T(8,128)} %copy.37, f32[1024,256]{1,0:T(8,128)} %rev.6, f32[2048,256]{1,0:T(8,128)S(1)} %bitcast.36), kind=kOutput, calls=%fused_computation.14 | convolution fusion | flops 1611661312 | bytes 8388608 | tf_op jit(solution)/shard_map/dot_general | solution.py:125
  94.6 1.8 %fusion.37 = f32[1024,256]{1,0:T(8,128)S(1)} fusion(f32[1024,1024]{0,1:T(8,128)S(1)} %copy-done.2, f32[256,1024]{1,0:T(8,128)S(1)} %fusion.6), kind=kOutput, calls=%fused_computation.71 | convolution fusion | flops 1610612736 | bytes 6291456 | tf_op jit(solution)/shard_map/dot_general | solution.py:156
  96.4 0.3 copy-done.3
  97.0 0.3 copy-done.7
  97.3 2.2 %fusion.8 = f32[256,1024]{1,0:T(8,128)S(1)} fusion(f32[1024,1024]{0,1:T(8,128)S(1)} %copy-done.3, f32[256,1024,1]{1,0,2:T(8,128)S(1)} %copy-done.7, f32[1024,256]{1,0:T(8,128)S(1)} %copy-done.4, f32[2048,256]{1,0:T(8,128)S(1)} %bitcast.37), kind=kOutput, calls=%fused_computation.17 | convolution fusion | flops 1611661312 | bytes 8388608 | tf_op jit(solution)/shard_map/dot_general | solution.py:125
  99.6 2.9 %fusion.34 = (f32[1024,256]{1,0:T(8,128)}, f32[1024,256]{1,0:T(8,128)S(1)}) fusion(f32[1024,256]{1,0:T(8,128)S(1)} %fusion.37, f32[1024,1024]{0,1:T(8,128)S(1)} %copy-done.3, f32[256,1024]{1,0:T(8,128)S(1)} %fusion.8), kind=kOutput, calls=%fused_computation.68 | convolution fusion | flops 1611137024 | bytes 8388608 | tf_op jit(solution)/shard_map/dot_general | solution.py:156
  102.4 0.4 rev.7
  102.9 2.7 %pad_maximum_fusion = f32[2048,256]{1,0:T(8,128)} fusion(f32[1024,256]{1,0:T(8,128)S(1)} %rev.7, f32[1024,256]{1,0:T(8,128)} %get-tuple-element.78), kind=kLoop, calls=%fused_computation.4 | loop fusion | flops 524288 | bytes 4194304 | tf_op jit(solution)/shard_map/concatenate | solution.py:167
  105.6 9.4 %all-to-all-start.1 = ((f32[16,128,256]{2,1,0:T(8,128)}), f32[16,128,256]{2,1,0:T(8,128)}, u32[]{:S(2)}, u32[]{:S(2)}) async-start(f32[16,128,256]{2,1,0:T(8,128)} %bitcast.12), calls=%async_computation.1 | async-start | bytes 4194304 | tf_op jit(solution)/shard_map/all_to_all | solution.py:370
  115.0 13.3 %shard_map.69 = (f32[4,128,32,128]{3,2,1,0:T(8,128)}, f32[32,32,128]{2,1,0:T(8,128)}, f32[128,32,128]{2,1,0:T(8,128)}, f32[32,32,128]{2,1,0:T(8,128)}) custom-call(s32[5]{0:T(128)} %stack.40.flags_ref, f32[32,32,128]{2,1,0:T(8,128)} %copy-done.9, f32[128,32,128]{2,1,0:T(8,128)} %own_ref.7, ...), custom_call_target="tpu_custom_call", output_to_operand_aliasing={{0}: (5, {}), {2}: (6, {})} | custom-call | tf_op jit(solution)/shard_map/pallas_call | solution.py:268
  128.3 13.4 %shard_map.70 = (f32[4,128,32,128]{3,2,1,0:T(8,128)}, f32[32,32,128]{2,1,0:T(8,128)}, f32[128,32,128]{2,1,0:T(8,128)}, f32[32,32,128]{2,1,0:T(8,128)}) custom-call(s32[5]{0:T(128)} %stack.40.flags_ref, f32[32,32,128]{2,1,0:T(8,128)} %copy-done.10, f32[128,32,128]{2,1,0:T(8,128)} %own_ref.7, ...), custom_call_target="tpu_custom_call", output_to_operand_aliasing={{0}: (5, {}), {2}: (6, {})} | custom-call | tf_op jit(solution)/shard_map/pallas_call | solution.py:268
  142.0 1.2 collective-permute-start.6
  143.2 1.5 pad_maximum_fusion.1
  144.6 2.8 %copy.34 = f32[256,1024,2]{0,2,1:T(2,128)S(1)} copy(f32[256,1024,2]{1,0,2:T(8,128)} %pad_maximum_fusion.1) | data formatting | bytes 4194304 | tf_op jit(solution)/shard_map/stack | solution.py:150
  147.5 2.5 %reshape.330 = f32[256,2048]{0,1:T(8,128)} reshape(f32[256,1024,2]{0,2,1:T(2,128)S(1)} %copy.34) | data formatting | bytes 4194304 | tf_op jit(solution)/shard_map/reshape | solution.py:150
  149.9 2.9 %copy.35 = f32[256,2048]{1,0:T(8,128)} copy(f32[256,2048]{0,1:T(8,128)} %reshape.330) | data formatting | bytes 4194304
  152.8 9.9 %all-to-all-done.1 = f32[16,128,256]{2,1,0:T(8,128)} async-done(((f32[16,128,256]{2,1,0:T(8,128)}), f32[16,128,256]{2,1,0:T(8,128)}, u32[]{:S(2)}, u32[]{:S(2)}) %all-to-all-start.1) | async-done | bytes 2097184 | tf_op jit(solution)/shard_map/all_to_all | solution.py:370
  162.7 4.1 %copy.33 = f32[1,128,16,256]{3,2,1,0:T(8,128)} copy(f32[1,128,16,256]{3,1,2,0:T(8,128)} %bitcast.14) | data formatting | bytes 4194304 | tf_op jit(solution)/shard_map/all_to_all | solution.py:370
  166.9 2.8 %reshape.329 = f32[128,32,128]{2,1,0:T(8,128)} reshape(f32[1,128,16,256]{3,2,1,0:T(8,128)} %copy.33) | data formatting | bytes 4194304 | tf_op jit(solution)/shard_map/reshape | solution.py:380
  169.7 5.7 %fusion.4 = f32[128,32,128]{2,1,0:T(8,128)} fusion(f32[128,32,128]{2,1,0:T(8,128)S(1)} %copy-done.1, f32[128,32,128]{2,1,0:T(8,128)} %reshape.329, f32[128,32,128]{2,1,0:T(8,128)} %param.5, f32[128,32,128]{2,1,0:T(8,128)} %get-tuple-element.62, f32[32,32,128]{2,1,0:T(8,128)S(1)} %collective-permute-done.7, f32[32,32,128]{2,1,0:T(8,128)S(1)} %collective-permute-done.6, ...), kind=kLoop, calls=%fused_computation.10 | loop fusion | flops 4718592 | bytes 12582912 | tf_op jit(solution)/shard_map/max | solution.py:381
  (43 shorter events, 1.0 us)
Async XLA Ops:
  3.6 6.7 %copy-start = (f32[128,32,128]{2,1,0:T(8,128)S(1)}, f32[128,32,128]{2,1,0:T(8,128)}, u32[]{:S(2)}) copy-start(f32[128,32,128]{2,1,0:T(8,128)} %own_ref.7) | copy-start | bytes 6291460
  3.6 78.0 %all-to-all-start = ((f32[128,16,256]{0,2,1:T(8,128)}), f32[128,16,256]{0,2,1:T(8,128)}, u32[]{:S(2)}, u32[]{:S(2)}) async-start(f32[128,16,256]{0,2,1:T(8,128)} %bitcast.40), calls=%async_computation | async-start | bytes 4194304 | tf_op jit(solution)/shard_map/all_to_all | solution.py:355
  11.6 13.5 %collective-permute-start = (f32[32,32,128]{2,1,0:T(8,128)}, f32[32,32,128]{2,1,0:T(8,128)}, u32[]{:S(2)}, u32[]{:S(2)}) collective-permute-start(f32[32,32,128]{2,1,0:T(8,128)} %get-tuple-element.83), channel_id=1, source_target_pairs={{0,1},{1,0},{2,3},{3,2},{4,5},{5,4},{6,7},{7,6},{8,9},{9,8},{10,11... | collective-permute-start | bytes 1572872 | tf_op jit(solution)/shard_map/ppermute | solution.py:305
  25.1 12.5 %collective-permute-start.1 = (f32[32,32,128]{2,1,0:T(8,128)}, f32[32,32,128]{2,1,0:T(8,128)S(1)}, u32[]{:S(2)}, u32[]{:S(2)}) collective-permute-start(f32[32,32,128]{2,1,0:T(8,128)} %get-tuple-element.36), channel_id=1, source_target_pairs={{0,1},{1,0},{2,3},{3,2},{4,5},{5,4},{6,7},{7,6},{8,9},{9,8},{10,11... | collective-permute-start | bytes 1572872 | tf_op jit(solution)/shard_map/ppermute | solution.py:305
  26.9 6.7 %copy-start.11 = (f32[1024,64]{0,1:T(8,128)S(1)}, f32[1024,64]{0,1:T(8,128)}, u32[]{:S(2)}) copy-start(f32[1024,64]{0,1:T(8,128)} %get-tuple-element.89) | copy-start | bytes 786436
  26.9 6.7 %copy-start.12 = (f32[1024,64]{0,1:T(8,128)S(1)}, f32[1024,64]{0,1:T(8,128)}, u32[]{:S(2)}) copy-start(f32[1024,64]{0,1:T(8,128)} %get-tuple-element.96) | copy-start | bytes 786436
  26.9 6.7 %copy-start.13 = (f32[1024,64]{0,1:T(8,128)S(1)}, f32[1024,64]{0,1:T(8,128)}, u32[]{:S(2)}) copy-start(f32[1024,64]{0,1:T(8,128)} %get-tuple-element.97) | copy-start | bytes 786436
  33.6 4.0 %copy-start.15 = (f32[32,32,128]{2,1,0:T(8,128)S(1)}, f32[32,32,128]{2,1,0:T(8,128)}, u32[]{:S(2)}) copy-start(f32[32,32,128]{2,1,0:T(8,128)} %get-tuple-element.45) | copy-start | bytes 1572868
  37.7 3.7 %copy-start.8 = (f32[32,32,128]{2,1,0:T(8,128)}, f32[32,32,128]{2,1,0:T(8,128)S(1)}, u32[]{:S(2)}) copy-start(f32[32,32,128]{2,1,0:T(8,128)S(1)} %collective-permute-done.1.above_ref.below_ref) | copy-start | bytes 1572868
  37.7 11.4 %collective-permute-start.2 = (f32[32,32,128]{2,1,0:T(8,128)S(1)}, f32[32,32,128]{2,1,0:T(8,128)S(1)}, u32[]{:S(2)}, u32[]{:S(2)}) collective-permute-start(f32[32,32,128]{2,1,0:T(8,128)S(1)} %copy-done.15), channel_id=1, source_target_pairs={{0,1},{1,0},{2,3},{3,2},{4,5},{5,4},{6,7},{7,6},{8,9},{9,8},{10,11... | collective-permute-start | bytes 1572872 | tf_op jit(solution)/shard_map/ppermute | solution.py:305
  38.9 11.0 %copy-start.14 = (f32[32,32,128]{2,1,0:T(8,128)S(1)}, f32[32,32,128]{2,1,0:T(8,128)}, u32[]{:S(2)}) copy-start(f32[32,32,128]{2,1,0:T(8,128)} %get-tuple-element.48) | copy-start | bytes 1572868
  49.1 0.8 copy-start.9
  49.9 33.7 %collective-permute-start.3 = (f32[32,32,128]{2,1,0:T(8,128)S(1)}, f32[32,32,128]{2,1,0:T(8,128)S(1)}, u32[]{:S(2)}, u32[]{:S(2)}) collective-permute-start(f32[32,32,128]{2,1,0:T(8,128)S(1)} %copy-done.14), channel_id=1, source_target_pairs={{0,1},{1,0},{2,3},{3,2},{4,5},{5,4},{6,7},{7,6},{8,9},{9,8},{10,11... | collective-permute-start | bytes 1572872 | tf_op jit(solution)/shard_map/ppermute | solution.py:305
  66.8 38.7 %collective-permute-start.4 = (f32[32,32,128]{2,1,0:T(8,128)}, f32[32,32,128]{2,1,0:T(8,128)}, u32[]{:S(2)}, u32[]{:S(2)}) collective-permute-start(f32[32,32,128]{2,1,0:T(8,128)} %get-tuple-element.56), channel_id=1, source_target_pairs={{0,1},{1,0},{2,3},{3,2},{4,5},{5,4},{6,7},{7,6},{8,9},{9,8},{10,11... | collective-permute-start | bytes 1572872 | tf_op jit(solution)/shard_map/ppermute | solution.py:335
  80.4 25.1 %collective-permute-start.5 = (f32[32,32,128]{2,1,0:T(8,128)}, f32[32,32,128]{2,1,0:T(8,128)}, u32[]{:S(2)}, u32[]{:S(2)}) collective-permute-start(f32[32,32,128]{2,1,0:T(8,128)} %get-tuple-element.57), channel_id=1, source_target_pairs={{0,1},{1,0},{2,3},{3,2},{4,5},{5,4},{6,7},{7,6},{8,9},{9,8},{10,11... | collective-permute-start | bytes 1572872 | tf_op jit(solution)/shard_map/ppermute | solution.py:335
  83.5 0.8 copy-start.10
  89.6 4.9 %copy-start.2 = (f32[1024,1024]{0,1:T(8,128)S(1)}, f32[1024,1024]{0,1:T(8,128)}, u32[]{:S(2)}) copy-start(f32[1024,1024]{0,1:T(8,128)} %bitcast_multiply_fusion) | copy-start | bytes 12582916
  94.5 2.2 %copy-start.3 = (f32[1024,1024]{0,1:T(8,128)S(1)}, f32[1024,1024]{0,1:T(8,128)}, u32[]{:S(2)}) copy-start(f32[1024,1024]{0,1:T(8,128)} %bitcast_multiply_fusion.1) | copy-start | bytes 12582916
  94.5 2.5 %copy-start.4 = (f32[1024,256]{1,0:T(8,128)S(1)}, f32[1024,256]{1,0:T(8,128)}, u32[]{:S(2)}) copy-start(f32[1024,256]{1,0:T(8,128)} %rev.6) | copy-start | bytes 3145732
  94.5 2.8 %copy-start.7 = (f32[256,1024,1]{1,0,2:T(8,128)S(1)}, f32[256,1024,1]{1,0,2:T(8,128)}, u32[]{:S(2)}) copy-start(f32[256,1024,1]{1,0,2:T(8,128)} %copy.36) | copy-start | bytes 3145732
  99.5 2.9 %copy-start.5 = (f32[256,1024]{1,0:T(8,128)}, f32[256,1024]{1,0:T(8,128)S(1)}, u32[]{:S(2)}) copy-start(f32[256,1024]{1,0:T(8,128)S(1)} %fusion.8) | copy-start | bytes 3145732
  105.6 57.1 %all-to-all-start.1 = ((f32[16,128,256]{2,1,0:T(8,128)}), f32[16,128,256]{2,1,0:T(8,128)}, u32[]{:S(2)}, u32[]{:S(2)}) async-start(f32[16,128,256]{2,1,0:T(8,128)} %bitcast.12), calls=%async_computation.1 | async-start | bytes 4194304 | tf_op jit(solution)/shard_map/all_to_all | solution.py:370
  128.3 14.9 %copy-start.6 = (f32[256,1024]{1,0:T(8,128)S(1)}, f32[256,1024]{1,0:T(8,128)}, u32[]{:S(2)}) copy-start(f32[256,1024]{1,0:T(8,128)} %copy-done.5) | copy-start | bytes 3145732
  141.7 28.0 %collective-permute-start.7 = (f32[32,32,128]{2,1,0:T(8,128)}, f32[32,32,128]{2,1,0:T(8,128)S(1)}, u32[]{:S(2)}, u32[]{:S(2)}) collective-permute-start(f32[32,32,128]{2,1,0:T(8,128)} %get-tuple-element.66), channel_id=1, source_target_pairs={{0,1},{1,0},{2,3},{3,2},{4,5},{5,4},{6,7},{7,6},{8,9},{9,8},{10,11... | collective-permute-start | bytes 1572872 | tf_op jit(solution)/shard_map/ppermute | solution.py:335
  142.0 27.7 %collective-permute-start.6 = (f32[32,32,128]{2,1,0:T(8,128)}, f32[32,32,128]{2,1,0:T(8,128)S(1)}, u32[]{:S(2)}, u32[]{:S(2)}) collective-permute-start(f32[32,32,128]{2,1,0:T(8,128)} %get-tuple-element.65), channel_id=1, source_target_pairs={{0,1},{1,0},{2,3},{3,2},{4,5},{5,4},{6,7},{7,6},{8,9},{9,8},{10,11... | collective-permute-start | bytes 1572872 | tf_op jit(solution)/shard_map/ppermute | solution.py:335
  166.8 2.8 %copy-start.1 = (f32[128,32,128]{2,1,0:T(8,128)S(1)}, f32[128,32,128]{2,1,0:T(8,128)}, u32[]{:S(2)}) copy-start(f32[128,32,128]{2,1,0:T(8,128)} %own_ref.7) | copy-start | bytes 6291460

commit v4 on v3

--- a/solution.py
+++ b/solution.py
@@ -252,17 +252,17 @@
     mid_ref[...] = rows_major(dst[own])
 
 
-def starlet(flags, above, own, below, duals, halo, group, groups, carry=(), interpret=False):
+def starlet(flags, above, own, below, duals, halo, group, groups, carry=(), near_base=0, interpret=False):
     chans, local_rows, columns = own.shape
     block = math.gcd(chans, 8)
     steps = chans // block // groups
     base = group * steps
     extent = 2 * halo + local_rows + 2 * 2**SCALES
-    near_spec = pl.BlockSpec((block, local_rows, columns), lambda i: (i, 0, 0))
+    near_spec = pl.BlockSpec((block, local_rows, columns), lambda i: (i + near_base, 0, 0))
+    edge_spec = pl.BlockSpec((block, local_rows, columns), lambda i: (i, 0, 0))
     own_spec = pl.BlockSpec((block, local_rows, columns), lambda i: (i + base, 0, 0))
     dual_spec = pl.BlockSpec((SCALES, block, local_rows, columns), lambda i: (0, i + base, 0, 0))
     assert local_rows - halo <= 2**SCALES <= halo
-    edge_spec = near_spec
     edge_shape = jax.ShapeDtypeStruct((chans // groups, local_rows, columns), jnp.float32)
     carry_specs = [pl.BlockSpec(memory_space=pl.ANY)] * len(carry)
     return pl.pallas_call(
@@ -290,22 +290,28 @@
     return halo, groups, chans // groups
 
 
-def exchange_halos(image_cube):
+def exchange_halos(image_cube, early):
     chans, local_rows, columns = image_cube.shape
     halo, groups, width = row_plan(chans, local_rows)
     count = lax.axis_size("rows")
     down = [(i, i + 1) for i in range(count - 1)]
     up = [(i + 1, i) for i in range(count - 1)]
+    cuts = [(0, early), (early, groups)] if 0 < early < groups else [(0, groups)]
     halos = []
-    for group in range(groups):
-        part = image_cube[group * width : (group + 1) * width]
-        if halos:
-            part, halos[-1] = lax.optimization_barrier((part, halos[-1]))
+    previous = None
+    for first, last in cuts:
+        part = image_cube[first * width : last * width]
+        if previous is not None:
+            part, previous = lax.optimization_barrier((part, previous))
         if count == 2:
             got = lax.ppermute(part, "rows", down + up)
-            halos.append((got, got))
+            pair = (got, got)
         else:
-            halos.append((lax.ppermute(part, "rows", down), lax.ppermute(part, "rows", up)))
+            pair = (lax.ppermute(part, "rows", down), lax.ppermute(part, "rows", up))
+        previous = pair
+        block = math.gcd(chans, 8)
+        steps = width // block
+        halos.extend((pair, (group - first) * steps) for group in range(first, last))
     return halos
 
 
@@ -327,9 +333,10 @@
         self.sends, self.keeps = [], []
 
     def run(self, group, halos, carry):
-        above, below = halos[group]
+        (above, below), near_base = halos[group]
         space_next, send, mid, keep = starlet(
-            self.flags, above, self.image_cube, below, self.space_duals, self.halo, group, self.groups, carry
+            self.flags, above, self.image_cube, below, self.space_duals, self.halo, group, self.groups, carry,
+            near_base,
         )
         if self.paired:
             self.sends.append(lax.ppermute(send, "rows", self.down + self.up))
@@ -351,17 +358,18 @@
     peers = lax.axis_size("freq")
     share = local_rows * columns // peers
     pieces = image_cube.reshape(chans, peers, share)
-    halos = exchange_halos(image_cube)
+    work = Spatial(image_cube, space_duals)
+    early = work.groups // 2
+    halos = exchange_halos(image_cube, early)
     pixel_cube = lax.all_to_all(pieces, "freq", split_axis=1, concat_axis=0, tiled=True).reshape(
         chans * peers, share
     )
-    work = Spatial(image_cube, space_duals)
-    early = work.groups // 2
     carry = ()
     for group in range(early):
         carry = work.run(group, halos, carry)
-    pixel_cube, carry, later = lax.optimization_barrier((pixel_cube, carry, halos[early:]))
-    halos = halos[:early] + list(later)
+    later = [pair for pair, _ in halos[early:]]
+    pixel_cube, carry, later = lax.optimization_barrier((pixel_cube, carry, later))
+    halos = halos[:early] + [(pair, base) for pair, (_, base) in zip(later, halos[early:])]
     tables, freq_next, fresh = spectral(pixel_cube, freq_duals)
     spectral_sum = spectral_back(tables, fresh)
     spectral_sum, carry, work.sends, work.keeps = lax.optimization_barrier(

time: 176 us -> 168 us (0.955)
  waiting for transfers between devices: 21.6 us -> 14.4 us
  starting transfers between devices: 23.9 us -> 19.7 us
  local copies, waits for them, and re-layouts: 44.2 us -> 47.5 us
    ppermute x4 -> x2, waiting for transfers between devices: 11.6 us -> 4.36 us  [exchange_halos(): got = lax.ppermute(part, 'rows', down + up)]
    rev x1, local copies, waits for them, and re-layouts: 0.44 us -> 6.83 us  [spectral_back(): (parts[0] - parts[1])[::-1]]
    rev x1, local copies, waits for them, and re-layouts: 5.15 us -> 0.47 us  [spectral(): tail = pixel_cube[half:][::-1]]
    ppermute x4 -> x2, starting transfers between devices: 4.84 us -> 2.42 us  [exchange_halos(): got = lax.ppermute(part, 'rows', down + up)]
    all_to_all x1, starting transfers between devices: 9.44 us -> 7.58 us  [local(): lax.all_to_all(spectral_sum.reshape(peers, chans, share), 'freq', split_a...]
    unnamed x37 -> x25, local copies, waits for them, and re-layouts: 17.4 us -> 15.9 us
  transfers between devices with their start and end apart: 10 -> 8, of which waited for: 4 -> 2; matrix products, arithmetic and copies ran while one was open for 37% -> 41% of each run, Pallas kernels for 30% -> 32%
where the time goes in v4:
time: 168 us; the launch traced here: 167 us
  Pallas kernels  53.3 us (32%)
  local copies, waits for them, and re-layouts  47.5 us (28%)
  starting transfers between devices  19.7 us (12%)
  other arithmetic  18.8 us (11%)
  waiting for transfers between devices  14.4 us (9%)
  matrix products  12.2 us (7%)
    pallas_call x4, Pallas kernels, starlet(): pl.pallas_call(starlet_kernel, grid=(steps,), in_specs=[pl.BlockSpec(memo...  53.3 us
    unnamed x25, local copies, waits for them, and re-layouts  15.9 us
    all_to_all x1, waiting for transfers between devices, local(): lax.all_to_all(spectral_sum.reshape(peers, chans, share), 'freq', split_a...  9.99 us
    all_to_all x1, starting transfers between devices, local(): lax.all_to_all(spectral_sum.reshape(peers, chans, share), 'freq', split_a...  7.58 us
    dot_general x2, matrix products, forward_dot(): lax.dot_general(samples, table, (((0,), (1,)), ((), ())), precision=lax.P...  7.14 us
    rev x1, local copies, waits for them, and re-layouts, spectral_back(): (parts[0] - parts[1])[::-1]  6.83 us
    all_to_all x1, starting transfers between devices, local(): lax.all_to_all(pieces, 'freq', split_axis=1, concat_axis=0, tiled=True)  6.69 us
    max x1, other arithmetic, local(): jnp.maximum(image_cube - TAU_STEP * (data_grad + space_term + spectral_te...  5.68 us
  transfers between devices with their start and end apart: 8, of which 2 were waited for; matrix products, arithmetic and copies ran while one was open for 41% of the time, Pallas kernels for 32%

profile of v4, /device:TPU:13, one launch (start us, length us, event | category | flops | bytes accessed | tf_op | source)
XLA Modules:
  0.0 166.6 jit_solution(8997226355736551053)
XLA Ops:
  0.6 3.0 %copy.28 = f32[128,32,128]{0,2,1:T(8,128)} copy(f32[128,32,128]{2,1,0:T(8,128)} %own_ref.7) | data formatting | bytes 4194304 | tf_op args[0]
  3.6 6.7 %all-to-all-start = ((f32[128,16,256]{0,2,1:T(8,128)}), f32[128,16,256]{0,2,1:T(8,128)}, u32[]{:S(2)}, u32[]{:S(2)}) async-start(f32[128,16,256]{0,2,1:T(8,128)} %bitcast.40), calls=%async_computation | async-start | bytes 4194304 | tf_op jit(solution)/shard_map/all_to_all | solution.py:364
  10.3 1.5 fusion.36
  11.8 1.2 collective-permute-start
  13.0 2.9 %copy.30 = f32[256,2048]{0,1:T(8,128)} copy(f32[256,2048]{1,0:T(8,128)} %param.7) | data formatting | bytes 4194304 | tf_op args[3]
  15.9 2.5 %reshape.327 = f32[256,1024,2]{0,2,1:T(2,128)S(1)} reshape(f32[256,2048]{0,1:T(8,128)} %copy.30) | data formatting | bytes 4194304 | tf_op jit(solution)/shard_map/reshape | solution.py:145
  18.4 2.9 %fusion.35 = (f32[256,1024,1]{0,2,1:T(1,128)}, f32[256,1024,1]{0,2,1:T(1,128)}) fusion(f32[256,1024,2]{0,2,1:T(2,128)S(1)} %reshape.327), kind=kLoop, calls=%fused_computation.69 | loop fusion | bytes 4194304 | tf_op jit(solution)/shard_map/slice | solution.py:147
  21.3 3.7 %copy.36 = f32[256,1024,1]{1,0,2:T(8,128)} copy(f32[256,1024,1]{0,2,1:T(1,128)} %get-tuple-element.65) | data formatting | bytes 2097152
  25.1 2.4 %copy.37 = f32[256,1024,1]{1,0,2:T(8,128)} copy(f32[256,1024,1]{0,2,1:T(1,128)S(1)} %copy-done.7) | data formatting | bytes 2097152
  27.5 0.6 stack.40.flags_ref
  28.1 0.6 fusion.30
  28.7 2.1 %fusion.20 = (f32[1024,64]{0,1:T(8,128)S(1)}, f32[1024,64]{0,1:T(8,128)S(1)}, f32[1024,64]{0,1:T(8,128)S(1)}, f32[1024,64]{0,1:T(8,128)S(1)}) fusion(s32[64]{0:T(128)S(1)} %multiply_add_fusion, s32[1024]{0:T(1024)S(1)} %fusion.33, s32[1024]{0:T(1024)S(1)} %iota_multiply_fusion), kind=kLoop, calls=%fused_computation.39 | loop fusion | flops 1835008 | bytes 1057024 | tf_op jit(solution)/shard_map/cos | solution.py:118
  30.8 1.3 multiply_subtract_fusion
  32.1 4.4 %collective-permute-done.above_ref.below_ref = f32[64,32,128]{2,1,0:T(8,128)S(1)} collective-permute-done((f32[64,32,128]{2,1,0:T(8,128)}, f32[64,32,128]{2,1,0:T(8,128)S(1)}, u32[]{:S(2)}, u32[]{:S(2)}) %collective-permute-start) | collective-permute-done | bytes 1048608 | tf_op jit(solution)/shard_map/ppermute | solution.py:307
  36.5 1.2 collective-permute-start.1
  37.7 2.5 %bitcast_multiply_fusion.1 = f32[1024,1024]{0,1:T(8,128)} fusion(f32[1024,16,64]{0,2,1:T(8,128)S(1)} %get-tuple-element.82, f32[1024]{0:T(1024)S(1)} %compare_select_fusion.1), kind=kLoop, calls=%fused_computation.1 | loop fusion | flops 1048576 | bytes 8392704 | tf_op jit(solution)/shard_map/mul | solution.py:117
  40.2 2.5 %bitcast_multiply_fusion = f32[1024,1024]{0,1:T(8,128)} fusion(f32[1024,16,64]{0,2,1:T(8,128)S(1)} %get-tuple-element.81, f32[1024]{0:T(1024)S(1)} %compare_select_fusion), kind=kLoop, calls=%fused_computation | loop fusion | flops 1048576 | bytes 8392704 | tf_op jit(solution)/shard_map/mul | solution.py:117
  42.7 13.2 %shard_map.67 = (f32[4,128,32,128]{3,2,1,0:T(8,128)}, f32[32,32,128]{2,1,0:T(8,128)}, f32[128,32,128]{2,1,0:T(8,128)}, f32[32,32,128]{2,1,0:T(8,128)}) custom-call(s32[5]{0:T(128)} %stack.40.flags_ref, f32[64,32,128]{2,1,0:T(8,128)} %copy-done.4, f32[128,32,128]{2,1,0:T(8,128)} %own_ref.7, f32[64,32,128]{2,1,0:T(8,128)} %copy-done.4, ...), custom_call_target="tpu_custom_call" | custom-call | tf_op jit(solution)/shard_map/pallas_call | solution.py:268
  55.9 13.5 %shard_map.68 = (f32[4,128,32,128]{3,2,1,0:T(8,128)}, f32[32,32,128]{2,1,0:T(8,128)}, f32[128,32,128]{2,1,0:T(8,128)}, f32[32,32,128]{2,1,0:T(8,128)}) custom-call(s32[5]{0:T(128)} %stack.40.flags_ref, f32[64,32,128]{2,1,0:T(8,128)} %copy-done.4, f32[128,32,128]{2,1,0:T(8,128)} %own_ref.7, ...), custom_call_target="tpu_custom_call", output_to_operand_aliasing={{0}: (5, {}), {2}: (6, {})} | custom-call | tf_op jit(solution)/shard_map/pallas_call | solution.py:268
  69.4 0.3 collective-permute-start.3
  69.7 1.2 collective-permute-start.2
  70.9 0.0 all-to-all-done
  70.9 2.9 %copy.29 = f32[16,128,1,256]{3,1,0,2:T(8,128)} copy(f32[16,128,1,256]{1,3,0,2:T(8,128)} %bitcast.6) | data formatting | bytes 4194304 | tf_op jit(solution)/shard_map/all_to_all | solution.py:364
  73.8 0.0 collective-permute-done.1.above_ref.below_ref
  73.8 1.7 %slice.22 = f32[1024,256]{1,0:T(8,128)S(1)} slice(f32[2048,256]{1,0:T(8,128)} %bitcast.35), slice={[1024:2048], [0:256]} | slice | bytes 2097152 | tf_op jit(solution)/shard_map/slice | solution.py:143
  75.4 0.5 rev.6
  76.0 4.9 %fusion.6 = f32[256,1024]{1,0:T(8,128)S(1)} fusion(f32[1024,1024]{0,1:T(8,128)} %bitcast_multiply_fusion, f32[256,1024,1]{1,0,2:T(8,128)} %copy.37, f32[1024,256]{1,0:T(8,128)S(1)} %rev.6, f32[2048,256]{1,0:T(8,128)} %bitcast.36), kind=kOutput, calls=%fused_computation.14 | convolution fusion | flops 1611661312 | bytes 8388608 | tf_op jit(solution)/shard_map/dot_general | solution.py:125
  80.9 0.0 copy-start.6
  80.9 1.8 %fusion.37 = f32[1024,256]{1,0:T(8,128)S(1)} fusion(f32[1024,1024]{0,1:T(8,128)S(1)} %copy-done.2, f32[256,1024]{1,0:T(8,128)S(1)} %fusion.6), kind=kOutput, calls=%fused_computation.71 | convolution fusion | flops 1610612736 | bytes 6291456 | tf_op jit(solution)/shard_map/dot_general | solution.py:156
  82.8 0.3 copy-done.3
  83.1 0.7 copy-done.6
  83.7 2.2 %fusion.8 = f32[256,1024]{1,0:T(8,128)S(1)} fusion(f32[1024,1024]{0,1:T(8,128)S(1)} %copy-done.3, f32[256,1024,1]{1,0,2:T(8,128)S(1)} %copy-done.8, f32[1024,256]{1,0:T(8,128)S(1)} %rev.6, f32[2048,256]{1,0:T(8,128)S(1)} %bitcast.37), kind=kOutput, calls=%fused_computation.17 | convolution fusion | flops 1611661312 | bytes 8388608 | tf_op jit(solution)/shard_map/dot_general | solution.py:125
  86.0 3.2 %fusion.34 = (f32[1024,256]{1,0:T(8,128)}, f32[1024,256]{1,0:T(8,128)}) fusion(f32[1024,256]{1,0:T(8,128)S(1)} %fusion.37, f32[1024,1024]{0,1:T(8,128)S(1)} %copy-done.3, f32[256,1024]{1,0:T(8,128)S(1)} %fusion.8), kind=kOutput, calls=%fused_computation.68 | convolution fusion | flops 1611137024 | bytes 8388608 | tf_op jit(solution)/shard_map/dot_general | solution.py:156
  89.2 6.8 %rev.7 = f32[1024,256]{1,0:T(8,128)S(1)} reverse(f32[1024,256]{1,0:T(8,128)} %get-tuple-element.63), dimensions={0} | reverse | bytes 2097152 | tf_op jit(solution)/shard_map/rev | solution.py:167
  96.0 2.7 %pad_maximum_fusion = f32[2048,256]{1,0:T(8,128)} fusion(f32[1024,256]{1,0:T(8,128)S(1)} %rev.7, f32[1024,256]{1,0:T(8,128)} %get-tuple-element.62), kind=kLoop, calls=%fused_computation.4 | loop fusion | flops 524288 | bytes 4194304 | tf_op jit(solution)/shard_map/concatenate | solution.py:167
  98.7 7.6 %all-to-all-start.1 = ((f32[16,128,256]{2,1,0:T(8,128)}), f32[16,128,256]{2,1,0:T(8,128)}, u32[]{:S(2)}, u32[]{:S(2)}) async-start(f32[16,128,256]{2,1,0:T(8,128)} %bitcast.41), calls=%async_computation.1 | async-start | bytes 4194304 | tf_op jit(solution)/shard_map/all_to_all | solution.py:378
  106.3 13.3 %shard_map.69 = (f32[4,128,32,128]{3,2,1,0:T(8,128)}, f32[32,32,128]{2,1,0:T(8,128)}, f32[128,32,128]{2,1,0:T(8,128)}, f32[32,32,128]{2,1,0:T(8,128)}) custom-call(s32[5]{0:T(128)} %stack.40.flags_ref, f32[64,32,128]{2,1,0:T(8,128)} %copy-done.5, f32[128,32,128]{2,1,0:T(8,128)} %own_ref.7, ...), custom_call_target="tpu_custom_call", output_to_operand_aliasing={{0}: (5, {}), {2}: (6, {})} | custom-call | tf_op jit(solution)/shard_map/pallas_call | solution.py:268
  119.6 13.3 %shard_map.70 = (f32[4,128,32,128]{3,2,1,0:T(8,128)}, f32[32,32,128]{2,1,0:T(8,128)}, f32[128,32,128]{2,1,0:T(8,128)}, f32[32,32,128]{2,1,0:T(8,128)}) custom-call(s32[5]{0:T(128)} %stack.40.flags_ref, f32[64,32,128]{2,1,0:T(8,128)} %copy-done.5, f32[128,32,128]{2,1,0:T(8,128)} %own_ref.7, ...), custom_call_target="tpu_custom_call", output_to_operand_aliasing={{0}: (5, {}), {2}: (6, {})} | custom-call | tf_op jit(solution)/shard_map/pallas_call | solution.py:268
  132.9 0.3 collective-permute-start.5
  133.2 1.2 collective-permute-start.4
  134.4 1.5 pad_maximum_fusion.1
  135.9 2.8 %copy.34 = f32[256,1024,2]{0,2,1:T(2,128)S(1)} copy(f32[256,1024,2]{1,0,2:T(8,128)} %pad_maximum_fusion.1) | data formatting | bytes 4194304 | tf_op jit(solution)/shard_map/stack | solution.py:150
  138.7 2.4 %reshape.330 = f32[256,2048]{0,1:T(8,128)} reshape(f32[256,1024,2]{0,2,1:T(2,128)S(1)} %copy.34) | data formatting | bytes 4194304 | tf_op jit(solution)/shard_map/reshape | solution.py:150
  141.2 2.9 %copy.35 = f32[256,2048]{1,0:T(8,128)} copy(f32[256,2048]{0,1:T(8,128)} %reshape.330) | data formatting | bytes 4194304
  144.0 10.0 %all-to-all-done.1 = f32[16,128,256]{2,1,0:T(8,128)} async-done(((f32[16,128,256]{2,1,0:T(8,128)}), f32[16,128,256]{2,1,0:T(8,128)}, u32[]{:S(2)}, u32[]{:S(2)}) %all-to-all-start.1) | async-done | bytes 2097184 | tf_op jit(solution)/shard_map/all_to_all | solution.py:378
  154.0 4.1 %copy.33 = f32[1,128,16,256]{3,2,1,0:T(8,128)} copy(f32[1,128,16,256]{3,1,2,0:T(8,128)} %bitcast.14) | data formatting | bytes 4194304 | tf_op jit(solution)/shard_map/all_to_all | solution.py:378
  158.1 2.8 %reshape.329 = f32[128,32,128]{2,1,0:T(8,128)} reshape(f32[1,128,16,256]{3,2,1,0:T(8,128)} %copy.33) | data formatting | bytes 4194304 | tf_op jit(solution)/shard_map/reshape | solution.py:388
  160.9 5.7 %fusion.4 = f32[128,32,128]{2,1,0:T(8,128)} fusion(f32[128,32,128]{2,1,0:T(8,128)S(1)} %copy-done.1, f32[128,32,128]{2,1,0:T(8,128)} %reshape.329, f32[128,32,128]{2,1,0:T(8,128)} %param.5, f32[128,32,128]{2,1,0:T(8,128)} %get-tuple-element.46, f32[32,32,128]{2,1,0:T(8,128)S(1)} %collective-permute-done.5, f32[32,32,128]{2,1,0:T(8,128)S(1)} %collective-permute-done.4, ...), kind=kLoop, calls=%fused_computation.10 | loop fusion | flops 4718592 | bytes 12582912 | tf_op jit(solution)/shard_map/max | solution.py:389
  (27 shorter events, 0.1 us)
Async XLA Ops:
  3.6 6.7 %copy-start = (f32[128,32,128]{2,1,0:T(8,128)S(1)}, f32[128,32,128]{2,1,0:T(8,128)}, u32[]{:S(2)}) copy-start(f32[128,32,128]{2,1,0:T(8,128)} %own_ref.7) | copy-start | bytes 6291460
  3.6 67.3 %all-to-all-start = ((f32[128,16,256]{0,2,1:T(8,128)}), f32[128,16,256]{0,2,1:T(8,128)}, u32[]{:S(2)}, u32[]{:S(2)}) async-start(f32[128,16,256]{0,2,1:T(8,128)} %bitcast.40), calls=%async_computation | async-start | bytes 4194304 | tf_op jit(solution)/shard_map/all_to_all | solution.py:364
  11.8 24.7 %collective-permute-start = (f32[64,32,128]{2,1,0:T(8,128)}, f32[64,32,128]{2,1,0:T(8,128)S(1)}, u32[]{:S(2)}, u32[]{:S(2)}) collective-permute-start(f32[64,32,128]{2,1,0:T(8,128)} %get-tuple-element.67), channel_id=1, source_target_pairs={{0,1},{1,0},{2,3},{3,2},{4,5},{5,4},{6,7},{7,6},{8,9},{9,8},{10,11... | collective-permute-start | bytes 3145736 | tf_op jit(solution)/shard_map/ppermute | solution.py:307
  21.3 3.7 %copy-start.7 = (f32[256,1024,1]{0,2,1:T(1,128)S(1)}, f32[256,1024,1]{0,2,1:T(1,128)}, u32[]{:S(2)}) copy-start(f32[256,1024,1]{0,2,1:T(1,128)} %get-tuple-element.64) | copy-start | bytes 3145732
  30.8 5.7 %copy-start.9 = (f32[64,32,128]{2,1,0:T(8,128)S(1)}, f32[64,32,128]{2,1,0:T(8,128)}, u32[]{:S(2)}) copy-start(f32[64,32,128]{2,1,0:T(8,128)} %get-tuple-element.32) | copy-start | bytes 3145732
  36.5 3.7 %copy-start.4 = (f32[64,32,128]{2,1,0:T(8,128)}, f32[64,32,128]{2,1,0:T(8,128)S(1)}, u32[]{:S(2)}) copy-start(f32[64,32,128]{2,1,0:T(8,128)S(1)} %collective-permute-done.above_ref.below_ref) | copy-start | bytes 3145732
  36.5 37.3 %collective-permute-start.1 = (f32[64,32,128]{2,1,0:T(8,128)S(1)}, f32[64,32,128]{2,1,0:T(8,128)S(1)}, u32[]{:S(2)}, u32[]{:S(2)}) collective-permute-start(f32[64,32,128]{2,1,0:T(8,128)S(1)} %copy-done.9), channel_id=1, source_target_pairs={{0,1},{1,0},{2,3},{3,2},{4,5},{5,4},{6,7},{7,6},{8,9},{9,8},{10,11... | collective-permute-start | bytes 3145736 | tf_op jit(solution)/shard_map/ppermute | solution.py:307
  69.4 29.3 %collective-permute-start.3 = (f32[32,32,128]{2,1,0:T(8,128)}, f32[32,32,128]{2,1,0:T(8,128)}, u32[]{:S(2)}, u32[]{:S(2)}) collective-permute-start(f32[32,32,128]{2,1,0:T(8,128)} %get-tuple-element.41), channel_id=1, source_target_pairs={{0,1},{1,0},{2,3},{3,2},{4,5},{5,4},{6,7},{7,6},{8,9},{9,8},{10,11... | collective-permute-start | bytes 1572872 | tf_op jit(solution)/shard_map/ppermute | solution.py:342
  69.7 29.0 %collective-permute-start.2 = (f32[32,32,128]{2,1,0:T(8,128)}, f32[32,32,128]{2,1,0:T(8,128)}, u32[]{:S(2)}, u32[]{:S(2)}) collective-permute-start(f32[32,32,128]{2,1,0:T(8,128)} %get-tuple-element.40), channel_id=1, source_target_pairs={{0,1},{1,0},{2,3},{3,2},{4,5},{5,4},{6,7},{7,6},{8,9},{9,8},{10,11... | collective-permute-start | bytes 1572872 | tf_op jit(solution)/shard_map/ppermute | solution.py:342
  73.8 2.2 %copy-start.5 = (f32[64,32,128]{2,1,0:T(8,128)}, f32[64,32,128]{2,1,0:T(8,128)S(1)}, u32[]{:S(2)}) copy-start(f32[64,32,128]{2,1,0:T(8,128)S(1)} %collective-permute-done.1.above_ref.below_ref) | copy-start | bytes 3145732
  75.9 4.9 %copy-start.2 = (f32[1024,1024]{0,1:T(8,128)S(1)}, f32[1024,1024]{0,1:T(8,128)}, u32[]{:S(2)}) copy-start(f32[1024,1024]{0,1:T(8,128)} %bitcast_multiply_fusion) | copy-start | bytes 12582916
  75.9 6.8 %copy-start.8 = (f32[256,1024,1]{1,0,2:T(8,128)S(1)}, f32[256,1024,1]{1,0,2:T(8,128)}, u32[]{:S(2)}) copy-start(f32[256,1024,1]{1,0,2:T(8,128)} %copy.36) | copy-start | bytes 3145732
  80.9 2.2 %copy-start.3 = (f32[1024,1024]{0,1:T(8,128)S(1)}, f32[1024,1024]{0,1:T(8,128)}, u32[]{:S(2)}) copy-start(f32[1024,1024]{0,1:T(8,128)} %bitcast_multiply_fusion.1) | copy-start | bytes 12582916
  80.9 2.9 %copy-start.6 = (f32[16,128,1,256]{3,1,0,2:T(8,128)S(1)}, f32[16,128,1,256]{3,1,0,2:T(8,128)}, u32[]{:S(2)}) copy-start(f32[16,128,1,256]{3,1,0,2:T(8,128)} %copy.29) | copy-start | bytes 6291460
  98.7 55.3 %all-to-all-start.1 = ((f32[16,128,256]{2,1,0:T(8,128)}), f32[16,128,256]{2,1,0:T(8,128)}, u32[]{:S(2)}, u32[]{:S(2)}) async-start(f32[16,128,256]{2,1,0:T(8,128)} %bitcast.41), calls=%async_computation.1 | async-start | bytes 4194304 | tf_op jit(solution)/shard_map/all_to_all | solution.py:378
  132.9 28.0 %collective-permute-start.5 = (f32[32,32,128]{2,1,0:T(8,128)}, f32[32,32,128]{2,1,0:T(8,128)S(1)}, u32[]{:S(2)}, u32[]{:S(2)}) collective-permute-start(f32[32,32,128]{2,1,0:T(8,128)} %get-tuple-element.50), channel_id=1, source_target_pairs={{0,1},{1,0},{2,3},{3,2},{4,5},{5,4},{6,7},{7,6},{8,9},{9,8},{10,11... | collective-permute-start | bytes 1572872 | tf_op jit(solution)/shard_map/ppermute | solution.py:342
  133.2 27.7 %collective-permute-start.4 = (f32[32,32,128]{2,1,0:T(8,128)}, f32[32,32,128]{2,1,0:T(8,128)S(1)}, u32[]{:S(2)}, u32[]{:S(2)}) collective-permute-start(f32[32,32,128]{2,1,0:T(8,128)} %get-tuple-element.49), channel_id=1, source_target_pairs={{0,1},{1,0},{2,3},{3,2},{4,5},{5,4},{6,7},{7,6},{8,9},{9,8},{10,11... | collective-permute-start | bytes 1572872 | tf_op jit(solution)/shard_map/ppermute | solution.py:342
  158.1 2.8 %copy-start.1 = (f32[128,32,128]{2,1,0:T(8,128)S(1)}, f32[128,32,128]{2,1,0:T(8,128)}, u32[]{:S(2)}) copy-start(f32[128,32,128]{2,1,0:T(8,128)} %own_ref.7) | copy-start | bytes 6291460

commit v5 on v4

--- a/solution.py
+++ b/solution.py
@@ -347,10 +347,34 @@
 
     def finish(self, carry):
         space_next, mid = carry
-        space_term = mid + jnp.concatenate(self.sends, axis=0)
+        got = jnp.concatenate(self.sends, axis=0)
         if not self.paired:
-            space_term = space_term + jnp.concatenate(self.keeps, axis=0)
-        return space_term, space_next
+            got = got + jnp.concatenate(self.keeps, axis=0)
+        return mid, got, space_next
+
+
+def combine_kernel(image_ref, grad_ref, mid_ref, got_ref, returned_ref, out_ref):
+    block, local_rows, columns = image_ref.shape
+    slabs = [returned_ref[:, pl.ds(row * columns, columns)] for row in range(local_rows)]
+    spectral_term = jnp.swapaxes(jnp.stack(slabs, axis=0), 0, 1)
+    space_term = mid_ref[...] + got_ref[...]
+    out_ref[...] = jnp.maximum(
+        image_ref[...] - TAU_STEP * (grad_ref[...] + space_term + spectral_term), 0.0
+    )
+
+
+def combine(image_cube, data_grad, mid, got, returned):
+    chans, local_rows, columns = image_cube.shape
+    block = math.gcd(chans, 8)
+    plane_spec = pl.BlockSpec((block, local_rows, columns), lambda i: (i, 0, 0))
+    flat_spec = pl.BlockSpec((block, local_rows * columns), lambda i: (i, 0))
+    return pl.pallas_call(
+        combine_kernel,
+        grid=(chans // block,),
+        in_specs=[plane_spec, plane_spec, plane_spec, plane_spec, flat_spec],
+        out_specs=plane_spec,
+        out_shape=jax.ShapeDtypeStruct(image_cube.shape, jnp.float32),
+    )(image_cube, data_grad, mid, got, returned)
 
 
 def local(image_cube, data_grad, space_duals, freq_duals):
@@ -384,9 +408,8 @@
     )
     for group in range(early, work.groups):
         carry = work.run(group, halos, carry)
-    space_term, space_next = work.finish(carry)
-    spectral_term = returned.reshape(chans, local_rows, columns)
-    image_next = jnp.maximum(image_cube - TAU_STEP * (data_grad + space_term + spectral_term), 0.0)
+    mid, got, space_next = work.finish(carry)
+    image_next = combine(image_cube, data_grad, mid, got, returned.reshape(chans, local_rows * columns))
     return (image_next, space_next, freq_next)
 
 

time: 168 us -> 178 us (1.060); the launches traced: 167 us -> 174 us
  Pallas kernels: 53.3 us -> 64.2 us
  other arithmetic: 18.8 us -> 15.8 us
  local copies, waits for them, and re-layouts: 47.5 us -> 45 us
  waiting for transfers between devices: 14.4 us -> 16.7 us
    ppermute x4, waiting for transfers between devices: 0.01 us -> 13.5 us  [run(): self.sends.append(lax.ppermute(send, 'rows', self.down + self.up))]
    pallas_call x0 -> x1, Pallas kernels: none -> 11 us  [combine(): pl.pallas_call(combine_kernel, grid=(chans // block,), in_specs=[plane_sp...]
    all_to_all x1, waiting for transfers between devices: 9.99 us -> 0.01 us  [local(): lax.all_to_all(spectral_sum.reshape(peers, chans, share), 'freq', split_a...]
    max x1 -> x0, other arithmetic: 5.68 us -> none  [local(): jnp.maximum(image_cube - TAU_STEP * (data_grad + space_term + spectral_te...]
    unnamed x25 -> x22, local copies, waits for them, and re-layouts: 15.9 us -> 20.3 us
    all_to_all x1 -> x0, local copies, waits for them, and re-layouts: 4.13 us -> none  [local(): lax.all_to_all(spectral_sum.reshape(peers, chans, share), 'freq', split_a...]
    reshape x1 -> x0, local copies, waits for them, and re-layouts: 2.78 us -> none  [local(): spectral_term = returned.reshape(chans, local_rows, columns)]
    concatenate x0 -> x1, other arithmetic: none -> 2.66 us  [finish(): got = jnp.concatenate(self.sends, axis=0)]
  transfers between devices with their start and end apart: 8 -> 8, of which waited for: 2 -> 3; matrix products, arithmetic and copies ran while one was open for 41% -> 38% of each run, Pallas kernels for 32% -> 31%
where the time goes in v5:
time: 178 us; the launch traced here: 174 us
  Pallas kernels  64.2 us (36%)
  local copies, waits for them, and re-layouts  45 us (25%)
  starting transfers between devices  19.5 us (11%)
  waiting for transfers between devices  16.7 us (9%)
  other arithmetic  15.8 us (9%)
  matrix products  12.2 us (7%)
    pallas_call x4, Pallas kernels, starlet(): pl.pallas_call(starlet_kernel, grid=(steps,), in_specs=[pl.BlockSpec(memo...  53.2 us
    unnamed x22, local copies, waits for them, and re-layouts  20.3 us
    ppermute x4, waiting for transfers between devices, run(): self.sends.append(lax.ppermute(send, 'rows', self.down + self.up))  13.5 us
    pallas_call x1, Pallas kernels, combine(): pl.pallas_call(combine_kernel, grid=(chans // block,), in_specs=[plane_sp...  11 us
    all_to_all x1, starting transfers between devices, local(): lax.all_to_all(spectral_sum.reshape(peers, chans, share), 'freq', split_a...  7.59 us
    dot_general x2, matrix products, forward_dot(): lax.dot_general(samples, table, (((0,), (1,)), ((), ())), precision=lax.P...  7.14 us
    rev x1, local copies, waits for them, and re-layouts, spectral_back(): (parts[0] - parts[1])[::-1]  6.83 us
    all_to_all x1, starting transfers between devices, local(): lax.all_to_all(pieces, 'freq', split_axis=1, concat_axis=0, tiled=True)  6.55 us
  transfers between devices with their start and end apart: 8, of which 3 were waited for; matrix products, arithmetic and copies ran while one was open for 38% of the time, Pallas kernels for 31%

profile of v5, /device:TPU:13, one launch (start us, length us, event | category | flops | bytes accessed | tf_op | source)
XLA Modules:
  0.0 174.2 jit_solution(14875714281214041438)
XLA Ops:
  0.6 0.0 copy-start
  0.6 3.1 %copy.28 = f32[128,32,128]{0,2,1:T(8,128)} copy(f32[128,32,128]{2,1,0:T(8,128)} %image_ref.1) | data formatting | bytes 4194304 | tf_op args[0]
  3.8 6.6 %all-to-all-start = ((f32[128,16,256]{0,2,1:T(8,128)}), f32[128,16,256]{0,2,1:T(8,128)}, u32[]{:S(2)}, u32[]{:S(2)}) async-start(f32[128,16,256]{0,2,1:T(8,128)} %bitcast.43), calls=%async_computation | async-start | bytes 4194304 | tf_op jit(solution)/shard_map/all_to_all | solution.py:388
  10.3 1.5 fusion.31
  11.8 1.2 collective-permute-start
  13.0 2.9 %copy.30 = f32[256,2048]{0,1:T(8,128)} copy(f32[256,2048]{1,0:T(8,128)} %param.7) | data formatting | bytes 4194304 | tf_op args[3]
  15.9 2.5 %reshape.327 = f32[256,1024,2]{0,2,1:T(2,128)S(1)} reshape(f32[256,2048]{0,1:T(8,128)} %copy.30) | data formatting | bytes 4194304 | tf_op jit(solution)/shard_map/reshape | solution.py:145
  18.4 2.9 %fusion.30 = (f32[256,1024,1]{0,2,1:T(1,128)}, f32[256,1024,1]{0,2,1:T(1,128)}) fusion(f32[256,1024,2]{0,2,1:T(2,128)S(1)} %reshape.327), kind=kLoop, calls=%fused_computation.64 | loop fusion | bytes 4194304 | tf_op jit(solution)/shard_map/slice | solution.py:147
  21.3 3.6 %copy.37 = f32[256,1024,1]{1,0,2:T(8,128)} copy(f32[256,1024,1]{0,2,1:T(1,128)} %get-tuple-element.64) | data formatting | bytes 2097152
  24.9 3.6 %copy.36 = f32[256,1024,1]{1,0,2:T(8,128)} copy(f32[256,1024,1]{0,2,1:T(1,128)} %get-tuple-element.65) | data formatting | bytes 2097152
  28.6 0.7 stack.40.flags_ref
  29.3 0.6 fusion.25
  29.9 2.1 %fusion.15 = (f32[1024,64]{0,1:T(8,128)S(1)}, f32[1024,64]{0,1:T(8,128)S(1)}, f32[1024,64]{0,1:T(8,128)S(1)}, f32[1024,64]{0,1:T(8,128)S(1)}) fusion(s32[64]{0:T(128)S(1)} %multiply_add_fusion, s32[1024]{0:T(1024)S(1)} %fusion.28, s32[1024]{0:T(1024)S(1)} %iota_multiply_fusion), kind=kLoop, calls=%fused_computation.34 | loop fusion | flops 1835008 | bytes 1057024 | tf_op jit(solution)/shard_map/cos | solution.py:118
  32.0 0.0 copy-start.7
  32.0 1.3 multiply_subtract_fusion
  33.3 3.2 %collective-permute-done.above_ref.below_ref = f32[64,32,128]{2,1,0:T(8,128)S(1)} collective-permute-done((f32[64,32,128]{2,1,0:T(8,128)}, f32[64,32,128]{2,1,0:T(8,128)S(1)}, u32[]{:S(2)}, u32[]{:S(2)}) %collective-permute-start) | collective-permute-done | bytes 1048608 | tf_op jit(solution)/shard_map/ppermute | solution.py:307
  36.5 1.2 collective-permute-start.1
  37.7 2.5 %bitcast_multiply_fusion = f32[1024,1024]{0,1:T(8,128)} fusion(f32[1024,16,64]{0,2,1:T(8,128)S(1)} %get-tuple-element.81, f32[1024]{0:T(1024)S(1)} %compare_select_fusion), kind=kLoop, calls=%fused_computation | loop fusion | flops 1048576 | bytes 8392704 | tf_op jit(solution)/shard_map/mul | solution.py:117
  40.3 2.5 %bitcast_multiply_fusion.1 = f32[1024,1024]{0,1:T(8,128)} fusion(f32[1024,16,64]{0,2,1:T(8,128)S(1)} %get-tuple-element.82, f32[1024]{0:T(1024)S(1)} %compare_select_fusion.1), kind=kLoop, calls=%fused_computation.1 | loop fusion | flops 1048576 | bytes 8392704 | tf_op jit(solution)/shard_map/mul | solution.py:117
  42.7 13.2 %shard_map.67 = (f32[4,128,32,128]{3,2,1,0:T(8,128)}, f32[32,32,128]{2,1,0:T(8,128)}, f32[128,32,128]{2,1,0:T(8,128)}, f32[32,32,128]{2,1,0:T(8,128)}) custom-call(s32[5]{0:T(128)} %stack.40.flags_ref, f32[64,32,128]{2,1,0:T(8,128)} %copy-done.3, f32[128,32,128]{2,1,0:T(8,128)} %image_ref.1, f32[64,32,128]{2,1,0:T(8,128)} %copy-done.3, ...), custom_call_target="tpu_custom_call" | custom-call | tf_op jit(solution)/shard_map/pallas_call | solution.py:268
  55.9 0.3 collective-permute-start.2
  56.2 13.3 %shard_map.68 = (f32[4,128,32,128]{3,2,1,0:T(8,128)}, f32[32,32,128]{2,1,0:T(8,128)}, f32[128,32,128]{2,1,0:T(8,128)}, f32[32,32,128]{2,1,0:T(8,128)}) custom-call(s32[5]{0:T(128)} %stack.40.flags_ref, f32[64,32,128]{2,1,0:T(8,128)} %copy-done.3, f32[128,32,128]{2,1,0:T(8,128)} %image_ref.1, ...), custom_call_target="tpu_custom_call", output_to_operand_aliasing={{0}: (5, {}), {2}: (6, {})} | custom-call | tf_op jit(solution)/shard_map/pallas_call | solution.py:268
  69.5 1.2 collective-permute-start.3
  70.7 2.9 %copy.29 = f32[16,128,1,256]{3,1,0,2:T(8,128)} copy(f32[16,128,1,256]{1,3,0,2:T(8,128)} %bitcast.6) | data formatting | bytes 4194304 | tf_op jit(solution)/shard_map/all_to_all | solution.py:388
  73.6 1.7 slice.22
  75.3 0.5 rev.6
  75.8 4.9 %fusion.1 = f32[256,1024]{1,0:T(8,128)S(1)} fusion(f32[1024,1024]{0,1:T(8,128)} %bitcast_multiply_fusion, f32[256,1024,1]{1,0,2:T(8,128)} %copy.37, f32[1024,256]{1,0:T(8,128)S(1)} %rev.6, f32[2048,256]{1,0:T(8,128)} %bitcast.39), kind=kOutput, calls=%fused_computation.9 | convolution fusion | flops 1611661312 | bytes 8388608 | tf_op jit(solution)/shard_map/dot_general | solution.py:125
  80.7 1.8 %fusion.32 = f32[1024,256]{1,0:T(8,128)S(1)} fusion(f32[1024,1024]{0,1:T(8,128)S(1)} %copy-done.1, f32[256,1024]{1,0:T(8,128)S(1)} %fusion.1), kind=kOutput, calls=%fused_computation.66 | convolution fusion | flops 1610612736 | bytes 6291456 | tf_op jit(solution)/shard_map/dot_general | solution.py:156
  82.6 0.3 copy-done.2
  82.9 0.7 copy-done.5
  83.5 2.2 %fusion.3 = f32[256,1024]{1,0:T(8,128)S(1)} fusion(f32[1024,1024]{0,1:T(8,128)S(1)} %copy-done.2, f32[256,1024,1]{1,0,2:T(8,128)S(1)} %copy-done.6, f32[1024,256]{1,0:T(8,128)S(1)} %rev.6, f32[2048,256]{1,0:T(8,128)S(1)} %bitcast.40), kind=kOutput, calls=%fused_computation.12 | convolution fusion | flops 1611661312 | bytes 8388608 | tf_op jit(solution)/shard_map/dot_general | solution.py:125
  85.8 3.2 %fusion.29 = (f32[1024,256]{1,0:T(8,128)}, f32[1024,256]{1,0:T(8,128)}) fusion(f32[1024,256]{1,0:T(8,128)S(1)} %fusion.32, f32[1024,1024]{0,1:T(8,128)S(1)} %copy-done.2, f32[256,1024]{1,0:T(8,128)S(1)} %fusion.3), kind=kOutput, calls=%fused_computation.63 | convolution fusion | flops 1611137024 | bytes 8388608 | tf_op jit(solution)/shard_map/dot_general | solution.py:156
  89.0 6.8 %rev.7 = f32[1024,256]{1,0:T(8,128)S(1)} reverse(f32[1024,256]{1,0:T(8,128)} %get-tuple-element.63), dimensions={0} | reverse | bytes 2097152 | tf_op jit(solution)/shard_map/rev | solution.py:167
  95.8 2.7 %pad_maximum_fusion = f32[2048,256]{1,0:T(8,128)} fusion(f32[1024,256]{1,0:T(8,128)S(1)} %rev.7, f32[1024,256]{1,0:T(8,128)} %get-tuple-element.62), kind=kLoop, calls=%fused_computation.4 | loop fusion | flops 524288 | bytes 4194304 | tf_op jit(solution)/shard_map/concatenate | solution.py:167
  98.5 7.6 %all-to-all-start.1 = ((f32[16,128,256]{2,1,0:T(8,128)}), f32[16,128,256]{2,1,0:T(8,128)}, u32[]{:S(2)}, u32[]{:S(2)}) async-start(f32[16,128,256]{2,1,0:T(8,128)} %bitcast.44), calls=%async_computation.1 | async-start | bytes 4194304 | tf_op jit(solution)/shard_map/all_to_all | solution.py:402
  106.1 13.3 %shard_map.69 = (f32[4,128,32,128]{3,2,1,0:T(8,128)}, f32[32,32,128]{2,1,0:T(8,128)}, f32[128,32,128]{2,1,0:T(8,128)}, f32[32,32,128]{2,1,0:T(8,128)}) custom-call(s32[5]{0:T(128)} %stack.40.flags_ref, f32[64,32,128]{2,1,0:T(8,128)} %copy-done.4, f32[128,32,128]{2,1,0:T(8,128)} %image_ref.1, ...), custom_call_target="tpu_custom_call", output_to_operand_aliasing={{0}: (5, {}), {2}: (6, {})} | custom-call | tf_op jit(solution)/shard_map/pallas_call | solution.py:268
  119.4 13.3 %shard_map.70 = (f32[4,128,32,128]{3,2,1,0:T(8,128)}, f32[32,32,128]{2,1,0:T(8,128)}, f32[128,32,128]{2,1,0:T(8,128)}, f32[32,32,128]{2,1,0:T(8,128)}) custom-call(s32[5]{0:T(128)} %stack.40.flags_ref, f32[64,32,128]{2,1,0:T(8,128)} %copy-done.4, f32[128,32,128]{2,1,0:T(8,128)} %image_ref.1, ...), custom_call_target="tpu_custom_call", output_to_operand_aliasing={{0}: (5, {}), {2}: (6, {})} | custom-call | tf_op jit(solution)/shard_map/pallas_call | solution.py:268
  132.7 0.3 collective-permute-start.5
  133.0 1.2 collective-permute-start.4
  134.2 1.5 pad_maximum_fusion.2
  135.7 2.8 %copy.34 = f32[256,1024,2]{0,2,1:T(2,128)S(1)} copy(f32[256,1024,2]{1,0,2:T(8,128)} %pad_maximum_fusion.2) | data formatting | bytes 4194304 | tf_op jit(solution)/shard_map/stack | solution.py:150
  138.5 2.4 %reshape.330 = f32[256,2048]{0,1:T(8,128)} reshape(f32[256,1024,2]{0,2,1:T(2,128)S(1)} %copy.34) | data formatting | bytes 4194304 | tf_op jit(solution)/shard_map/reshape | solution.py:150
  141.0 2.9 %copy.35 = f32[256,2048]{1,0:T(8,128)} copy(f32[256,2048]{0,1:T(8,128)} %reshape.330) | data formatting | bytes 4194304
  143.8 2.3 %collective-permute-done.5 = f32[32,32,128]{2,1,0:T(8,128)S(1)} collective-permute-done((f32[32,32,128]{2,1,0:T(8,128)}, f32[32,32,128]{2,1,0:T(8,128)S(1)}, u32[]{:S(2)}, u32[]{:S(2)}) %collective-permute-start.5) | collective-permute-done | bytes 524320 | tf_op jit(solution)/shard_map/ppermute | solution.py:342
  146.1 11.2 %collective-permute-done.4 = f32[32,32,128]{2,1,0:T(8,128)S(1)} collective-permute-done((f32[32,32,128]{2,1,0:T(8,128)}, f32[32,32,128]{2,1,0:T(8,128)S(1)}, u32[]{:S(2)}, u32[]{:S(2)}) %collective-permute-start.4) | collective-permute-done | bytes 524320 | tf_op jit(solution)/shard_map/ppermute | solution.py:342
  157.4 2.7 %pad_maximum_fusion.1.got_ref = f32[128,32,128]{2,1,0:T(8,128)} fusion(f32[32,32,128]{2,1,0:T(8,128)S(1)} %collective-permute-done.5, f32[32,32,128]{2,1,0:T(8,128)S(1)} %collective-permute-done.4, f32[32,32,128]{2,1,0:T(8,128)} %collective-permute-done.3, f32[32,32,128]{2,1,0:T(8,128)} %collective-permute-done.2), kind=kLoop, calls=%fused_computation.5 | loop fusion | flops 1572864 | bytes 4194304 | tf_op jit(solution)/shard_map/concatenate | solution.py:350
  160.0 3.2 %copy.38 = f32[16,8,16,256]{3,1,2,0:T(8,128)} copy(f32[16,8,16,256]{3,1,0,2:T(8,128)} %bitcast.28) | data formatting | bytes 4194304
  163.2 11.0 %shard_map.71 = f32[128,32,128]{2,1,0:T(8,128)} custom-call(f32[128,32,128]{2,1,0:T(8,128)} %image_ref.1, f32[128,32,128]{2,1,0:T(8,128)} %grad_ref.1, f32[128,32,128]{2,1,0:T(8,128)} %get-tuple-element.46.mid_ref, f32[128,32,128]{2,1,0:T(8,128)} %pad_maximum_fusion.1.got_ref, f32[128,4096]{1,0:T(8,128)} %bitcast.45), custom_call_target="tpu_custom_call" | custom-call | tf_op jit(solution)/shard_map/pallas_call | solution.py:371
  (23 shorter events, 0.1 us)
Async XLA Ops:
  0.6 9.7 %copy-start = (f32[128,32,128]{2,1,0:T(8,128)S(1)}, f32[128,32,128]{2,1,0:T(8,128)}, u32[]{:S(2)}) copy-start(f32[128,32,128]{2,1,0:T(8,128)} %image_ref.1) | copy-start | bytes 6291460
  3.8 66.9 %all-to-all-start = ((f32[128,16,256]{0,2,1:T(8,128)}), f32[128,16,256]{0,2,1:T(8,128)}, u32[]{:S(2)}, u32[]{:S(2)}) async-start(f32[128,16,256]{0,2,1:T(8,128)} %bitcast.43), calls=%async_computation | async-start | bytes 4194304 | tf_op jit(solution)/shard_map/all_to_all | solution.py:388
  11.8 24.7 %collective-permute-start = (f32[64,32,128]{2,1,0:T(8,128)}, f32[64,32,128]{2,1,0:T(8,128)S(1)}, u32[]{:S(2)}, u32[]{:S(2)}) collective-permute-start(f32[64,32,128]{2,1,0:T(8,128)} %get-tuple-element.67), channel_id=1, source_target_pairs={{0,1},{1,0},{2,3},{3,2},{4,5},{5,4},{6,7},{7,6},{8,9},{9,8},{10,11... | collective-permute-start | bytes 3145736 | tf_op jit(solution)/shard_map/ppermute | solution.py:307
  32.0 4.5 %copy-start.7 = (f32[64,32,128]{2,1,0:T(8,128)S(1)}, f32[64,32,128]{2,1,0:T(8,128)}, u32[]{:S(2)}) copy-start(f32[64,32,128]{2,1,0:T(8,128)} %get-tuple-element.32) | copy-start | bytes 3145732
  36.5 3.8 %copy-start.3 = (f32[64,32,128]{2,1,0:T(8,128)}, f32[64,32,128]{2,1,0:T(8,128)S(1)}, u32[]{:S(2)}) copy-start(f32[64,32,128]{2,1,0:T(8,128)S(1)} %collective-permute-done.above_ref.below_ref) | copy-start | bytes 3145732
  36.5 37.1 %collective-permute-start.1 = (f32[64,32,128]{2,1,0:T(8,128)S(1)}, f32[64,32,128]{2,1,0:T(8,128)S(1)}, u32[]{:S(2)}, u32[]{:S(2)}) collective-permute-start(f32[64,32,128]{2,1,0:T(8,128)S(1)} %copy-done.7), channel_id=1, source_target_pairs={{0,1},{1,0},{2,3},{3,2},{4,5},{5,4},{6,7},{7,6},{8,9},{9,8},{10,11... | collective-permute-start | bytes 3145736 | tf_op jit(solution)/shard_map/ppermute | solution.py:307
  55.9 42.6 %collective-permute-start.2 = (f32[32,32,128]{2,1,0:T(8,128)}, f32[32,32,128]{2,1,0:T(8,128)}, u32[]{:S(2)}, u32[]{:S(2)}) collective-permute-start(f32[32,32,128]{2,1,0:T(8,128)} %get-tuple-element.40), channel_id=1, source_target_pairs={{0,1},{1,0},{2,3},{3,2},{4,5},{5,4},{6,7},{7,6},{8,9},{9,8},{10,11... | collective-permute-start | bytes 1572872 | tf_op jit(solution)/shard_map/ppermute | solution.py:342
  69.5 29.0 %collective-permute-start.3 = (f32[32,32,128]{2,1,0:T(8,128)}, f32[32,32,128]{2,1,0:T(8,128)}, u32[]{:S(2)}, u32[]{:S(2)}) collective-permute-start(f32[32,32,128]{2,1,0:T(8,128)} %get-tuple-element.41), channel_id=1, source_target_pairs={{0,1},{1,0},{2,3},{3,2},{4,5},{5,4},{6,7},{7,6},{8,9},{9,8},{10,11... | collective-permute-start | bytes 1572872 | tf_op jit(solution)/shard_map/ppermute | solution.py:342
  73.6 7.1 %copy-start.4 = (f32[64,32,128]{2,1,0:T(8,128)}, f32[64,32,128]{2,1,0:T(8,128)S(1)}, u32[]{:S(2)}) copy-start(f32[64,32,128]{2,1,0:T(8,128)S(1)} %collective-permute-done.1.above_ref.below_ref) | copy-start | bytes 3145732
  75.7 4.9 %copy-start.1 = (f32[1024,1024]{0,1:T(8,128)S(1)}, f32[1024,1024]{0,1:T(8,128)}, u32[]{:S(2)}) copy-start(f32[1024,1024]{0,1:T(8,128)} %bitcast_multiply_fusion) | copy-start | bytes 12582916
  75.7 6.8 %copy-start.6 = (f32[256,1024,1]{1,0,2:T(8,128)S(1)}, f32[256,1024,1]{1,0,2:T(8,128)}, u32[]{:S(2)}) copy-start(f32[256,1024,1]{1,0,2:T(8,128)} %copy.36) | copy-start | bytes 3145732
  80.7 2.2 %copy-start.2 = (f32[1024,1024]{0,1:T(8,128)S(1)}, f32[1024,1024]{0,1:T(8,128)}, u32[]{:S(2)}) copy-start(f32[1024,1024]{0,1:T(8,128)} %bitcast_multiply_fusion.1) | copy-start | bytes 12582916
  80.7 2.9 %copy-start.5 = (f32[16,128,1,256]{3,1,0,2:T(8,128)S(1)}, f32[16,128,1,256]{3,1,0,2:T(8,128)}, u32[]{:S(2)}) copy-start(f32[16,128,1,256]{3,1,0,2:T(8,128)} %copy.29) | copy-start | bytes 6291460
  98.5 61.5 %all-to-all-start.1 = ((f32[16,128,256]{2,1,0:T(8,128)}), f32[16,128,256]{2,1,0:T(8,128)}, u32[]{:S(2)}, u32[]{:S(2)}) async-start(f32[16,128,256]{2,1,0:T(8,128)} %bitcast.44), calls=%async_computation.1 | async-start | bytes 4194304 | tf_op jit(solution)/shard_map/all_to_all | solution.py:402
  132.7 13.4 %collective-permute-start.5 = (f32[32,32,128]{2,1,0:T(8,128)}, f32[32,32,128]{2,1,0:T(8,128)S(1)}, u32[]{:S(2)}, u32[]{:S(2)}) collective-permute-start(f32[32,32,128]{2,1,0:T(8,128)} %get-tuple-element.50), channel_id=1, source_target_pairs={{0,1},{1,0},{2,3},{3,2},{4,5},{5,4},{6,7},{7,6},{8,9},{9,8},{10,11... | collective-permute-start | bytes 1572872 | tf_op jit(solution)/shard_map/ppermute | solution.py:342
  133.0 24.3 %collective-permute-start.4 = (f32[32,32,128]{2,1,0:T(8,128)}, f32[32,32,128]{2,1,0:T(8,128)S(1)}, u32[]{:S(2)}, u32[]{:S(2)}) collective-permute-start(f32[32,32,128]{2,1,0:T(8,128)} %get-tuple-element.49), channel_id=1, source_target_pairs={{0,1},{1,0},{2,3},{3,2},{4,5},{5,4},{6,7},{7,6},{8,9},{9,8},{10,11... | collective-permute-start | bytes 1572872 | tf_op jit(solution)/shard_map/ppermute | solution.py:342

commit v6 on v4

--- a/solution.py
+++ b/solution.py
@@ -168,7 +168,7 @@
 
 
 def starlet_kernel(flags_ref, above_ref, own_ref, below_ref, duals_ref, *refs):
-    sn_ref, send_ref, mid_ref, keep_ref, buf_a, buf_b = refs[-6:]
+    sn_ref, send_ref, mid_ref, keep_ref, buf_a, buf_b, planes = refs[-7:]
     block, local_rows, columns = own_ref.shape
     halo = 2 ** (SCALES + 1) - 2
     extent = 2 * halo + local_rows
@@ -213,7 +213,6 @@
     def rows_major(value):
         return jnp.swapaxes(value, 0, 1)
 
-    buf_a[...] = jnp.zeros_like(buf_a)
     above = rows_major(above_ref[...])[local_rows - halo :]
     below = rows_major(below_ref[...])[:halo]
     buf_a[pl.ds(pad, halo)] = jnp.where(flags_ref[2] > 0, above, 0.0)
@@ -229,9 +228,10 @@
         lo, hi = lo + 2 * dilation, hi - 2 * dilation
         smooth_rows(src, dst, dilation, lo, hi)
         plane = jnp.clip(
-            duals_ref[level_idx] + SIGMA * rows_major(src[own] - dst[own]), -SPACE_BOUND, SPACE_BOUND
-        )
-        sn_ref[level_idx] = plane
+            rows_major(duals_ref[level_idx]) + SIGMA * (src[own] - dst[own]), -SPACE_BOUND, SPACE_BOUND
+        )
+        planes[level_idx] = plane
+        sn_ref[level_idx] = rows_major(plane)
 
     buf_a[...] = jnp.zeros_like(buf_a)
     buf_b[...] = jnp.zeros_like(buf_b)
@@ -239,7 +239,7 @@
     for count, level_idx in enumerate(reversed(range(SCALES))):
         dilation = 2**level_idx
         src, dst = bufs[count % 2], bufs[(count + 1) % 2]
-        plane = rows_major(sn_ref[level_idx])
+        plane = planes[level_idx]
         src[own] = src[own] - plane
         lo, hi = lo - 2 * dilation, hi + 2 * dilation
         smooth_rows(src, dst, dilation, max(lo, 0), min(hi, extent))
@@ -276,7 +276,8 @@
             jax.ShapeDtypeStruct(own.shape, jnp.float32),
             edge_shape,
         ],
-        scratch_shapes=[pltpu.VMEM((extent, block, columns), jnp.float32)] * 2,
+        scratch_shapes=[pltpu.VMEM((extent, block, columns), jnp.float32)] * 2
+        + [pltpu.VMEM((SCALES, local_rows, block, columns), jnp.float32)],
         input_output_aliases={5: 0, 6: 2} if carry else {},
         interpret=interpret,
     )(flags, above, own, below, duals, *carry)

time: 168 us -> 168 us (level)
  no operation moved by 1% of the time
where the time goes in v6:
time: 168 us; the launch traced here: 167 us
  Pallas kernels  53.5 us (32%)
  local copies, waits for them, and re-layouts  47.5 us (28%)
  starting transfers between devices  19.7 us (12%)
  other arithmetic  18.8 us (11%)
  waiting for transfers between devices  14.2 us (8%)
  matrix products  12.2 us (7%)
    pallas_call x4, Pallas kernels, starlet(): pl.pallas_call(starlet_kernel, grid=(steps,), in_specs=[pl.BlockSpec(memo...  53.5 us
    unnamed x25, local copies, waits for them, and re-layouts  15.9 us
    all_to_all x1, waiting for transfers between devices, local(): lax.all_to_all(spectral_sum.reshape(peers, chans, share), 'freq', split_a...  9.87 us
    all_to_all x1, starting transfers between devices, local(): lax.all_to_all(spectral_sum.reshape(peers, chans, share), 'freq', split_a...  7.58 us
    dot_general x2, matrix products, forward_dot(): lax.dot_general(samples, table, (((0,), (1,)), ((), ())), precision=lax.P...  7.14 us
    rev x1, local copies, waits for them, and re-layouts, spectral_back(): (parts[0] - parts[1])[::-1]  6.83 us
    all_to_all x1, starting transfers between devices, local(): lax.all_to_all(pieces, 'freq', split_axis=1, concat_axis=0, tiled=True)  6.69 us
    max x1, other arithmetic, local(): jnp.maximum(image_cube - TAU_STEP * (data_grad + space_term + spectral_te...  5.68 us
  transfers between devices with their start and end apart: 8, of which 2 were waited for; matrix products, arithmetic and copies ran while one was open for 41% of the time, Pallas kernels for 32%

profile of v6, /device:TPU:13, one launch (start us, length us, event | category | flops | bytes accessed | tf_op | source)
XLA Modules:
  0.0 166.7 jit_solution(9850488653351939258)
XLA Ops:
  0.6 3.0 %copy.28 = f32[128,32,128]{0,2,1:T(8,128)} copy(f32[128,32,128]{2,1,0:T(8,128)} %own_ref.7) | data formatting | bytes 4194304 | tf_op args[0]
  3.6 6.7 %all-to-all-start = ((f32[128,16,256]{0,2,1:T(8,128)}), f32[128,16,256]{0,2,1:T(8,128)}, u32[]{:S(2)}, u32[]{:S(2)}) async-start(f32[128,16,256]{0,2,1:T(8,128)} %bitcast.40), calls=%async_computation | async-start | bytes 4194304 | tf_op jit(solution)/shard_map/all_to_all | solution.py:365
  10.3 1.5 fusion.36
  11.8 1.2 collective-permute-start
  13.0 2.9 %copy.30 = f32[256,2048]{0,1:T(8,128)} copy(f32[256,2048]{1,0:T(8,128)} %param.7) | data formatting | bytes 4194304 | tf_op args[3]
  15.9 2.5 %reshape.327 = f32[256,1024,2]{0,2,1:T(2,128)S(1)} reshape(f32[256,2048]{0,1:T(8,128)} %copy.30) | data formatting | bytes 4194304 | tf_op jit(solution)/shard_map/reshape | solution.py:145
  18.4 2.9 %fusion.35 = (f32[256,1024,1]{0,2,1:T(1,128)}, f32[256,1024,1]{0,2,1:T(1,128)}) fusion(f32[256,1024,2]{0,2,1:T(2,128)S(1)} %reshape.327), kind=kLoop, calls=%fused_computation.69 | loop fusion | bytes 4194304 | tf_op jit(solution)/shard_map/slice | solution.py:147
  21.3 3.7 %copy.36 = f32[256,1024,1]{1,0,2:T(8,128)} copy(f32[256,1024,1]{0,2,1:T(1,128)} %get-tuple-element.65) | data formatting | bytes 2097152
  25.1 2.4 %copy.37 = f32[256,1024,1]{1,0,2:T(8,128)} copy(f32[256,1024,1]{0,2,1:T(1,128)S(1)} %copy-done.7) | data formatting | bytes 2097152
  27.5 0.6 stack.40.flags_ref
  28.1 0.6 fusion.30
  28.7 2.1 %fusion.20 = (f32[1024,64]{0,1:T(8,128)S(1)}, f32[1024,64]{0,1:T(8,128)S(1)}, f32[1024,64]{0,1:T(8,128)S(1)}, f32[1024,64]{0,1:T(8,128)S(1)}) fusion(s32[64]{0:T(128)S(1)} %multiply_add_fusion, s32[1024]{0:T(1024)S(1)} %fusion.33, s32[1024]{0:T(1024)S(1)} %iota_multiply_fusion), kind=kLoop, calls=%fused_computation.39 | loop fusion | flops 1835008 | bytes 1057024 | tf_op jit(solution)/shard_map/cos | solution.py:118
  30.8 1.3 multiply_subtract_fusion
  32.1 4.4 %collective-permute-done.above_ref.below_ref = f32[64,32,128]{2,1,0:T(8,128)S(1)} collective-permute-done((f32[64,32,128]{2,1,0:T(8,128)}, f32[64,32,128]{2,1,0:T(8,128)S(1)}, u32[]{:S(2)}, u32[]{:S(2)}) %collective-permute-start) | collective-permute-done | bytes 1048608 | tf_op jit(solution)/shard_map/ppermute | solution.py:308
  36.5 1.2 collective-permute-start.1
  37.7 2.5 %bitcast_multiply_fusion.1 = f32[1024,1024]{0,1:T(8,128)} fusion(f32[1024,16,64]{0,2,1:T(8,128)S(1)} %get-tuple-element.82, f32[1024]{0:T(1024)S(1)} %compare_select_fusion.1), kind=kLoop, calls=%fused_computation.1 | loop fusion | flops 1048576 | bytes 8392704 | tf_op jit(solution)/shard_map/mul | solution.py:117
  40.2 2.5 %bitcast_multiply_fusion = f32[1024,1024]{0,1:T(8,128)} fusion(f32[1024,16,64]{0,2,1:T(8,128)S(1)} %get-tuple-element.81, f32[1024]{0:T(1024)S(1)} %compare_select_fusion), kind=kLoop, calls=%fused_computation | loop fusion | flops 1048576 | bytes 8392704 | tf_op jit(solution)/shard_map/mul | solution.py:117
  42.7 13.3 %shard_map.67 = (f32[4,128,32,128]{3,2,1,0:T(8,128)}, f32[32,32,128]{2,1,0:T(8,128)}, f32[128,32,128]{2,1,0:T(8,128)}, f32[32,32,128]{2,1,0:T(8,128)}) custom-call(s32[5]{0:T(128)} %stack.40.flags_ref, f32[64,32,128]{2,1,0:T(8,128)} %copy-done.4, f32[128,32,128]{2,1,0:T(8,128)} %own_ref.7, f32[64,32,128]{2,1,0:T(8,128)} %copy-done.4, ...), custom_call_target="tpu_custom_call" | custom-call | tf_op jit(solution)/shard_map/pallas_call | solution.py:268
  56.0 13.5 %shard_map.68 = (f32[4,128,32,128]{3,2,1,0:T(8,128)}, f32[32,32,128]{2,1,0:T(8,128)}, f32[128,32,128]{2,1,0:T(8,128)}, f32[32,32,128]{2,1,0:T(8,128)}) custom-call(s32[5]{0:T(128)} %stack.40.flags_ref, f32[64,32,128]{2,1,0:T(8,128)} %copy-done.4, f32[128,32,128]{2,1,0:T(8,128)} %own_ref.7, ...), custom_call_target="tpu_custom_call", output_to_operand_aliasing={{0}: (5, {}), {2}: (6, {})} | custom-call | tf_op jit(solution)/shard_map/pallas_call | solution.py:268
  69.5 0.3 collective-permute-start.3
  69.8 1.2 collective-permute-start.2
  71.0 0.0 all-to-all-done
  71.0 2.9 %copy.29 = f32[16,128,1,256]{3,1,0,2:T(8,128)} copy(f32[16,128,1,256]{1,3,0,2:T(8,128)} %bitcast.6) | data formatting | bytes 4194304 | tf_op jit(solution)/shard_map/all_to_all | solution.py:365
  73.9 0.0 collective-permute-done.1.above_ref.below_ref
  73.9 1.7 %slice.22 = f32[1024,256]{1,0:T(8,128)S(1)} slice(f32[2048,256]{1,0:T(8,128)} %bitcast.35), slice={[1024:2048], [0:256]} | slice | bytes 2097152 | tf_op jit(solution)/shard_map/slice | solution.py:143
  75.6 0.5 rev.6
  76.1 4.9 %fusion.6 = f32[256,1024]{1,0:T(8,128)S(1)} fusion(f32[1024,1024]{0,1:T(8,128)} %bitcast_multiply_fusion, f32[256,1024,1]{1,0,2:T(8,128)} %copy.37, f32[1024,256]{1,0:T(8,128)S(1)} %rev.6, f32[2048,256]{1,0:T(8,128)} %bitcast.36), kind=kOutput, calls=%fused_computation.14 | convolution fusion | flops 1611661312 | bytes 8388608 | tf_op jit(solution)/shard_map/dot_general | solution.py:125
  81.0 0.0 copy-start.6
  81.0 1.8 %fusion.37 = f32[1024,256]{1,0:T(8,128)S(1)} fusion(f32[1024,1024]{0,1:T(8,128)S(1)} %copy-done.2, f32[256,1024]{1,0:T(8,128)S(1)} %fusion.6), kind=kOutput, calls=%fused_computation.71 | convolution fusion | flops 1610612736 | bytes 6291456 | tf_op jit(solution)/shard_map/dot_general | solution.py:156
  82.9 0.3 copy-done.3
  83.2 0.7 copy-done.6
  83.9 2.2 %fusion.8 = f32[256,1024]{1,0:T(8,128)S(1)} fusion(f32[1024,1024]{0,1:T(8,128)S(1)} %copy-done.3, f32[256,1024,1]{1,0,2:T(8,128)S(1)} %copy-done.8, f32[1024,256]{1,0:T(8,128)S(1)} %rev.6, f32[2048,256]{1,0:T(8,128)S(1)} %bitcast.37), kind=kOutput, calls=%fused_computation.17 | convolution fusion | flops 1611661312 | bytes 8388608 | tf_op jit(solution)/shard_map/dot_general | solution.py:125
  86.1 3.2 %fusion.34 = (f32[1024,256]{1,0:T(8,128)}, f32[1024,256]{1,0:T(8,128)}) fusion(f32[1024,256]{1,0:T(8,128)S(1)} %fusion.37, f32[1024,1024]{0,1:T(8,128)S(1)} %copy-done.3, f32[256,1024]{1,0:T(8,128)S(1)} %fusion.8), kind=kOutput, calls=%fused_computation.68 | convolution fusion | flops 1611137024 | bytes 8388608 | tf_op jit(solution)/shard_map/dot_general | solution.py:156
  89.3 6.8 %rev.7 = f32[1024,256]{1,0:T(8,128)S(1)} reverse(f32[1024,256]{1,0:T(8,128)} %get-tuple-element.63), dimensions={0} | reverse | bytes 2097152 | tf_op jit(solution)/shard_map/rev | solution.py:167
  96.2 2.7 %pad_maximum_fusion = f32[2048,256]{1,0:T(8,128)} fusion(f32[1024,256]{1,0:T(8,128)S(1)} %rev.7, f32[1024,256]{1,0:T(8,128)} %get-tuple-element.62), kind=kLoop, calls=%fused_computation.4 | loop fusion | flops 524288 | bytes 4194304 | tf_op jit(solution)/shard_map/concatenate | solution.py:167
  98.8 7.6 %all-to-all-start.1 = ((f32[16,128,256]{2,1,0:T(8,128)}), f32[16,128,256]{2,1,0:T(8,128)}, u32[]{:S(2)}, u32[]{:S(2)}) async-start(f32[16,128,256]{2,1,0:T(8,128)} %bitcast.41), calls=%async_computation.1 | async-start | bytes 4194304 | tf_op jit(solution)/shard_map/all_to_all | solution.py:379
  106.4 13.4 %shard_map.69 = (f32[4,128,32,128]{3,2,1,0:T(8,128)}, f32[32,32,128]{2,1,0:T(8,128)}, f32[128,32,128]{2,1,0:T(8,128)}, f32[32,32,128]{2,1,0:T(8,128)}) custom-call(s32[5]{0:T(128)} %stack.40.flags_ref, f32[64,32,128]{2,1,0:T(8,128)} %copy-done.5, f32[128,32,128]{2,1,0:T(8,128)} %own_ref.7, ...), custom_call_target="tpu_custom_call", output_to_operand_aliasing={{0}: (5, {}), {2}: (6, {})} | custom-call | tf_op jit(solution)/shard_map/pallas_call | solution.py:268
  119.8 13.4 %shard_map.70 = (f32[4,128,32,128]{3,2,1,0:T(8,128)}, f32[32,32,128]{2,1,0:T(8,128)}, f32[128,32,128]{2,1,0:T(8,128)}, f32[32,32,128]{2,1,0:T(8,128)}) custom-call(s32[5]{0:T(128)} %stack.40.flags_ref, f32[64,32,128]{2,1,0:T(8,128)} %copy-done.5, f32[128,32,128]{2,1,0:T(8,128)} %own_ref.7, ...), custom_call_target="tpu_custom_call", output_to_operand_aliasing={{0}: (5, {}), {2}: (6, {})} | custom-call | tf_op jit(solution)/shard_map/pallas_call | solution.py:268
  133.2 0.3 collective-permute-start.5
  133.5 1.2 collective-permute-start.4
  134.7 1.5 pad_maximum_fusion.1
  136.1 2.8 %copy.34 = f32[256,1024,2]{0,2,1:T(2,128)S(1)} copy(f32[256,1024,2]{1,0,2:T(8,128)} %pad_maximum_fusion.1) | data formatting | bytes 4194304 | tf_op jit(solution)/shard_map/stack | solution.py:150
  139.0 2.4 %reshape.330 = f32[256,2048]{0,1:T(8,128)} reshape(f32[256,1024,2]{0,2,1:T(2,128)S(1)} %copy.34) | data formatting | bytes 4194304 | tf_op jit(solution)/shard_map/reshape | solution.py:150
  141.4 2.9 %copy.35 = f32[256,2048]{1,0:T(8,128)} copy(f32[256,2048]{0,1:T(8,128)} %reshape.330) | data formatting | bytes 4194304
  144.3 9.9 %all-to-all-done.1 = f32[16,128,256]{2,1,0:T(8,128)} async-done(((f32[16,128,256]{2,1,0:T(8,128)}), f32[16,128,256]{2,1,0:T(8,128)}, u32[]{:S(2)}, u32[]{:S(2)}) %all-to-all-start.1) | async-done | bytes 2097184 | tf_op jit(solution)/shard_map/all_to_all | solution.py:379
  154.1 4.1 %copy.33 = f32[1,128,16,256]{3,2,1,0:T(8,128)} copy(f32[1,128,16,256]{3,1,2,0:T(8,128)} %bitcast.14) | data formatting | bytes 4194304 | tf_op jit(solution)/shard_map/all_to_all | solution.py:379
  158.3 2.8 %reshape.329 = f32[128,32,128]{2,1,0:T(8,128)} reshape(f32[1,128,16,256]{3,2,1,0:T(8,128)} %copy.33) | data formatting | bytes 4194304 | tf_op jit(solution)/shard_map/reshape | solution.py:389
  161.1 5.7 %fusion.4 = f32[128,32,128]{2,1,0:T(8,128)} fusion(f32[128,32,128]{2,1,0:T(8,128)S(1)} %copy-done.1, f32[128,32,128]{2,1,0:T(8,128)} %reshape.329, f32[128,32,128]{2,1,0:T(8,128)} %param.5, f32[128,32,128]{2,1,0:T(8,128)} %get-tuple-element.46, f32[32,32,128]{2,1,0:T(8,128)S(1)} %collective-permute-done.5, f32[32,32,128]{2,1,0:T(8,128)S(1)} %collective-permute-done.4, ...), kind=kLoop, calls=%fused_computation.10 | loop fusion | flops 4718592 | bytes 12582912 | tf_op jit(solution)/shard_map/max | solution.py:390
  (27 shorter events, 0.1 us)
Async XLA Ops:
  3.6 6.7 %copy-start = (f32[128,32,128]{2,1,0:T(8,128)S(1)}, f32[128,32,128]{2,1,0:T(8,128)}, u32[]{:S(2)}) copy-start(f32[128,32,128]{2,1,0:T(8,128)} %own_ref.7) | copy-start | bytes 6291460
  3.6 67.4 %all-to-all-start = ((f32[128,16,256]{0,2,1:T(8,128)}), f32[128,16,256]{0,2,1:T(8,128)}, u32[]{:S(2)}, u32[]{:S(2)}) async-start(f32[128,16,256]{0,2,1:T(8,128)} %bitcast.40), calls=%async_computation | async-start | bytes 4194304 | tf_op jit(solution)/shard_map/all_to_all | solution.py:365
  11.8 24.7 %collective-permute-start = (f32[64,32,128]{2,1,0:T(8,128)}, f32[64,32,128]{2,1,0:T(8,128)S(1)}, u32[]{:S(2)}, u32[]{:S(2)}) collective-permute-start(f32[64,32,128]{2,1,0:T(8,128)} %get-tuple-element.67), channel_id=1, source_target_pairs={{0,1},{1,0},{2,3},{3,2},{4,5},{5,4},{6,7},{7,6},{8,9},{9,8},{10,11... | collective-permute-start | bytes 3145736 | tf_op jit(solution)/shard_map/ppermute | solution.py:308
  21.3 3.7 %copy-start.7 = (f32[256,1024,1]{0,2,1:T(1,128)S(1)}, f32[256,1024,1]{0,2,1:T(1,128)}, u32[]{:S(2)}) copy-start(f32[256,1024,1]{0,2,1:T(1,128)} %get-tuple-element.64) | copy-start | bytes 3145732
  30.8 5.7 %copy-start.9 = (f32[64,32,128]{2,1,0:T(8,128)S(1)}, f32[64,32,128]{2,1,0:T(8,128)}, u32[]{:S(2)}) copy-start(f32[64,32,128]{2,1,0:T(8,128)} %get-tuple-element.32) | copy-start | bytes 3145732
  36.5 3.7 %copy-start.4 = (f32[64,32,128]{2,1,0:T(8,128)}, f32[64,32,128]{2,1,0:T(8,128)S(1)}, u32[]{:S(2)}) copy-start(f32[64,32,128]{2,1,0:T(8,128)S(1)} %collective-permute-done.above_ref.below_ref) | copy-start | bytes 3145732
  36.5 37.4 %collective-permute-start.1 = (f32[64,32,128]{2,1,0:T(8,128)S(1)}, f32[64,32,128]{2,1,0:T(8,128)S(1)}, u32[]{:S(2)}, u32[]{:S(2)}) collective-permute-start(f32[64,32,128]{2,1,0:T(8,128)S(1)} %copy-done.9), channel_id=1, source_target_pairs={{0,1},{1,0},{2,3},{3,2},{4,5},{5,4},{6,7},{7,6},{8,9},{9,8},{10,11... | collective-permute-start | bytes 3145736 | tf_op jit(solution)/shard_map/ppermute | solution.py:308
  69.5 29.3 %collective-permute-start.3 = (f32[32,32,128]{2,1,0:T(8,128)}, f32[32,32,128]{2,1,0:T(8,128)}, u32[]{:S(2)}, u32[]{:S(2)}) collective-permute-start(f32[32,32,128]{2,1,0:T(8,128)} %get-tuple-element.41), channel_id=1, source_target_pairs={{0,1},{1,0},{2,3},{3,2},{4,5},{5,4},{6,7},{7,6},{8,9},{9,8},{10,11... | collective-permute-start | bytes 1572872 | tf_op jit(solution)/shard_map/ppermute | solution.py:343
  69.8 29.0 %collective-permute-start.2 = (f32[32,32,128]{2,1,0:T(8,128)}, f32[32,32,128]{2,1,0:T(8,128)}, u32[]{:S(2)}, u32[]{:S(2)}) collective-permute-start(f32[32,32,128]{2,1,0:T(8,128)} %get-tuple-element.40), channel_id=1, source_target_pairs={{0,1},{1,0},{2,3},{3,2},{4,5},{5,4},{6,7},{7,6},{8,9},{9,8},{10,11... | collective-permute-start | bytes 1572872 | tf_op jit(solution)/shard_map/ppermute | solution.py:343
  73.9 2.2 %copy-start.5 = (f32[64,32,128]{2,1,0:T(8,128)}, f32[64,32,128]{2,1,0:T(8,128)S(1)}, u32[]{:S(2)}) copy-start(f32[64,32,128]{2,1,0:T(8,128)S(1)} %collective-permute-done.1.above_ref.below_ref) | copy-start | bytes 3145732
  76.0 4.9 %copy-start.2 = (f32[1024,1024]{0,1:T(8,128)S(1)}, f32[1024,1024]{0,1:T(8,128)}, u32[]{:S(2)}) copy-start(f32[1024,1024]{0,1:T(8,128)} %bitcast_multiply_fusion) | copy-start | bytes 12582916
  76.1 6.8 %copy-start.8 = (f32[256,1024,1]{1,0,2:T(8,128)S(1)}, f32[256,1024,1]{1,0,2:T(8,128)}, u32[]{:S(2)}) copy-start(f32[256,1024,1]{1,0,2:T(8,128)} %copy.36) | copy-start | bytes 3145732
  81.0 2.2 %copy-start.3 = (f32[1024,1024]{0,1:T(8,128)S(1)}, f32[1024,1024]{0,1:T(8,128)}, u32[]{:S(2)}) copy-start(f32[1024,1024]{0,1:T(8,128)} %bitcast_multiply_fusion.1) | copy-start | bytes 12582916
  81.0 2.9 %copy-start.6 = (f32[16,128,1,256]{3,1,0,2:T(8,128)S(1)}, f32[16,128,1,256]{3,1,0,2:T(8,128)}, u32[]{:S(2)}) copy-start(f32[16,128,1,256]{3,1,0,2:T(8,128)} %copy.29) | copy-start | bytes 6291460
  98.8 55.3 %all-to-all-start.1 = ((f32[16,128,256]{2,1,0:T(8,128)}), f32[16,128,256]{2,1,0:T(8,128)}, u32[]{:S(2)}, u32[]{:S(2)}) async-start(f32[16,128,256]{2,1,0:T(8,128)} %bitcast.41), calls=%async_computation.1 | async-start | bytes 4194304 | tf_op jit(solution)/shard_map/all_to_all | solution.py:379
  133.2 27.9 %collective-permute-start.5 = (f32[32,32,128]{2,1,0:T(8,128)}, f32[32,32,128]{2,1,0:T(8,128)S(1)}, u32[]{:S(2)}, u32[]{:S(2)}) collective-permute-start(f32[32,32,128]{2,1,0:T(8,128)} %get-tuple-element.50), channel_id=1, source_target_pairs={{0,1},{1,0},{2,3},{3,2},{4,5},{5,4},{6,7},{7,6},{8,9},{9,8},{10,11... | collective-permute-start | bytes 1572872 | tf_op jit(solution)/shard_map/ppermute | solution.py:343
  133.5 27.6 %collective-permute-start.4 = (f32[32,32,128]{2,1,0:T(8,128)}, f32[32,32,128]{2,1,0:T(8,128)S(1)}, u32[]{:S(2)}, u32[]{:S(2)}) collective-permute-start(f32[32,32,128]{2,1,0:T(8,128)} %get-tuple-element.49), channel_id=1, source_target_pairs={{0,1},{1,0},{2,3},{3,2},{4,5},{5,4},{6,7},{7,6},{8,9},{9,8},{10,11... | collective-permute-start | bytes 1572872 | tf_op jit(solution)/shard_map/ppermute | solution.py:343
  158.3 2.8 %copy-start.1 = (f32[128,32,128]{2,1,0:T(8,128)S(1)}, f32[128,32,128]{2,1,0:T(8,128)}, u32[]{:S(2)}) copy-start(f32[128,32,128]{2,1,0:T(8,128)} %own_ref.7) | copy-start | bytes 6291460

commit v7 on v4

--- a/solution.py
+++ b/solution.py
@@ -15,7 +15,7 @@
 TAU_STEP = 0.5
 SPACE_BOUND = 0.5
 FREQ_BOUND = 1.0
-CHUNK = 8
+CHUNK = 16
 GROUPS = 4
 
 

time: 168 us -> 169 us (level)
  transfers between devices with their start and end apart: 8 -> 8, of which waited for: 2 -> 2; matrix products, arithmetic and copies ran while one was open for 41% -> 41% of each run, Pallas kernels for 32% -> 33%
where the time goes in v7:
time: 169 us; the launch traced here: 167 us
  Pallas kernels  54.9 us (32%)
  local copies, waits for them, and re-layouts  47.5 us (28%)
  starting transfers between devices  19.7 us (12%)
  other arithmetic  18.8 us (11%)
  waiting for transfers between devices  13.5 us (8%)
  matrix products  12.2 us (7%)
    pallas_call x4, Pallas kernels, starlet(): pl.pallas_call(starlet_kernel, grid=(steps,), in_specs=[pl.BlockSpec(memo...  54.9 us
    unnamed x25, local copies, waits for them, and re-layouts  15.9 us
    all_to_all x1, waiting for transfers between devices, local(): lax.all_to_all(spectral_sum.reshape(peers, chans, share), 'freq', split_a...  9.16 us
    all_to_all x1, starting transfers between devices, local(): lax.all_to_all(spectral_sum.reshape(peers, chans, share), 'freq', split_a...  7.58 us
    dot_general x2, matrix products, forward_dot(): lax.dot_general(samples, table, (((0,), (1,)), ((), ())), precision=lax.P...  7.14 us
    rev x1, local copies, waits for them, and re-layouts, spectral_back(): (parts[0] - parts[1])[::-1]  6.83 us
    all_to_all x1, starting transfers between devices, local(): lax.all_to_all(pieces, 'freq', split_axis=1, concat_axis=0, tiled=True)  6.69 us
    max x1, other arithmetic, local(): jnp.maximum(image_cube - TAU_STEP * (data_grad + space_term + spectral_te...  5.68 us
  transfers between devices with their start and end apart: 8, of which 2 were waited for; matrix products, arithmetic and copies ran while one was open for 41% of the time, Pallas kernels for 33%

profile of v7, /device:TPU:13, one launch (start us, length us, event | category | flops | bytes accessed | tf_op | source)
XLA Modules:
  0.0 167.4 jit_solution(4603679478757715135)
XLA Ops:
  0.6 3.0 %copy.28 = f32[128,32,128]{0,2,1:T(8,128)} copy(f32[128,32,128]{2,1,0:T(8,128)} %own_ref.7) | data formatting | bytes 4194304 | tf_op args[0]
  3.6 6.7 %all-to-all-start = ((f32[128,16,256]{0,2,1:T(8,128)}), f32[128,16,256]{0,2,1:T(8,128)}, u32[]{:S(2)}, u32[]{:S(2)}) async-start(f32[128,16,256]{0,2,1:T(8,128)} %bitcast.40), calls=%async_computation | async-start | bytes 4194304 | tf_op jit(solution)/shard_map/all_to_all | solution.py:364
  10.3 1.5 fusion.36
  11.8 1.2 collective-permute-start
  13.0 2.9 %copy.30 = f32[256,2048]{0,1:T(8,128)} copy(f32[256,2048]{1,0:T(8,128)} %param.7) | data formatting | bytes 4194304 | tf_op args[3]
  15.9 2.5 %reshape.327 = f32[256,1024,2]{0,2,1:T(2,128)S(1)} reshape(f32[256,2048]{0,1:T(8,128)} %copy.30) | data formatting | bytes 4194304 | tf_op jit(solution)/shard_map/reshape | solution.py:145
  18.4 2.9 %fusion.35 = (f32[256,1024,1]{0,2,1:T(1,128)}, f32[256,1024,1]{0,2,1:T(1,128)}) fusion(f32[256,1024,2]{0,2,1:T(2,128)S(1)} %reshape.327), kind=kLoop, calls=%fused_computation.69 | loop fusion | bytes 4194304 | tf_op jit(solution)/shard_map/slice | solution.py:147
  21.3 3.7 %copy.36 = f32[256,1024,1]{1,0,2:T(8,128)} copy(f32[256,1024,1]{0,2,1:T(1,128)} %get-tuple-element.65) | data formatting | bytes 2097152
  25.1 2.4 %copy.37 = f32[256,1024,1]{1,0,2:T(8,128)} copy(f32[256,1024,1]{0,2,1:T(1,128)S(1)} %copy-done.7) | data formatting | bytes 2097152
  27.5 0.6 stack.40.flags_ref
  28.1 0.6 fusion.30
  28.7 2.1 %fusion.20 = (f32[1024,64]{0,1:T(8,128)S(1)}, f32[1024,64]{0,1:T(8,128)S(1)}, f32[1024,64]{0,1:T(8,128)S(1)}, f32[1024,64]{0,1:T(8,128)S(1)}) fusion(s32[64]{0:T(128)S(1)} %multiply_add_fusion, s32[1024]{0:T(1024)S(1)} %fusion.33, s32[1024]{0:T(1024)S(1)} %iota_multiply_fusion), kind=kLoop, calls=%fused_computation.39 | loop fusion | flops 1835008 | bytes 1057024 | tf_op jit(solution)/shard_map/cos | solution.py:118
  30.8 1.3 multiply_subtract_fusion
  32.1 4.4 %collective-permute-done.above_ref.below_ref = f32[64,32,128]{2,1,0:T(8,128)S(1)} collective-permute-done((f32[64,32,128]{2,1,0:T(8,128)}, f32[64,32,128]{2,1,0:T(8,128)S(1)}, u32[]{:S(2)}, u32[]{:S(2)}) %collective-permute-start) | collective-permute-done | bytes 1048608 | tf_op jit(solution)/shard_map/ppermute | solution.py:307
  36.5 1.2 collective-permute-start.1
  37.7 2.5 %bitcast_multiply_fusion.1 = f32[1024,1024]{0,1:T(8,128)} fusion(f32[1024,16,64]{0,2,1:T(8,128)S(1)} %get-tuple-element.82, f32[1024]{0:T(1024)S(1)} %compare_select_fusion.1), kind=kLoop, calls=%fused_computation.1 | loop fusion | flops 1048576 | bytes 8392704 | tf_op jit(solution)/shard_map/mul | solution.py:117
  40.2 2.5 %bitcast_multiply_fusion = f32[1024,1024]{0,1:T(8,128)} fusion(f32[1024,16,64]{0,2,1:T(8,128)S(1)} %get-tuple-element.81, f32[1024]{0:T(1024)S(1)} %compare_select_fusion), kind=kLoop, calls=%fused_computation | loop fusion | flops 1048576 | bytes 8392704 | tf_op jit(solution)/shard_map/mul | solution.py:117
  42.7 13.6 %shard_map.67 = (f32[4,128,32,128]{3,2,1,0:T(8,128)}, f32[32,32,128]{2,1,0:T(8,128)}, f32[128,32,128]{2,1,0:T(8,128)}, f32[32,32,128]{2,1,0:T(8,128)}) custom-call(s32[5]{0:T(128)} %stack.40.flags_ref, f32[64,32,128]{2,1,0:T(8,128)} %copy-done.4, f32[128,32,128]{2,1,0:T(8,128)} %own_ref.7, f32[64,32,128]{2,1,0:T(8,128)} %copy-done.4, ...), custom_call_target="tpu_custom_call" | custom-call | tf_op jit(solution)/shard_map/pallas_call | solution.py:268
  56.4 13.9 %shard_map.68 = (f32[4,128,32,128]{3,2,1,0:T(8,128)}, f32[32,32,128]{2,1,0:T(8,128)}, f32[128,32,128]{2,1,0:T(8,128)}, f32[32,32,128]{2,1,0:T(8,128)}) custom-call(s32[5]{0:T(128)} %stack.40.flags_ref, f32[64,32,128]{2,1,0:T(8,128)} %copy-done.4, f32[128,32,128]{2,1,0:T(8,128)} %own_ref.7, ...), custom_call_target="tpu_custom_call", output_to_operand_aliasing={{0}: (5, {}), {2}: (6, {})} | custom-call | tf_op jit(solution)/shard_map/pallas_call | solution.py:268
  70.2 0.3 collective-permute-start.3
  70.5 1.2 collective-permute-start.2
  71.7 0.0 all-to-all-done
  71.7 2.9 %copy.29 = f32[16,128,1,256]{3,1,0,2:T(8,128)} copy(f32[16,128,1,256]{1,3,0,2:T(8,128)} %bitcast.6) | data formatting | bytes 4194304 | tf_op jit(solution)/shard_map/all_to_all | solution.py:364
  74.6 1.7 slice.22
  76.3 0.5 rev.6
  76.8 4.9 %fusion.6 = f32[256,1024]{1,0:T(8,128)S(1)} fusion(f32[1024,1024]{0,1:T(8,128)} %bitcast_multiply_fusion, f32[256,1024,1]{1,0,2:T(8,128)} %copy.37, f32[1024,256]{1,0:T(8,128)S(1)} %rev.6, f32[2048,256]{1,0:T(8,128)} %bitcast.36), kind=kOutput, calls=%fused_computation.14 | convolution fusion | flops 1611661312 | bytes 8388608 | tf_op jit(solution)/shard_map/dot_general | solution.py:125
  81.7 0.0 copy-start.6
  81.7 1.8 %fusion.37 = f32[1024,256]{1,0:T(8,128)S(1)} fusion(f32[1024,1024]{0,1:T(8,128)S(1)} %copy-done.2, f32[256,1024]{1,0:T(8,128)S(1)} %fusion.6), kind=kOutput, calls=%fused_computation.71 | convolution fusion | flops 1610612736 | bytes 6291456 | tf_op jit(solution)/shard_map/dot_general | solution.py:156
  83.6 0.3 copy-done.3
  83.9 0.7 copy-done.6
  84.6 2.2 %fusion.8 = f32[256,1024]{1,0:T(8,128)S(1)} fusion(f32[1024,1024]{0,1:T(8,128)S(1)} %copy-done.3, f32[256,1024,1]{1,0,2:T(8,128)S(1)} %copy-done.8, f32[1024,256]{1,0:T(8,128)S(1)} %rev.6, f32[2048,256]{1,0:T(8,128)S(1)} %bitcast.37), kind=kOutput, calls=%fused_computation.17 | convolution fusion | flops 1611661312 | bytes 8388608 | tf_op jit(solution)/shard_map/dot_general | solution.py:125
  86.8 3.2 %fusion.34 = (f32[1024,256]{1,0:T(8,128)}, f32[1024,256]{1,0:T(8,128)}) fusion(f32[1024,256]{1,0:T(8,128)S(1)} %fusion.37, f32[1024,1024]{0,1:T(8,128)S(1)} %copy-done.3, f32[256,1024]{1,0:T(8,128)S(1)} %fusion.8), kind=kOutput, calls=%fused_computation.68 | convolution fusion | flops 1611137024 | bytes 8388608 | tf_op jit(solution)/shard_map/dot_general | solution.py:156
  90.0 6.8 %rev.7 = f32[1024,256]{1,0:T(8,128)S(1)} reverse(f32[1024,256]{1,0:T(8,128)} %get-tuple-element.63), dimensions={0} | reverse | bytes 2097152 | tf_op jit(solution)/shard_map/rev | solution.py:167
  96.9 2.7 %pad_maximum_fusion = f32[2048,256]{1,0:T(8,128)} fusion(f32[1024,256]{1,0:T(8,128)S(1)} %rev.7, f32[1024,256]{1,0:T(8,128)} %get-tuple-element.62), kind=kLoop, calls=%fused_computation.4 | loop fusion | flops 524288 | bytes 4194304 | tf_op jit(solution)/shard_map/concatenate | solution.py:167
  99.5 0.0 collective-permute-done.3
  99.5 7.6 %all-to-all-start.1 = ((f32[16,128,256]{2,1,0:T(8,128)}), f32[16,128,256]{2,1,0:T(8,128)}, u32[]{:S(2)}, u32[]{:S(2)}) async-start(f32[16,128,256]{2,1,0:T(8,128)} %bitcast.41), calls=%async_computation.1 | async-start | bytes 4194304 | tf_op jit(solution)/shard_map/all_to_all | solution.py:378
  107.1 13.7 %shard_map.69 = (f32[4,128,32,128]{3,2,1,0:T(8,128)}, f32[32,32,128]{2,1,0:T(8,128)}, f32[128,32,128]{2,1,0:T(8,128)}, f32[32,32,128]{2,1,0:T(8,128)}) custom-call(s32[5]{0:T(128)} %stack.40.flags_ref, f32[64,32,128]{2,1,0:T(8,128)} %copy-done.5, f32[128,32,128]{2,1,0:T(8,128)} %own_ref.7, ...), custom_call_target="tpu_custom_call", output_to_operand_aliasing={{0}: (5, {}), {2}: (6, {})} | custom-call | tf_op jit(solution)/shard_map/pallas_call | solution.py:268
  120.8 13.7 %shard_map.70 = (f32[4,128,32,128]{3,2,1,0:T(8,128)}, f32[32,32,128]{2,1,0:T(8,128)}, f32[128,32,128]{2,1,0:T(8,128)}, f32[32,32,128]{2,1,0:T(8,128)}) custom-call(s32[5]{0:T(128)} %stack.40.flags_ref, f32[64,32,128]{2,1,0:T(8,128)} %copy-done.5, f32[128,32,128]{2,1,0:T(8,128)} %own_ref.7, ...), custom_call_target="tpu_custom_call", output_to_operand_aliasing={{0}: (5, {}), {2}: (6, {})} | custom-call | tf_op jit(solution)/shard_map/pallas_call | solution.py:268
  134.6 0.3 collective-permute-start.5
  134.9 1.2 collective-permute-start.4
  136.1 1.5 pad_maximum_fusion.1
  137.5 2.8 %copy.34 = f32[256,1024,2]{0,2,1:T(2,128)S(1)} copy(f32[256,1024,2]{1,0,2:T(8,128)} %pad_maximum_fusion.1) | data formatting | bytes 4194304 | tf_op jit(solution)/shard_map/stack | solution.py:150
  140.4 2.4 %reshape.330 = f32[256,2048]{0,1:T(8,128)} reshape(f32[256,1024,2]{0,2,1:T(2,128)S(1)} %copy.34) | data formatting | bytes 4194304 | tf_op jit(solution)/shard_map/reshape | solution.py:150
  142.8 2.9 %copy.35 = f32[256,2048]{1,0:T(8,128)} copy(f32[256,2048]{0,1:T(8,128)} %reshape.330) | data formatting | bytes 4194304
  145.7 9.2 %all-to-all-done.1 = f32[16,128,256]{2,1,0:T(8,128)} async-done(((f32[16,128,256]{2,1,0:T(8,128)}), f32[16,128,256]{2,1,0:T(8,128)}, u32[]{:S(2)}, u32[]{:S(2)}) %all-to-all-start.1) | async-done | bytes 2097184 | tf_op jit(solution)/shard_map/all_to_all | solution.py:378
  154.8 4.1 %copy.33 = f32[1,128,16,256]{3,2,1,0:T(8,128)} copy(f32[1,128,16,256]{3,1,2,0:T(8,128)} %bitcast.14) | data formatting | bytes 4194304 | tf_op jit(solution)/shard_map/all_to_all | solution.py:378
  159.0 2.8 %reshape.329 = f32[128,32,128]{2,1,0:T(8,128)} reshape(f32[1,128,16,256]{3,2,1,0:T(8,128)} %copy.33) | data formatting | bytes 4194304 | tf_op jit(solution)/shard_map/reshape | solution.py:388
  161.8 5.7 %fusion.4 = f32[128,32,128]{2,1,0:T(8,128)} fusion(f32[128,32,128]{2,1,0:T(8,128)S(1)} %copy-done.1, f32[128,32,128]{2,1,0:T(8,128)} %reshape.329, f32[128,32,128]{2,1,0:T(8,128)} %param.5, f32[128,32,128]{2,1,0:T(8,128)} %get-tuple-element.46, f32[32,32,128]{2,1,0:T(8,128)S(1)} %collective-permute-done.5, f32[32,32,128]{2,1,0:T(8,128)S(1)} %collective-permute-done.4, ...), kind=kLoop, calls=%fused_computation.10 | loop fusion | flops 4718592 | bytes 12582912 | tf_op jit(solution)/shard_map/max | solution.py:389
  (27 shorter events, 0.1 us)
Async XLA Ops:
  3.6 6.7 %copy-start = (f32[128,32,128]{2,1,0:T(8,128)S(1)}, f32[128,32,128]{2,1,0:T(8,128)}, u32[]{:S(2)}) copy-start(f32[128,32,128]{2,1,0:T(8,128)} %own_ref.7) | copy-start | bytes 6291460
  3.6 68.1 %all-to-all-start = ((f32[128,16,256]{0,2,1:T(8,128)}), f32[128,16,256]{0,2,1:T(8,128)}, u32[]{:S(2)}, u32[]{:S(2)}) async-start(f32[128,16,256]{0,2,1:T(8,128)} %bitcast.40), calls=%async_computation | async-start | bytes 4194304 | tf_op jit(solution)/shard_map/all_to_all | solution.py:364
  11.8 24.7 %collective-permute-start = (f32[64,32,128]{2,1,0:T(8,128)}, f32[64,32,128]{2,1,0:T(8,128)S(1)}, u32[]{:S(2)}, u32[]{:S(2)}) collective-permute-start(f32[64,32,128]{2,1,0:T(8,128)} %get-tuple-element.67), channel_id=1, source_target_pairs={{0,1},{1,0},{2,3},{3,2},{4,5},{5,4},{6,7},{7,6},{8,9},{9,8},{10,11... | collective-permute-start | bytes 3145736 | tf_op jit(solution)/shard_map/ppermute | solution.py:307
  21.3 3.7 %copy-start.7 = (f32[256,1024,1]{0,2,1:T(1,128)S(1)}, f32[256,1024,1]{0,2,1:T(1,128)}, u32[]{:S(2)}) copy-start(f32[256,1024,1]{0,2,1:T(1,128)} %get-tuple-element.64) | copy-start | bytes 3145732
  30.8 5.7 %copy-start.9 = (f32[64,32,128]{2,1,0:T(8,128)S(1)}, f32[64,32,128]{2,1,0:T(8,128)}, u32[]{:S(2)}) copy-start(f32[64,32,128]{2,1,0:T(8,128)} %get-tuple-element.32) | copy-start | bytes 3145732
  36.5 3.7 %copy-start.4 = (f32[64,32,128]{2,1,0:T(8,128)}, f32[64,32,128]{2,1,0:T(8,128)S(1)}, u32[]{:S(2)}) copy-start(f32[64,32,128]{2,1,0:T(8,128)S(1)} %collective-permute-done.above_ref.below_ref) | copy-start | bytes 3145732
  36.5 38.1 %collective-permute-start.1 = (f32[64,32,128]{2,1,0:T(8,128)S(1)}, f32[64,32,128]{2,1,0:T(8,128)S(1)}, u32[]{:S(2)}, u32[]{:S(2)}) collective-permute-start(f32[64,32,128]{2,1,0:T(8,128)S(1)} %copy-done.9), channel_id=1, source_target_pairs={{0,1},{1,0},{2,3},{3,2},{4,5},{5,4},{6,7},{7,6},{8,9},{9,8},{10,11... | collective-permute-start | bytes 3145736 | tf_op jit(solution)/shard_map/ppermute | solution.py:307
  70.2 29.3 %collective-permute-start.3 = (f32[32,32,128]{2,1,0:T(8,128)}, f32[32,32,128]{2,1,0:T(8,128)}, u32[]{:S(2)}, u32[]{:S(2)}) collective-permute-start(f32[32,32,128]{2,1,0:T(8,128)} %get-tuple-element.41), channel_id=1, source_target_pairs={{0,1},{1,0},{2,3},{3,2},{4,5},{5,4},{6,7},{7,6},{8,9},{9,8},{10,11... | collective-permute-start | bytes 1572872 | tf_op jit(solution)/shard_map/ppermute | solution.py:342
  70.5 29.0 %collective-permute-start.2 = (f32[32,32,128]{2,1,0:T(8,128)}, f32[32,32,128]{2,1,0:T(8,128)}, u32[]{:S(2)}, u32[]{:S(2)}) collective-permute-start(f32[32,32,128]{2,1,0:T(8,128)} %get-tuple-element.40), channel_id=1, source_target_pairs={{0,1},{1,0},{2,3},{3,2},{4,5},{5,4},{6,7},{7,6},{8,9},{9,8},{10,11... | collective-permute-start | bytes 1572872 | tf_op jit(solution)/shard_map/ppermute | solution.py:342
  74.6 2.2 %copy-start.5 = (f32[64,32,128]{2,1,0:T(8,128)}, f32[64,32,128]{2,1,0:T(8,128)S(1)}, u32[]{:S(2)}) copy-start(f32[64,32,128]{2,1,0:T(8,128)S(1)} %collective-permute-done.1.above_ref.below_ref) | copy-start | bytes 3145732
  76.8 4.9 %copy-start.2 = (f32[1024,1024]{0,1:T(8,128)S(1)}, f32[1024,1024]{0,1:T(8,128)}, u32[]{:S(2)}) copy-start(f32[1024,1024]{0,1:T(8,128)} %bitcast_multiply_fusion) | copy-start | bytes 12582916
  76.8 6.8 %copy-start.8 = (f32[256,1024,1]{1,0,2:T(8,128)S(1)}, f32[256,1024,1]{1,0,2:T(8,128)}, u32[]{:S(2)}) copy-start(f32[256,1024,1]{1,0,2:T(8,128)} %copy.36) | copy-start | bytes 3145732
  81.7 2.2 %copy-start.3 = (f32[1024,1024]{0,1:T(8,128)S(1)}, f32[1024,1024]{0,1:T(8,128)}, u32[]{:S(2)}) copy-start(f32[1024,1024]{0,1:T(8,128)} %bitcast_multiply_fusion.1) | copy-start | bytes 12582916
  81.7 2.9 %copy-start.6 = (f32[16,128,1,256]{3,1,0,2:T(8,128)S(1)}, f32[16,128,1,256]{3,1,0,2:T(8,128)}, u32[]{:S(2)}) copy-start(f32[16,128,1,256]{3,1,0,2:T(8,128)} %copy.29) | copy-start | bytes 6291460
  99.5 55.3 %all-to-all-start.1 = ((f32[16,128,256]{2,1,0:T(8,128)}), f32[16,128,256]{2,1,0:T(8,128)}, u32[]{:S(2)}, u32[]{:S(2)}) async-start(f32[16,128,256]{2,1,0:T(8,128)} %bitcast.41), calls=%async_computation.1 | async-start | bytes 4194304 | tf_op jit(solution)/shard_map/all_to_all | solution.py:378
  134.6 27.2 %collective-permute-start.5 = (f32[32,32,128]{2,1,0:T(8,128)}, f32[32,32,128]{2,1,0:T(8,128)S(1)}, u32[]{:S(2)}, u32[]{:S(2)}) collective-permute-start(f32[32,32,128]{2,1,0:T(8,128)} %get-tuple-element.50), channel_id=1, source_target_pairs={{0,1},{1,0},{2,3},{3,2},{4,5},{5,4},{6,7},{7,6},{8,9},{9,8},{10,11... | collective-permute-start | bytes 1572872 | tf_op jit(solution)/shard_map/ppermute | solution.py:342
  134.9 26.9 %collective-permute-start.4 = (f32[32,32,128]{2,1,0:T(8,128)}, f32[32,32,128]{2,1,0:T(8,128)S(1)}, u32[]{:S(2)}, u32[]{:S(2)}) collective-permute-start(f32[32,32,128]{2,1,0:T(8,128)} %get-tuple-element.49), channel_id=1, source_target_pairs={{0,1},{1,0},{2,3},{3,2},{4,5},{5,4},{6,7},{7,6},{8,9},{9,8},{10,11... | collective-permute-start | bytes 1572872 | tf_op jit(solution)/shard_map/ppermute | solution.py:342
  159.0 2.8 %copy-start.1 = (f32[128,32,128]{2,1,0:T(8,128)S(1)}, f32[128,32,128]{2,1,0:T(8,128)}, u32[]{:S(2)}) copy-start(f32[128,32,128]{2,1,0:T(8,128)} %own_ref.7) | copy-start | bytes 6291460

commit v8 on v4

--- a/solution.py
+++ b/solution.py
@@ -359,7 +359,7 @@
     share = local_rows * columns // peers
     pieces = image_cube.reshape(chans, peers, share)
     work = Spatial(image_cube, space_duals)
-    early = work.groups // 2
+    early = max(1, work.groups // 4)
     halos = exchange_halos(image_cube, early)
     pixel_cube = lax.all_to_all(pieces, "freq", split_axis=1, concat_axis=0, tiled=True).reshape(
         chans * peers, share

time: 168 us -> 181 us (1.077)
  local copies, waits for them, and re-layouts: 47.5 us -> 55.9 us
  waiting for transfers between devices: 14.4 us -> 17.4 us
    all_to_all x1, waiting for transfers between devices: 9.99 us -> 0.01 us  [local(): lax.all_to_all(spectral_sum.reshape(peers, chans, share), 'freq', split_a...]
    ppermute x4, waiting for transfers between devices: 0.01 us -> 6.39 us  [run(): self.sends.append(lax.ppermute(send, 'rows', self.down + self.up))]
    rev x1, local copies, waits for them, and re-layouts: 0.47 us -> 5.15 us  [spectral(): tail = pixel_cube[half:][::-1]]
    ppermute x2, waiting for transfers between devices: 4.36 us -> 8.47 us  [exchange_halos(): got = lax.ppermute(part, 'rows', down + up)]
    all_to_all x1, waiting for transfers between devices: 0.01 us -> 2.52 us  [local(): lax.all_to_all(pieces, 'freq', split_axis=1, concat_axis=0, tiled=True)]
    slice x1, local copies, waits for them, and re-layouts: 2.93 us -> 4.99 us  [spectral(): pairs[:, :, parity] + SIGMA * forward_dot(samples, tables[parity])]
    unnamed x25 -> x21, local copies, waits for them, and re-layouts: 15.9 us -> 15.9 us
  transfers between devices with their start and end apart: 8 -> 8, of which waited for: 2 -> 3; matrix products, arithmetic and copies ran while one was open for 41% -> 44% of each run, Pallas kernels for 32% -> 30%
where the time goes in v8:
time: 181 us; the launch traced here: 178 us
  local copies, waits for them, and re-layouts  55.9 us (31%)
  Pallas kernels  53.1 us (29%)
  starting transfers between devices  19.5 us (11%)
  other arithmetic  18.9 us (10%)
  waiting for transfers between devices  17.4 us (10%)
  matrix products  12.5 us (7%)
    pallas_call x4, Pallas kernels, starlet(): pl.pallas_call(starlet_kernel, grid=(steps,), in_specs=[pl.BlockSpec(memo...  53.1 us
    unnamed x21, local copies, waits for them, and re-layouts  15.9 us
    ppermute x2, waiting for transfers between devices, exchange_halos(): got = lax.ppermute(part, 'rows', down + up)  8.47 us
    all_to_all x1, starting transfers between devices, local(): lax.all_to_all(spectral_sum.reshape(peers, chans, share), 'freq', split_a...  8.27 us
    dot_general x2, matrix products, forward_dot(): lax.dot_general(samples, table, (((0,), (1,)), ((), ())), precision=lax.P...  7.4 us
    rev x1, local copies, waits for them, and re-layouts, spectral_back(): (parts[0] - parts[1])[::-1]  6.83 us
    all_to_all x1, starting transfers between devices, local(): lax.all_to_all(pieces, 'freq', split_axis=1, concat_axis=0, tiled=True)  6.69 us
    ppermute x4, waiting for transfers between devices, run(): self.sends.append(lax.ppermute(send, 'rows', self.down + self.up))  6.39 us
  transfers between devices with their start and end apart: 8, of which 3 were waited for; matrix products, arithmetic and copies ran while one was open for 44% of the time, Pallas kernels for 30%

profile of v8, /device:TPU:13, one launch (start us, length us, event | category | flops | bytes accessed | tf_op | source)
XLA Modules:
  0.0 178.0 jit_solution(2897716032820455769)
XLA Ops:
  0.6 3.0 %copy.28 = f32[128,32,128]{0,2,1:T(8,128)} copy(f32[128,32,128]{2,1,0:T(8,128)} %own_ref.7) | data formatting | bytes 4194304 | tf_op args[0]
  3.6 6.7 %all-to-all-start = ((f32[128,16,256]{0,2,1:T(8,128)}), f32[128,16,256]{0,2,1:T(8,128)}, u32[]{:S(2)}, u32[]{:S(2)}) async-start(f32[128,16,256]{0,2,1:T(8,128)} %bitcast.40), calls=%async_computation | async-start | bytes 4194304 | tf_op jit(solution)/shard_map/all_to_all | solution.py:364
  10.3 0.8 slice.18
  11.1 1.2 collective-permute-start
  12.4 2.9 %copy.30 = f32[256,2048]{0,1:T(8,128)} copy(f32[256,2048]{1,0:T(8,128)} %param.7) | data formatting | bytes 4194304 | tf_op args[3]
  15.2 3.4 %reshape.327 = f32[256,1024,2]{0,2,1:T(2,128)} reshape(f32[256,2048]{0,1:T(8,128)} %copy.30) | data formatting | bytes 4194304 | tf_op jit(solution)/shard_map/reshape | solution.py:145
  18.7 5.0 %fusion.35 = (f32[256,1024,1]{0,2,1:T(1,128)}, f32[256,1024,1]{0,2,1:T(1,128)S(1)}) fusion(f32[256,1024,2]{0,2,1:T(2,128)} %reshape.327), kind=kLoop, calls=%fused_computation.69 | loop fusion | bytes 4194304 | tf_op jit(solution)/shard_map/slice | solution.py:147
  23.7 1.3 slice.19
  25.0 3.7 %copy.37 = f32[256,1024,1]{1,0,2:T(8,128)} copy(f32[256,1024,1]{0,2,1:T(1,128)} %get-tuple-element.66) | data formatting | bytes 2097152
  28.6 2.4 %copy.36 = f32[256,1024,1]{1,0,2:T(8,128)} copy(f32[256,1024,1]{0,2,1:T(1,128)S(1)} %get-tuple-element.67) | data formatting | bytes 2097152
  31.1 0.6 stack.40.flags_ref
  31.7 2.1 %fusion.20 = (f32[1024,64]{0,1:T(8,128)S(1)}, f32[1024,64]{0,1:T(8,128)S(1)}, f32[1024,64]{0,1:T(8,128)S(1)}, f32[1024,64]{0,1:T(8,128)S(1)}) fusion(s32[64]{0:T(128)S(1)} %multiply_add_fusion, s32[1024]{0:T(1024)S(1)} %fusion.33, s32[1024]{0:T(1024)S(1)} %iota_multiply_fusion), kind=kLoop, calls=%fused_computation.39 | loop fusion | flops 1835008 | bytes 1057024 | tf_op jit(solution)/shard_map/cos | solution.py:118
  33.8 0.3 collective-permute-start.1
  34.1 0.6 fusion.30
  34.7 1.4 multiply_subtract_fusion
  36.1 2.5 %bitcast_multiply_fusion = f32[1024,1024]{0,1:T(8,128)} fusion(f32[1024,16,64]{0,2,1:T(8,128)S(1)} %get-tuple-element.81, f32[1024]{0:T(1024)S(1)} %compare_select_fusion), kind=kLoop, calls=%fused_computation | loop fusion | flops 1048576 | bytes 8392704 | tf_op jit(solution)/shard_map/mul | solution.py:117
  38.6 2.4 %bitcast_multiply_fusion.1 = f32[1024,1024]{0,1:T(8,128)} fusion(f32[1024,16,64]{0,2,1:T(8,128)S(1)} %get-tuple-element.82, f32[1024]{0:T(1024)S(1)} %compare_select_fusion.1), kind=kLoop, calls=%fused_computation.1 | loop fusion | flops 1048576 | bytes 8392704 | tf_op jit(solution)/shard_map/mul | solution.py:117
  41.0 13.2 %shard_map.67 = (f32[4,128,32,128]{3,2,1,0:T(8,128)}, f32[32,32,128]{2,1,0:T(8,128)}, f32[128,32,128]{2,1,0:T(8,128)}, f32[32,32,128]{2,1,0:T(8,128)}) custom-call(s32[5]{0:T(128)} %stack.40.flags_ref, f32[32,32,128]{2,1,0:T(8,128)} %collective-permute-done.above_ref.below_ref, f32[128,32,128]{2,1,0:T(8,128)} %own_ref.7, ...), custom_call_target="tpu_custom_call" | custom-call | tf_op jit(solution)/shard_map/pallas_call | solution.py:268
  54.3 1.2 collective-permute-start.2
  55.5 2.5 %all-to-all-done = f32[128,16,256]{0,2,1:T(8,128)} async-done(((f32[128,16,256]{0,2,1:T(8,128)}), f32[128,16,256]{0,2,1:T(8,128)}, u32[]{:S(2)}, u32[]{:S(2)}) %all-to-all-start) | async-done | bytes 2097184 | tf_op jit(solution)/shard_map/all_to_all | solution.py:364
  58.0 2.9 %copy.29 = f32[16,128,1,256]{3,1,0,2:T(8,128)} copy(f32[16,128,1,256]{1,3,0,2:T(8,128)} %bitcast.6) | data formatting | bytes 4194304 | tf_op jit(solution)/shard_map/all_to_all | solution.py:364
  60.9 8.5 %collective-permute-done.1.above_ref.below_ref = f32[96,32,128]{2,1,0:T(8,128)S(1)} collective-permute-done((f32[96,32,128]{2,1,0:T(8,128)}, f32[96,32,128]{2,1,0:T(8,128)S(1)}, u32[]{:S(2)}, u32[]{:S(2)}) %collective-permute-start.1) | collective-permute-done | bytes 1572896 | tf_op jit(solution)/shard_map/ppermute | solution.py:307
  69.4 1.9 %slice.22 = f32[1024,256]{1,0:T(8,128)S(1)} slice(f32[2048,256]{1,0:T(8,128)} %bitcast.35), slice={[1024:2048], [0:256]} | slice | bytes 2097152 | tf_op jit(solution)/shard_map/slice | solution.py:143
  71.2 5.2 %rev.6 = f32[1024,256]{1,0:T(8,128)} reverse(f32[1024,256]{1,0:T(8,128)S(1)} %slice.22), dimensions={0} | reverse | bytes 2097152 | tf_op jit(solution)/shard_map/rev | solution.py:143
  76.4 5.2 %fusion.6 = f32[256,1024]{1,0:T(8,128)S(1)} fusion(f32[1024,1024]{0,1:T(8,128)} %bitcast_multiply_fusion, f32[256,1024,1]{1,0,2:T(8,128)} %copy.37, f32[1024,256]{1,0:T(8,128)} %rev.6, f32[2048,256]{1,0:T(8,128)} %bitcast.36), kind=kOutput, calls=%fused_computation.14 | convolution fusion | flops 1611661312 | bytes 8388608 | tf_op jit(solution)/shard_map/dot_general | solution.py:125
  81.6 0.0 copy-start.5
  81.6 1.8 %fusion.36 = f32[1024,256]{1,0:T(8,128)S(1)} fusion(f32[1024,1024]{0,1:T(8,128)S(1)} %copy-done.3, f32[256,1024]{1,0:T(8,128)S(1)} %fusion.6), kind=kOutput, calls=%fused_computation.70 | convolution fusion | flops 1610612736 | bytes 6291456 | tf_op jit(solution)/shard_map/dot_general | solution.py:156
  83.5 0.3 copy-done.4
  83.8 0.7 copy-done.5
  84.5 2.2 %fusion.8 = f32[256,1024]{1,0:T(8,128)S(1)} fusion(f32[1024,1024]{0,1:T(8,128)S(1)} %copy-done.4, f32[256,1024,1]{1,0,2:T(8,128)S(1)} %copy-done.7, f32[1024,256]{1,0:T(8,128)S(1)} %copy-done.6, f32[2048,256]{1,0:T(8,128)S(1)} %bitcast.37), kind=kOutput, calls=%fused_computation.17 | convolution fusion | flops 1611661312 | bytes 8388608 | tf_op jit(solution)/shard_map/dot_general | solution.py:125
  86.7 3.2 %fusion.34 = (f32[1024,256]{1,0:T(8,128)}, f32[1024,256]{1,0:T(8,128)}) fusion(f32[1024,256]{1,0:T(8,128)S(1)} %fusion.36, f32[1024,1024]{0,1:T(8,128)S(1)} %copy-done.4, f32[256,1024]{1,0:T(8,128)S(1)} %fusion.8), kind=kOutput, calls=%fused_computation.68 | convolution fusion | flops 1611137024 | bytes 8388608 | tf_op jit(solution)/shard_map/dot_general | solution.py:156
  89.9 6.8 %rev.7 = f32[1024,256]{1,0:T(8,128)S(1)} reverse(f32[1024,256]{1,0:T(8,128)} %get-tuple-element.65), dimensions={0} | reverse | bytes 2097152 | tf_op jit(solution)/shard_map/rev | solution.py:167
  96.7 2.7 %pad_maximum_fusion = f32[2048,256]{1,0:T(8,128)} fusion(f32[1024,256]{1,0:T(8,128)S(1)} %rev.7, f32[1024,256]{1,0:T(8,128)} %get-tuple-element.64), kind=kLoop, calls=%fused_computation.4 | loop fusion | flops 524288 | bytes 4194304 | tf_op jit(solution)/shard_map/concatenate | solution.py:167
  99.4 8.3 %all-to-all-start.1 = ((f32[16,128,256]{2,1,0:T(8,128)}), f32[16,128,256]{2,1,0:T(8,128)}, u32[]{:S(2)}, u32[]{:S(2)}) async-start(f32[16,128,256]{2,1,0:T(8,128)} %bitcast.41), calls=%async_computation.1 | async-start | bytes 4194304 | tf_op jit(solution)/shard_map/all_to_all | solution.py:378
  107.7 13.3 %shard_map.68 = (f32[4,128,32,128]{3,2,1,0:T(8,128)}, f32[32,32,128]{2,1,0:T(8,128)}, f32[128,32,128]{2,1,0:T(8,128)}, f32[32,32,128]{2,1,0:T(8,128)}) custom-call(s32[5]{0:T(128)} %stack.40.flags_ref, f32[96,32,128]{2,1,0:T(8,128)} %copy-done.2, f32[128,32,128]{2,1,0:T(8,128)} %own_ref.7, ...), custom_call_target="tpu_custom_call", output_to_operand_aliasing={{0}: (5, {}), {2}: (6, {})} | custom-call | tf_op jit(solution)/shard_map/pallas_call | solution.py:268
  121.0 0.3 collective-permute-start.3
  121.3 13.3 %shard_map.69 = (f32[4,128,32,128]{3,2,1,0:T(8,128)}, f32[32,32,128]{2,1,0:T(8,128)}, f32[128,32,128]{2,1,0:T(8,128)}, f32[32,32,128]{2,1,0:T(8,128)}) custom-call(s32[5]{0:T(128)} %stack.40.flags_ref, f32[96,32,128]{2,1,0:T(8,128)} %copy-done.2, f32[128,32,128]{2,1,0:T(8,128)} %own_ref.7, ...), custom_call_target="tpu_custom_call", output_to_operand_aliasing={{0}: (5, {}), {2}: (6, {})} | custom-call | tf_op jit(solution)/shard_map/pallas_call | solution.py:268
  134.6 13.3 %shard_map.70 = (f32[4,128,32,128]{3,2,1,0:T(8,128)}, f32[32,32,128]{2,1,0:T(8,128)}, f32[128,32,128]{2,1,0:T(8,128)}, f32[32,32,128]{2,1,0:T(8,128)}) custom-call(s32[5]{0:T(128)} %stack.40.flags_ref, f32[96,32,128]{2,1,0:T(8,128)} %copy-done.2, f32[128,32,128]{2,1,0:T(8,128)} %own_ref.7, ...), custom_call_target="tpu_custom_call", output_to_operand_aliasing={{0}: (5, {}), {2}: (6, {})} | custom-call | tf_op jit(solution)/shard_map/pallas_call | solution.py:268
  147.9 1.2 collective-permute-start.5
  149.1 0.3 collective-permute-start.4
  149.4 1.5 pad_maximum_fusion.1
  150.8 2.8 %copy.34 = f32[256,1024,2]{0,2,1:T(2,128)S(1)} copy(f32[256,1024,2]{1,0,2:T(8,128)} %pad_maximum_fusion.1) | data formatting | bytes 4194304 | tf_op jit(solution)/shard_map/stack | solution.py:150
  153.7 2.4 %reshape.330 = f32[256,2048]{0,1:T(8,128)} reshape(f32[256,1024,2]{0,2,1:T(2,128)S(1)} %copy.34) | data formatting | bytes 4194304 | tf_op jit(solution)/shard_map/reshape | solution.py:150
  156.1 2.9 %copy.35 = f32[256,2048]{1,0:T(8,128)} copy(f32[256,2048]{0,1:T(8,128)} %reshape.330) | data formatting | bytes 4194304
  159.0 4.1 %copy.33 = f32[1,128,16,256]{3,2,1,0:T(8,128)} copy(f32[1,128,16,256]{3,1,2,0:T(8,128)} %bitcast.14) | data formatting | bytes 4194304 | tf_op jit(solution)/shard_map/all_to_all | solution.py:378
  163.1 2.8 %reshape.329 = f32[128,32,128]{2,1,0:T(8,128)} reshape(f32[1,128,16,256]{3,2,1,0:T(8,128)} %copy.33) | data formatting | bytes 4194304 | tf_op jit(solution)/shard_map/reshape | solution.py:388
  165.9 6.4 %collective-permute-done.4 = f32[32,32,128]{2,1,0:T(8,128)} collective-permute-done((f32[32,32,128]{2,1,0:T(8,128)}, f32[32,32,128]{2,1,0:T(8,128)}, u32[]{:S(2)}, u32[]{:S(2)}) %collective-permute-start.4) | collective-permute-done | bytes 524320 | tf_op jit(solution)/shard_map/ppermute | solution.py:342
  172.3 5.7 %fusion.4 = f32[128,32,128]{2,1,0:T(8,128)} fusion(f32[128,32,128]{2,1,0:T(8,128)S(1)} %copy-done.1, f32[128,32,128]{2,1,0:T(8,128)} %reshape.329, f32[128,32,128]{2,1,0:T(8,128)} %param.5, f32[128,32,128]{2,1,0:T(8,128)} %get-tuple-element.48, f32[32,32,128]{2,1,0:T(8,128)S(1)} %collective-permute-done.5, f32[32,32,128]{2,1,0:T(8,128)} %collective-permute-done.4, ...), kind=kLoop, calls=%fused_computation.10 | loop fusion | flops 4718592 | bytes 12582912 | tf_op jit(solution)/shard_map/max | solution.py:389
  (24 shorter events, 0.1 us)
Async XLA Ops:
  3.6 6.7 %copy-start = (f32[128,32,128]{2,1,0:T(8,128)S(1)}, f32[128,32,128]{2,1,0:T(8,128)}, u32[]{:S(2)}) copy-start(f32[128,32,128]{2,1,0:T(8,128)} %own_ref.7) | copy-start | bytes 6291460
  3.6 54.4 %all-to-all-start = ((f32[128,16,256]{0,2,1:T(8,128)}), f32[128,16,256]{0,2,1:T(8,128)}, u32[]{:S(2)}, u32[]{:S(2)}) async-start(f32[128,16,256]{0,2,1:T(8,128)} %bitcast.40), calls=%async_computation | async-start | bytes 4194304 | tf_op jit(solution)/shard_map/all_to_all | solution.py:364
  11.1 22.6 %collective-permute-start = (f32[32,32,128]{2,1,0:T(8,128)}, f32[32,32,128]{2,1,0:T(8,128)}, u32[]{:S(2)}, u32[]{:S(2)}) collective-permute-start(f32[32,32,128]{2,1,0:T(8,128)} %slice.18), channel_id=1, source_target_pairs={{0,1},{1,0},{2,3},{3,2},{4,5},{5,4},{6,7},{7,6},{8,9},{9,8},{10,11... | collective-permute-start | bytes 1572872 | tf_op jit(solution)/shard_map/ppermute | solution.py:307
  33.8 35.6 %collective-permute-start.1 = (f32[96,32,128]{2,1,0:T(8,128)}, f32[96,32,128]{2,1,0:T(8,128)S(1)}, u32[]{:S(2)}, u32[]{:S(2)}) collective-permute-start(f32[96,32,128]{2,1,0:T(8,128)} %slice.19), channel_id=1, source_target_pairs={{0,1},{1,0},{2,3},{3,2},{4,5},{5,4},{6,7},{7,6},{8,9},{9,8},{10,11... | collective-permute-start | bytes 4718600 | tf_op jit(solution)/shard_map/ppermute | solution.py:307
  54.3 45.2 %collective-permute-start.2 = (f32[32,32,128]{2,1,0:T(8,128)}, f32[32,32,128]{2,1,0:T(8,128)}, u32[]{:S(2)}, u32[]{:S(2)}) collective-permute-start(f32[32,32,128]{2,1,0:T(8,128)} %get-tuple-element.41), channel_id=1, source_target_pairs={{0,1},{1,0},{2,3},{3,2},{4,5},{5,4},{6,7},{7,6},{8,9},{9,8},{10,11... | collective-permute-start | bytes 1572872 | tf_op jit(solution)/shard_map/ppermute | solution.py:342
  69.4 7.0 %copy-start.2 = (f32[96,32,128]{2,1,0:T(8,128)}, f32[96,32,128]{2,1,0:T(8,128)S(1)}, u32[]{:S(2)}) copy-start(f32[96,32,128]{2,1,0:T(8,128)S(1)} %collective-permute-done.1.above_ref.below_ref) | copy-start | bytes 4718596
  76.4 5.2 %copy-start.3 = (f32[1024,1024]{0,1:T(8,128)S(1)}, f32[1024,1024]{0,1:T(8,128)}, u32[]{:S(2)}) copy-start(f32[1024,1024]{0,1:T(8,128)} %bitcast_multiply_fusion) | copy-start | bytes 12582916
  76.4 7.1 %copy-start.6 = (f32[1024,256]{1,0:T(8,128)S(1)}, f32[1024,256]{1,0:T(8,128)}, u32[]{:S(2)}) copy-start(f32[1024,256]{1,0:T(8,128)} %rev.6) | copy-start | bytes 3145732
  76.4 7.1 %copy-start.7 = (f32[256,1024,1]{1,0,2:T(8,128)S(1)}, f32[256,1024,1]{1,0,2:T(8,128)}, u32[]{:S(2)}) copy-start(f32[256,1024,1]{1,0,2:T(8,128)} %copy.36) | copy-start | bytes 3145732
  81.6 2.2 %copy-start.4 = (f32[1024,1024]{0,1:T(8,128)S(1)}, f32[1024,1024]{0,1:T(8,128)}, u32[]{:S(2)}) copy-start(f32[1024,1024]{0,1:T(8,128)} %bitcast_multiply_fusion.1) | copy-start | bytes 12582916
  81.6 2.9 %copy-start.5 = (f32[16,128,1,256]{3,1,0,2:T(8,128)S(1)}, f32[16,128,1,256]{3,1,0,2:T(8,128)}, u32[]{:S(2)}) copy-start(f32[16,128,1,256]{3,1,0,2:T(8,128)} %copy.29) | copy-start | bytes 6291460
  99.4 59.6 %all-to-all-start.1 = ((f32[16,128,256]{2,1,0:T(8,128)}), f32[16,128,256]{2,1,0:T(8,128)}, u32[]{:S(2)}, u32[]{:S(2)}) async-start(f32[16,128,256]{2,1,0:T(8,128)} %bitcast.41), calls=%async_computation.1 | async-start | bytes 4194304 | tf_op jit(solution)/shard_map/all_to_all | solution.py:378
  121.0 44.9 %collective-permute-start.3 = (f32[32,32,128]{2,1,0:T(8,128)}, f32[32,32,128]{2,1,0:T(8,128)S(1)}, u32[]{:S(2)}, u32[]{:S(2)}) collective-permute-start(f32[32,32,128]{2,1,0:T(8,128)} %get-tuple-element.50), channel_id=1, source_target_pairs={{0,1},{1,0},{2,3},{3,2},{4,5},{5,4},{6,7},{7,6},{8,9},{9,8},{10,11... | collective-permute-start | bytes 1572872 | tf_op jit(solution)/shard_map/ppermute | solution.py:342
  147.9 18.0 %collective-permute-start.5 = (f32[32,32,128]{2,1,0:T(8,128)}, f32[32,32,128]{2,1,0:T(8,128)S(1)}, u32[]{:S(2)}, u32[]{:S(2)}) collective-permute-start(f32[32,32,128]{2,1,0:T(8,128)} %get-tuple-element.52), channel_id=1, source_target_pairs={{0,1},{1,0},{2,3},{3,2},{4,5},{5,4},{6,7},{7,6},{8,9},{9,8},{10,11... | collective-permute-start | bytes 1572872 | tf_op jit(solution)/shard_map/ppermute | solution.py:342
  149.1 23.2 %collective-permute-start.4 = (f32[32,32,128]{2,1,0:T(8,128)}, f32[32,32,128]{2,1,0:T(8,128)}, u32[]{:S(2)}, u32[]{:S(2)}) collective-permute-start(f32[32,32,128]{2,1,0:T(8,128)} %get-tuple-element.51), channel_id=1, source_target_pairs={{0,1},{1,0},{2,3},{3,2},{4,5},{5,4},{6,7},{7,6},{8,9},{9,8},{10,11... | collective-permute-start | bytes 1572872 | tf_op jit(solution)/shard_map/ppermute | solution.py:342
  163.1 9.2 %copy-start.1 = (f32[128,32,128]{2,1,0:T(8,128)S(1)}, f32[128,32,128]{2,1,0:T(8,128)}, u32[]{:S(2)}) copy-start(f32[128,32,128]{2,1,0:T(8,128)} %own_ref.7) | copy-start | bytes 6291460

commit v9 on v4

--- a/solution.py
+++ b/solution.py
@@ -16,7 +16,7 @@
 SPACE_BOUND = 0.5
 FREQ_BOUND = 1.0
 CHUNK = 8
-GROUPS = 4
+GROUPS = 2
 
 
 def padded_2(cells, sides, width):

time: 168 us -> 163 us (0.970)
  Pallas kernels: 53.3 us -> 48.9 us
  waiting for transfers between devices: 14.4 us -> 16.6 us
  starting transfers between devices: 19.7 us -> 17.9 us
    rev x1, local copies, waits for them, and re-layouts: 0.47 us -> 8.86 us  [spectral(): tail = pixel_cube[half:][::-1]]
    rev x1, local copies, waits for them, and re-layouts: 6.83 us -> 0.44 us  [spectral_back(): (parts[0] - parts[1])[::-1]]
    pallas_call x4 -> x2, Pallas kernels: 53.3 us -> 48.9 us  [starlet(): pl.pallas_call(starlet_kernel, grid=(steps,), in_specs=[pl.BlockSpec(memo...]
    all_to_all x1, waiting for transfers between devices: 9.99 us -> 12.3 us  [local(): lax.all_to_all(spectral_sum.reshape(peers, chans, share), 'freq', split_a...]
    unnamed x25 -> x27, local copies, waits for them, and re-layouts: 15.9 us -> 15.1 us
  transfers between devices with their start and end apart: 8 -> 6, of which waited for: 2 -> 2; matrix products, arithmetic and copies ran while one was open for 41% -> 43% of each run, Pallas kernels for 32% -> 30%
where the time goes in v9:
time: 163 us; the launch traced here: 162 us
  Pallas kernels  48.9 us (30%)
  local copies, waits for them, and re-layouts  47.2 us (29%)
  other arithmetic  18.9 us (12%)
  starting transfers between devices  17.9 us (11%)
  waiting for transfers between devices  16.6 us (10%)
  matrix products  11.8 us (7%)
    pallas_call x2, Pallas kernels, starlet(): pl.pallas_call(starlet_kernel, grid=(steps,), in_specs=[pl.BlockSpec(memo...  48.9 us
    unnamed x27, local copies, waits for them, and re-layouts  15.1 us
    all_to_all x1, waiting for transfers between devices, local(): lax.all_to_all(spectral_sum.reshape(peers, chans, share), 'freq', split_a...  12.3 us
    rev x1, local copies, waits for them, and re-layouts, spectral(): tail = pixel_cube[half:][::-1]  8.86 us
    all_to_all x1, starting transfers between devices, local(): lax.all_to_all(spectral_sum.reshape(peers, chans, share), 'freq', split_a...  7.3 us
    dot_general x2, matrix products, forward_dot(): lax.dot_general(samples, table, (((0,), (1,)), ((), ())), precision=lax.P...  7.12 us
    all_to_all x1, starting transfers between devices, local(): lax.all_to_all(pieces, 'freq', split_axis=1, concat_axis=0, tiled=True)  6.69 us
    max x1, other arithmetic, local(): jnp.maximum(image_cube - TAU_STEP * (data_grad + space_term + spectral_te...  5.75 us
  transfers between devices with their start and end apart: 6, of which 2 were waited for; matrix products, arithmetic and copies ran while one was open for 43% of the time, Pallas kernels for 30%

profile of v9, /device:TPU:13, one launch (start us, length us, event | category | flops | bytes accessed | tf_op | source)
XLA Modules:
  0.0 162.1 jit_solution(282198548663489304)
XLA Ops:
  0.6 3.0 %copy.24 = f32[128,32,128]{0,2,1:T(8,128)} copy(f32[128,32,128]{2,1,0:T(8,128)} %own_ref.3) | data formatting | bytes 4194304 | tf_op args[0]
  3.6 6.7 %all-to-all-start = ((f32[128,16,256]{0,2,1:T(8,128)}), f32[128,16,256]{0,2,1:T(8,128)}, u32[]{:S(2)}, u32[]{:S(2)}) async-start(f32[128,16,256]{0,2,1:T(8,128)} %bitcast.40), calls=%async_computation | async-start | bytes 4194304 | tf_op jit(solution)/shard_map/all_to_all | solution.py:364
  10.3 0.0 copy-done
  10.3 1.5 fusion.36
  11.8 1.2 collective-permute-start
  13.0 2.9 %copy.26 = f32[256,2048]{0,1:T(8,128)} copy(f32[256,2048]{1,0:T(8,128)} %param.7) | data formatting | bytes 4194304 | tf_op args[3]
  15.9 2.5 %reshape.327 = f32[256,1024,2]{0,2,1:T(2,128)S(1)} reshape(f32[256,2048]{0,1:T(8,128)} %copy.26) | data formatting | bytes 4194304 | tf_op jit(solution)/shard_map/reshape | solution.py:145
  18.4 2.9 %fusion.35 = (f32[256,1024,1]{0,2,1:T(1,128)}, f32[256,1024,1]{0,2,1:T(1,128)}) fusion(f32[256,1024,2]{0,2,1:T(2,128)S(1)} %reshape.327), kind=kLoop, calls=%fused_computation.69 | loop fusion | bytes 4194304 | tf_op jit(solution)/shard_map/slice | solution.py:147
  21.4 3.7 %copy.33 = f32[256,1024,1]{1,0,2:T(8,128)} copy(f32[256,1024,1]{0,2,1:T(1,128)} %get-tuple-element.46) | data formatting | bytes 2097152
  25.1 0.0 copy-done.9
  25.1 2.4 %copy.32 = f32[256,1024,1]{1,0,2:T(8,128)} copy(f32[256,1024,1]{0,2,1:T(1,128)S(1)} %copy-done.9) | data formatting | bytes 2097152
  27.5 0.6 stack.40.flags_ref
  28.2 0.6 fusion.30
  28.8 2.1 %fusion.20 = (f32[1024,64]{0,1:T(8,128)S(1)}, f32[1024,64]{0,1:T(8,128)S(1)}, f32[1024,64]{0,1:T(8,128)S(1)}, f32[1024,64]{0,1:T(8,128)S(1)}) fusion(s32[64]{0:T(128)S(1)} %multiply_add_fusion, s32[1024]{0:T(1024)S(1)} %fusion.33, s32[1024]{0:T(1024)S(1)} %iota_multiply_fusion), kind=kLoop, calls=%fused_computation.39 | loop fusion | flops 1835008 | bytes 1057024 | tf_op jit(solution)/shard_map/cos | solution.py:118
  30.9 1.4 multiply_subtract_fusion
  32.3 4.3 %collective-permute-done.above_ref.below_ref = f32[64,32,128]{2,1,0:T(8,128)S(1)} collective-permute-done((f32[64,32,128]{2,1,0:T(8,128)}, f32[64,32,128]{2,1,0:T(8,128)S(1)}, u32[]{:S(2)}, u32[]{:S(2)}) %collective-permute-start) | collective-permute-done | bytes 1048608 | tf_op jit(solution)/shard_map/ppermute | solution.py:307
  36.5 1.2 collective-permute-start.1
  37.8 2.4 %bitcast_multiply_fusion = f32[1024,1024]{0,1:T(8,128)} fusion(f32[1024,16,64]{0,2,1:T(8,128)S(1)} %get-tuple-element.63, f32[1024]{0:T(1024)S(1)} %compare_select_fusion), kind=kLoop, calls=%fused_computation | loop fusion | flops 1048576 | bytes 8392704 | tf_op jit(solution)/shard_map/mul | solution.py:117
  40.2 0.0 copy-done.7
  40.2 2.5 %bitcast_multiply_fusion.1 = f32[1024,1024]{0,1:T(8,128)} fusion(f32[1024,16,64]{0,2,1:T(8,128)S(1)} %get-tuple-element.64, f32[1024]{0:T(1024)S(1)} %compare_select_fusion.1), kind=kLoop, calls=%fused_computation.1 | loop fusion | flops 1048576 | bytes 8392704 | tf_op jit(solution)/shard_map/mul | solution.py:117
  42.7 24.3 %shard_map.67 = (f32[4,128,32,128]{3,2,1,0:T(8,128)}, f32[64,32,128]{2,1,0:T(8,128)}, f32[128,32,128]{2,1,0:T(8,128)}, f32[64,32,128]{2,1,0:T(8,128)}) custom-call(s32[5]{0:T(128)} %stack.40.flags_ref, f32[64,32,128]{2,1,0:T(8,128)} %copy-done.7, f32[128,32,128]{2,1,0:T(8,128)} %own_ref.3, f32[64,32,128]{2,1,0:T(8,128)} %copy-done.7, ...), custom_call_target="tpu_custom_call" | custom-call | tf_op jit(solution)/shard_map/pallas_call | solution.py:268
  67.0 0.3 collective-permute-start.2
  67.3 0.0 all-to-all-done
  67.3 1.9 %copy.25 = f32[16,128,1,256]{3,1,0,2:T(8,128)S(1)} copy(f32[16,128,1,256]{1,3,0,2:T(8,128)} %bitcast.6) | data formatting | bytes 4194304 | tf_op jit(solution)/shard_map/all_to_all | solution.py:364
  69.3 0.0 collective-permute-done.1.above_ref.below_ref
  69.3 0.0 copy-start.8
  69.3 1.1 slice.22
  70.4 0.2 copy-done.8
  70.6 8.9 %rev.6 = f32[1024,256]{1,0:T(8,128)} reverse(f32[1024,256]{1,0:T(8,128)} %slice.22), dimensions={0} | reverse | bytes 2097152 | tf_op jit(solution)/shard_map/rev | solution.py:143
  79.5 4.9 %fusion.6 = f32[256,1024]{1,0:T(8,128)S(1)} fusion(f32[1024,1024]{0,1:T(8,128)} %bitcast_multiply_fusion, f32[256,1024,1]{1,0,2:T(8,128)} %copy.33, f32[1024,256]{1,0:T(8,128)} %rev.6, f32[2048,256]{1,0:T(8,128)S(1)} %bitcast.36), kind=kOutput, calls=%fused_computation.14 | convolution fusion | flops 1611661312 | bytes 8388608 | tf_op jit(solution)/shard_map/dot_general | solution.py:125
  84.4 2.2 %fusion.8 = f32[256,1024]{1,0:T(8,128)S(1)} fusion(f32[1024,1024]{0,1:T(8,128)S(1)} %copy-done.3, f32[256,1024,1]{1,0,2:T(8,128)S(1)} %copy-done.10, f32[1024,256]{1,0:T(8,128)S(1)} %copy-done.4, f32[2048,256]{1,0:T(8,128)S(1)} %bitcast.37), kind=kOutput, calls=%fused_computation.17 | convolution fusion | flops 1611661312 | bytes 8388608 | tf_op jit(solution)/shard_map/dot_general | solution.py:125
  86.7 1.8 %fusion.37 = f32[1024,256]{1,0:T(8,128)S(1)} fusion(f32[1024,1024]{0,1:T(8,128)S(1)} %copy-done.2, f32[256,1024]{1,0:T(8,128)S(1)} %fusion.6), kind=kOutput, calls=%fused_computation.71 | convolution fusion | flops 1610612736 | bytes 6291456 | tf_op jit(solution)/shard_map/dot_general | solution.py:156
  88.5 2.8 %fusion.34 = (f32[1024,256]{1,0:T(8,128)}, f32[1024,256]{1,0:T(8,128)S(1)}) fusion(f32[1024,256]{1,0:T(8,128)S(1)} %fusion.37, f32[1024,1024]{0,1:T(8,128)S(1)} %copy-done.3, f32[256,1024]{1,0:T(8,128)S(1)} %fusion.8), kind=kOutput, calls=%fused_computation.68 | convolution fusion | flops 1611137024 | bytes 8388608 | tf_op jit(solution)/shard_map/dot_general | solution.py:156
  91.3 0.4 rev.7
  91.8 2.7 %pad_maximum_fusion = f32[2048,256]{1,0:T(8,128)} fusion(f32[1024,256]{1,0:T(8,128)S(1)} %rev.7, f32[1024,256]{1,0:T(8,128)} %get-tuple-element.44), kind=kLoop, calls=%fused_computation.4 | loop fusion | flops 524288 | bytes 4194304 | tf_op jit(solution)/shard_map/concatenate | solution.py:167
  94.5 0.0 collective-permute-done.2
  94.5 7.3 %all-to-all-start.1 = ((f32[16,128,256]{2,1,0:T(8,128)}), f32[16,128,256]{2,1,0:T(8,128)}, u32[]{:S(2)}, u32[]{:S(2)}) async-start(f32[16,128,256]{2,1,0:T(8,128)} %bitcast.12), calls=%async_computation.1 | async-start | bytes 4194304 | tf_op jit(solution)/shard_map/all_to_all | solution.py:378
  101.8 24.6 %shard_map.68 = (f32[4,128,32,128]{3,2,1,0:T(8,128)}, f32[64,32,128]{2,1,0:T(8,128)}, f32[128,32,128]{2,1,0:T(8,128)}, f32[64,32,128]{2,1,0:T(8,128)}) custom-call(s32[5]{0:T(128)} %stack.40.flags_ref, f32[64,32,128]{2,1,0:T(8,128)} %copy-done.8, f32[128,32,128]{2,1,0:T(8,128)} %own_ref.3, ...), custom_call_target="tpu_custom_call", output_to_operand_aliasing={{0}: (5, {}), {2}: (6, {})} | custom-call | tf_op jit(solution)/shard_map/pallas_call | solution.py:268
  126.3 1.2 collective-permute-start.3
  127.6 1.5 pad_maximum_fusion.1
  129.0 2.8 %copy.30 = f32[256,1024,2]{0,2,1:T(2,128)S(1)} copy(f32[256,1024,2]{1,0,2:T(8,128)} %pad_maximum_fusion.1) | data formatting | bytes 4194304 | tf_op jit(solution)/shard_map/stack | solution.py:150
  131.9 2.4 %reshape.330 = f32[256,2048]{0,1:T(8,128)} reshape(f32[256,1024,2]{0,2,1:T(2,128)S(1)} %copy.30) | data formatting | bytes 4194304 | tf_op jit(solution)/shard_map/reshape | solution.py:150
  134.3 2.9 %copy.31 = f32[256,2048]{1,0:T(8,128)} copy(f32[256,2048]{0,1:T(8,128)} %reshape.330) | data formatting | bytes 4194304
  137.2 12.3 %all-to-all-done.1 = f32[16,128,256]{2,1,0:T(8,128)} async-done(((f32[16,128,256]{2,1,0:T(8,128)}), f32[16,128,256]{2,1,0:T(8,128)}, u32[]{:S(2)}, u32[]{:S(2)}) %all-to-all-start.1) | async-done | bytes 2097184 | tf_op jit(solution)/shard_map/all_to_all | solution.py:378
  149.5 4.1 %copy.29 = f32[1,128,16,256]{3,2,1,0:T(8,128)} copy(f32[1,128,16,256]{3,1,2,0:T(8,128)} %bitcast.14) | data formatting | bytes 4194304 | tf_op jit(solution)/shard_map/all_to_all | solution.py:378
  153.6 2.8 %reshape.329 = f32[128,32,128]{2,1,0:T(8,128)} reshape(f32[1,128,16,256]{3,2,1,0:T(8,128)} %copy.29) | data formatting | bytes 4194304 | tf_op jit(solution)/shard_map/reshape | solution.py:388
  156.4 0.0 collective-permute-done.3
  156.4 5.8 %fusion.4 = f32[128,32,128]{2,1,0:T(8,128)} fusion(f32[128,32,128]{2,1,0:T(8,128)S(1)} %copy-done.1, f32[128,32,128]{2,1,0:T(8,128)} %reshape.329, f32[128,32,128]{2,1,0:T(8,128)} %param.5, f32[128,32,128]{2,1,0:T(8,128)} %get-tuple-element.30, f32[64,32,128]{2,1,0:T(8,128)S(1)} %collective-permute-done.3, f32[64,32,128]{2,1,0:T(8,128)} %collective-permute-done.2), kind=kLoop, calls=%fused_computation.10 | loop fusion | flops 3670016 | bytes 12582912 | tf_op jit(solution)/shard_map/max | solution.py:389
  (23 shorter events, 0.1 us)
Async XLA Ops:
  3.6 6.7 %copy-start = (f32[128,32,128]{2,1,0:T(8,128)S(1)}, f32[128,32,128]{2,1,0:T(8,128)}, u32[]{:S(2)}) copy-start(f32[128,32,128]{2,1,0:T(8,128)} %own_ref.3) | copy-start | bytes 6291460
  3.6 63.7 %all-to-all-start = ((f32[128,16,256]{0,2,1:T(8,128)}), f32[128,16,256]{0,2,1:T(8,128)}, u32[]{:S(2)}, u32[]{:S(2)}) async-start(f32[128,16,256]{0,2,1:T(8,128)} %bitcast.40), calls=%async_computation | async-start | bytes 4194304 | tf_op jit(solution)/shard_map/all_to_all | solution.py:364
  11.8 24.7 %collective-permute-start = (f32[64,32,128]{2,1,0:T(8,128)}, f32[64,32,128]{2,1,0:T(8,128)S(1)}, u32[]{:S(2)}, u32[]{:S(2)}) collective-permute-start(f32[64,32,128]{2,1,0:T(8,128)} %get-tuple-element.49), channel_id=1, source_target_pairs={{0,1},{1,0},{2,3},{3,2},{4,5},{5,4},{6,7},{7,6},{8,9},{9,8},{10,11... | collective-permute-start | bytes 3145736 | tf_op jit(solution)/shard_map/ppermute | solution.py:307
  21.4 3.7 %copy-start.9 = (f32[256,1024,1]{0,2,1:T(1,128)S(1)}, f32[256,1024,1]{0,2,1:T(1,128)}, u32[]{:S(2)}) copy-start(f32[256,1024,1]{0,2,1:T(1,128)} %get-tuple-element.47) | copy-start | bytes 3145732
  36.5 3.7 %copy-start.7 = (f32[64,32,128]{2,1,0:T(8,128)}, f32[64,32,128]{2,1,0:T(8,128)S(1)}, u32[]{:S(2)}) copy-start(f32[64,32,128]{2,1,0:T(8,128)S(1)} %collective-permute-done.above_ref.below_ref) | copy-start | bytes 3145732
  36.5 32.7 %collective-permute-start.1 = (f32[64,32,128]{2,1,0:T(8,128)}, f32[64,32,128]{2,1,0:T(8,128)S(1)}, u32[]{:S(2)}, u32[]{:S(2)}) collective-permute-start(f32[64,32,128]{2,1,0:T(8,128)} %get-tuple-element.21), channel_id=1, source_target_pairs={{0,1},{1,0},{2,3},{3,2},{4,5},{5,4},{6,7},{7,6},{8,9},{9,8},{10,11... | collective-permute-start | bytes 3145736 | tf_op jit(solution)/shard_map/ppermute | solution.py:307
  67.0 27.4 %collective-permute-start.2 = (f32[64,32,128]{2,1,0:T(8,128)}, f32[64,32,128]{2,1,0:T(8,128)}, u32[]{:S(2)}, u32[]{:S(2)}) collective-permute-start(f32[64,32,128]{2,1,0:T(8,128)} %get-tuple-element.27), channel_id=1, source_target_pairs={{0,1},{1,0},{2,3},{3,2},{4,5},{5,4},{6,7},{7,6},{8,9},{9,8},{10,11... | collective-permute-start | bytes 3145736 | tf_op jit(solution)/shard_map/ppermute | solution.py:342
  69.3 1.3 copy-start.8
  79.5 4.9 %copy-start.3 = (f32[1024,1024]{0,1:T(8,128)S(1)}, f32[1024,1024]{0,1:T(8,128)}, u32[]{:S(2)}) copy-start(f32[1024,1024]{0,1:T(8,128)} %bitcast_multiply_fusion.1) | copy-start | bytes 12582916
  79.5 4.9 %copy-start.4 = (f32[1024,256]{1,0:T(8,128)S(1)}, f32[1024,256]{1,0:T(8,128)}, u32[]{:S(2)}) copy-start(f32[1024,256]{1,0:T(8,128)} %rev.6) | copy-start | bytes 3145732
  79.5 4.9 %copy-start.10 = (f32[256,1024,1]{1,0,2:T(8,128)S(1)}, f32[256,1024,1]{1,0,2:T(8,128)}, u32[]{:S(2)}) copy-start(f32[256,1024,1]{1,0,2:T(8,128)} %copy.32) | copy-start | bytes 3145732
  84.4 2.2 %copy-start.2 = (f32[1024,1024]{0,1:T(8,128)S(1)}, f32[1024,1024]{0,1:T(8,128)}, u32[]{:S(2)}) copy-start(f32[1024,1024]{0,1:T(8,128)} %bitcast_multiply_fusion) | copy-start | bytes 12582916
  86.6 1.9 %copy-start.5 = (f32[256,1024]{1,0:T(8,128)}, f32[256,1024]{1,0:T(8,128)S(1)}, u32[]{:S(2)}) copy-start(f32[256,1024]{1,0:T(8,128)S(1)} %fusion.8) | copy-start | bytes 3145732
  94.5 55.0 %all-to-all-start.1 = ((f32[16,128,256]{2,1,0:T(8,128)}), f32[16,128,256]{2,1,0:T(8,128)}, u32[]{:S(2)}, u32[]{:S(2)}) async-start(f32[16,128,256]{2,1,0:T(8,128)} %bitcast.12), calls=%async_computation.1 | async-start | bytes 4194304 | tf_op jit(solution)/shard_map/all_to_all | solution.py:378
  101.8 25.8 %copy-start.6 = (f32[256,1024]{1,0:T(8,128)S(1)}, f32[256,1024]{1,0:T(8,128)}, u32[]{:S(2)}) copy-start(f32[256,1024]{1,0:T(8,128)} %copy-done.5) | copy-start | bytes 3145732
  126.3 30.0 %collective-permute-start.3 = (f32[64,32,128]{2,1,0:T(8,128)}, f32[64,32,128]{2,1,0:T(8,128)S(1)}, u32[]{:S(2)}, u32[]{:S(2)}) collective-permute-start(f32[64,32,128]{2,1,0:T(8,128)} %get-tuple-element.32), channel_id=1, source_target_pairs={{0,1},{1,0},{2,3},{3,2},{4,5},{5,4},{6,7},{7,6},{8,9},{9,8},{10,11... | collective-permute-start | bytes 3145736 | tf_op jit(solution)/shard_map/ppermute | solution.py:342
  153.6 2.8 %copy-start.1 = (f32[128,32,128]{2,1,0:T(8,128)S(1)}, f32[128,32,128]{2,1,0:T(8,128)}, u32[]{:S(2)}) copy-start(f32[128,32,128]{2,1,0:T(8,128)} %own_ref.3) | copy-start | bytes 6291460

commit v10 on v9

--- a/solution.py
+++ b/solution.py
@@ -15,7 +15,7 @@
 TAU_STEP = 0.5
 SPACE_BOUND = 0.5
 FREQ_BOUND = 1.0
-CHUNK = 8
+CHUNK = 4
 GROUPS = 2
 
 

time: 163 us -> 163 us (level)
  no operation moved by 1% of the time
where the time goes in v10:
time: 163 us; the launch traced here: 162 us
  Pallas kernels  47.8 us (29%)
  local copies, waits for them, and re-layouts  47.2 us (29%)
  other arithmetic  18.9 us (12%)
  starting transfers between devices  17.9 us (11%)
  waiting for transfers between devices  17.1 us (10%)
  matrix products  11.8 us (7%)
    pallas_call x2, Pallas kernels, starlet(): pl.pallas_call(starlet_kernel, grid=(steps,), in_specs=[pl.BlockSpec(memo...  47.8 us
    unnamed x27, local copies, waits for them, and re-layouts  15.1 us
    all_to_all x1, waiting for transfers between devices, local(): lax.all_to_all(spectral_sum.reshape(peers, chans, share), 'freq', split_a...  12.8 us
    rev x1, local copies, waits for them, and re-layouts, spectral(): tail = pixel_cube[half:][::-1]  8.86 us
    all_to_all x1, starting transfers between devices, local(): lax.all_to_all(spectral_sum.reshape(peers, chans, share), 'freq', split_a...  7.3 us
    dot_general x2, matrix products, forward_dot(): lax.dot_general(samples, table, (((0,), (1,)), ((), ())), precision=lax.P...  7.12 us
    all_to_all x1, starting transfers between devices, local(): lax.all_to_all(pieces, 'freq', split_axis=1, concat_axis=0, tiled=True)  6.69 us
    max x1, other arithmetic, local(): jnp.maximum(image_cube - TAU_STEP * (data_grad + space_term + spectral_te...  5.75 us
  transfers between devices with their start and end apart: 6, of which 2 were waited for; matrix products, arithmetic and copies ran while one was open for 43% of the time, Pallas kernels for 30%

profile of v10, /device:TPU:13, one launch (start us, length us, event | category | flops | bytes accessed | tf_op | source)
XLA Modules:
  0.0 161.6 jit_solution(7299827582391592726)
XLA Ops:
  0.6 3.0 %copy.24 = f32[128,32,128]{0,2,1:T(8,128)} copy(f32[128,32,128]{2,1,0:T(8,128)} %own_ref.3) | data formatting | bytes 4194304 | tf_op args[0]
  3.6 6.7 %all-to-all-start = ((f32[128,16,256]{0,2,1:T(8,128)}), f32[128,16,256]{0,2,1:T(8,128)}, u32[]{:S(2)}, u32[]{:S(2)}) async-start(f32[128,16,256]{0,2,1:T(8,128)} %bitcast.40), calls=%async_computation | async-start | bytes 4194304 | tf_op jit(solution)/shard_map/all_to_all | solution.py:364
  10.3 0.0 copy-done
  10.3 1.5 fusion.36
  11.8 1.2 collective-permute-start
  13.0 2.9 %copy.26 = f32[256,2048]{0,1:T(8,128)} copy(f32[256,2048]{1,0:T(8,128)} %param.7) | data formatting | bytes 4194304 | tf_op args[3]
  15.9 2.5 %reshape.327 = f32[256,1024,2]{0,2,1:T(2,128)S(1)} reshape(f32[256,2048]{0,1:T(8,128)} %copy.26) | data formatting | bytes 4194304 | tf_op jit(solution)/shard_map/reshape | solution.py:145
  18.4 2.9 %fusion.35 = (f32[256,1024,1]{0,2,1:T(1,128)}, f32[256,1024,1]{0,2,1:T(1,128)}) fusion(f32[256,1024,2]{0,2,1:T(2,128)S(1)} %reshape.327), kind=kLoop, calls=%fused_computation.69 | loop fusion | bytes 4194304 | tf_op jit(solution)/shard_map/slice | solution.py:147
  21.4 3.7 %copy.33 = f32[256,1024,1]{1,0,2:T(8,128)} copy(f32[256,1024,1]{0,2,1:T(1,128)} %get-tuple-element.46) | data formatting | bytes 2097152
  25.1 0.0 copy-done.9
  25.1 2.4 %copy.32 = f32[256,1024,1]{1,0,2:T(8,128)} copy(f32[256,1024,1]{0,2,1:T(1,128)S(1)} %copy-done.9) | data formatting | bytes 2097152
  27.5 0.6 stack.40.flags_ref
  28.2 0.6 fusion.30
  28.8 2.1 %fusion.20 = (f32[1024,64]{0,1:T(8,128)S(1)}, f32[1024,64]{0,1:T(8,128)S(1)}, f32[1024,64]{0,1:T(8,128)S(1)}, f32[1024,64]{0,1:T(8,128)S(1)}) fusion(s32[64]{0:T(128)S(1)} %multiply_add_fusion, s32[1024]{0:T(1024)S(1)} %fusion.33, s32[1024]{0:T(1024)S(1)} %iota_multiply_fusion), kind=kLoop, calls=%fused_computation.39 | loop fusion | flops 1835008 | bytes 1057024 | tf_op jit(solution)/shard_map/cos | solution.py:118
  30.9 1.4 multiply_subtract_fusion
  32.3 4.3 %collective-permute-done.above_ref.below_ref = f32[64,32,128]{2,1,0:T(8,128)S(1)} collective-permute-done((f32[64,32,128]{2,1,0:T(8,128)}, f32[64,32,128]{2,1,0:T(8,128)S(1)}, u32[]{:S(2)}, u32[]{:S(2)}) %collective-permute-start) | collective-permute-done | bytes 1048608 | tf_op jit(solution)/shard_map/ppermute | solution.py:307
  36.5 1.2 collective-permute-start.1
  37.8 2.4 %bitcast_multiply_fusion = f32[1024,1024]{0,1:T(8,128)} fusion(f32[1024,16,64]{0,2,1:T(8,128)S(1)} %get-tuple-element.63, f32[1024]{0:T(1024)S(1)} %compare_select_fusion), kind=kLoop, calls=%fused_computation | loop fusion | flops 1048576 | bytes 8392704 | tf_op jit(solution)/shard_map/mul | solution.py:117
  40.2 0.0 copy-done.7
  40.2 2.5 %bitcast_multiply_fusion.1 = f32[1024,1024]{0,1:T(8,128)} fusion(f32[1024,16,64]{0,2,1:T(8,128)S(1)} %get-tuple-element.64, f32[1024]{0:T(1024)S(1)} %compare_select_fusion.1), kind=kLoop, calls=%fused_computation.1 | loop fusion | flops 1048576 | bytes 8392704 | tf_op jit(solution)/shard_map/mul | solution.py:117
  42.7 23.8 %shard_map.67 = (f32[4,128,32,128]{3,2,1,0:T(8,128)}, f32[64,32,128]{2,1,0:T(8,128)}, f32[128,32,128]{2,1,0:T(8,128)}, f32[64,32,128]{2,1,0:T(8,128)}) custom-call(s32[5]{0:T(128)} %stack.40.flags_ref, f32[64,32,128]{2,1,0:T(8,128)} %copy-done.7, f32[128,32,128]{2,1,0:T(8,128)} %own_ref.3, f32[64,32,128]{2,1,0:T(8,128)} %copy-done.7, ...), custom_call_target="tpu_custom_call" | custom-call | tf_op jit(solution)/shard_map/pallas_call | solution.py:268
  66.5 0.3 collective-permute-start.2
  66.8 0.0 all-to-all-done
  66.8 1.9 %copy.25 = f32[16,128,1,256]{3,1,0,2:T(8,128)S(1)} copy(f32[16,128,1,256]{1,3,0,2:T(8,128)} %bitcast.6) | data formatting | bytes 4194304 | tf_op jit(solution)/shard_map/all_to_all | solution.py:364
  68.7 0.0 collective-permute-done.1.above_ref.below_ref
  68.7 0.0 copy-start.8
  68.8 1.1 slice.22
  69.9 0.2 copy-done.8
  70.1 8.9 %rev.6 = f32[1024,256]{1,0:T(8,128)} reverse(f32[1024,256]{1,0:T(8,128)} %slice.22), dimensions={0} | reverse | bytes 2097152 | tf_op jit(solution)/shard_map/rev | solution.py:143
  78.9 4.9 %fusion.6 = f32[256,1024]{1,0:T(8,128)S(1)} fusion(f32[1024,1024]{0,1:T(8,128)} %bitcast_multiply_fusion, f32[256,1024,1]{1,0,2:T(8,128)} %copy.33, f32[1024,256]{1,0:T(8,128)} %rev.6, f32[2048,256]{1,0:T(8,128)S(1)} %bitcast.36), kind=kOutput, calls=%fused_computation.14 | convolution fusion | flops 1611661312 | bytes 8388608 | tf_op jit(solution)/shard_map/dot_general | solution.py:125
  83.9 2.2 %fusion.8 = f32[256,1024]{1,0:T(8,128)S(1)} fusion(f32[1024,1024]{0,1:T(8,128)S(1)} %copy-done.3, f32[256,1024,1]{1,0,2:T(8,128)S(1)} %copy-done.10, f32[1024,256]{1,0:T(8,128)S(1)} %copy-done.4, f32[2048,256]{1,0:T(8,128)S(1)} %bitcast.37), kind=kOutput, calls=%fused_computation.17 | convolution fusion | flops 1611661312 | bytes 8388608 | tf_op jit(solution)/shard_map/dot_general | solution.py:125
  86.1 1.8 %fusion.37 = f32[1024,256]{1,0:T(8,128)S(1)} fusion(f32[1024,1024]{0,1:T(8,128)S(1)} %copy-done.2, f32[256,1024]{1,0:T(8,128)S(1)} %fusion.6), kind=kOutput, calls=%fused_computation.71 | convolution fusion | flops 1610612736 | bytes 6291456 | tf_op jit(solution)/shard_map/dot_general | solution.py:156
  88.0 2.8 %fusion.34 = (f32[1024,256]{1,0:T(8,128)}, f32[1024,256]{1,0:T(8,128)S(1)}) fusion(f32[1024,256]{1,0:T(8,128)S(1)} %fusion.37, f32[1024,1024]{0,1:T(8,128)S(1)} %copy-done.3, f32[256,1024]{1,0:T(8,128)S(1)} %fusion.8), kind=kOutput, calls=%fused_computation.68 | convolution fusion | flops 1611137024 | bytes 8388608 | tf_op jit(solution)/shard_map/dot_general | solution.py:156
  90.8 0.4 rev.7
  91.3 2.7 %pad_maximum_fusion = f32[2048,256]{1,0:T(8,128)} fusion(f32[1024,256]{1,0:T(8,128)S(1)} %rev.7, f32[1024,256]{1,0:T(8,128)} %get-tuple-element.44), kind=kLoop, calls=%fused_computation.4 | loop fusion | flops 524288 | bytes 4194304 | tf_op jit(solution)/shard_map/concatenate | solution.py:167
  93.9 0.0 collective-permute-done.2
  93.9 7.3 %all-to-all-start.1 = ((f32[16,128,256]{2,1,0:T(8,128)}), f32[16,128,256]{2,1,0:T(8,128)}, u32[]{:S(2)}, u32[]{:S(2)}) async-start(f32[16,128,256]{2,1,0:T(8,128)} %bitcast.12), calls=%async_computation.1 | async-start | bytes 4194304 | tf_op jit(solution)/shard_map/all_to_all | solution.py:378
  101.3 24.0 %shard_map.68 = (f32[4,128,32,128]{3,2,1,0:T(8,128)}, f32[64,32,128]{2,1,0:T(8,128)}, f32[128,32,128]{2,1,0:T(8,128)}, f32[64,32,128]{2,1,0:T(8,128)}) custom-call(s32[5]{0:T(128)} %stack.40.flags_ref, f32[64,32,128]{2,1,0:T(8,128)} %copy-done.8, f32[128,32,128]{2,1,0:T(8,128)} %own_ref.3, ...), custom_call_target="tpu_custom_call", output_to_operand_aliasing={{0}: (5, {}), {2}: (6, {})} | custom-call | tf_op jit(solution)/shard_map/pallas_call | solution.py:268
  125.3 1.2 collective-permute-start.3
  126.5 1.5 pad_maximum_fusion.1
  128.0 2.8 %copy.30 = f32[256,1024,2]{0,2,1:T(2,128)S(1)} copy(f32[256,1024,2]{1,0,2:T(8,128)} %pad_maximum_fusion.1) | data formatting | bytes 4194304 | tf_op jit(solution)/shard_map/stack | solution.py:150
  130.8 2.4 %reshape.330 = f32[256,2048]{0,1:T(8,128)} reshape(f32[256,1024,2]{0,2,1:T(2,128)S(1)} %copy.30) | data formatting | bytes 4194304 | tf_op jit(solution)/shard_map/reshape | solution.py:150
  133.3 2.9 %copy.31 = f32[256,2048]{1,0:T(8,128)} copy(f32[256,2048]{0,1:T(8,128)} %reshape.330) | data formatting | bytes 4194304
  136.1 12.8 %all-to-all-done.1 = f32[16,128,256]{2,1,0:T(8,128)} async-done(((f32[16,128,256]{2,1,0:T(8,128)}), f32[16,128,256]{2,1,0:T(8,128)}, u32[]{:S(2)}, u32[]{:S(2)}) %all-to-all-start.1) | async-done | bytes 2097184 | tf_op jit(solution)/shard_map/all_to_all | solution.py:378
  149.0 4.1 %copy.29 = f32[1,128,16,256]{3,2,1,0:T(8,128)} copy(f32[1,128,16,256]{3,1,2,0:T(8,128)} %bitcast.14) | data formatting | bytes 4194304 | tf_op jit(solution)/shard_map/all_to_all | solution.py:378
  153.1 2.8 %reshape.329 = f32[128,32,128]{2,1,0:T(8,128)} reshape(f32[1,128,16,256]{3,2,1,0:T(8,128)} %copy.29) | data formatting | bytes 4194304 | tf_op jit(solution)/shard_map/reshape | solution.py:388
  155.9 0.0 collective-permute-done.3
  155.9 5.8 %fusion.4 = f32[128,32,128]{2,1,0:T(8,128)} fusion(f32[128,32,128]{2,1,0:T(8,128)S(1)} %copy-done.1, f32[128,32,128]{2,1,0:T(8,128)} %reshape.329, f32[128,32,128]{2,1,0:T(8,128)} %param.5, f32[128,32,128]{2,1,0:T(8,128)} %get-tuple-element.30, f32[64,32,128]{2,1,0:T(8,128)S(1)} %collective-permute-done.3, f32[64,32,128]{2,1,0:T(8,128)} %collective-permute-done.2), kind=kLoop, calls=%fused_computation.10 | loop fusion | flops 3670016 | bytes 12582912 | tf_op jit(solution)/shard_map/max | solution.py:389
  (23 shorter events, 0.1 us)
Async XLA Ops:
  3.6 6.7 %copy-start = (f32[128,32,128]{2,1,0:T(8,128)S(1)}, f32[128,32,128]{2,1,0:T(8,128)}, u32[]{:S(2)}) copy-start(f32[128,32,128]{2,1,0:T(8,128)} %own_ref.3) | copy-start | bytes 6291460
  3.6 63.2 %all-to-all-start = ((f32[128,16,256]{0,2,1:T(8,128)}), f32[128,16,256]{0,2,1:T(8,128)}, u32[]{:S(2)}, u32[]{:S(2)}) async-start(f32[128,16,256]{0,2,1:T(8,128)} %bitcast.40), calls=%async_computation | async-start | bytes 4194304 | tf_op jit(solution)/shard_map/all_to_all | solution.py:364
  11.8 24.7 %collective-permute-start = (f32[64,32,128]{2,1,0:T(8,128)}, f32[64,32,128]{2,1,0:T(8,128)S(1)}, u32[]{:S(2)}, u32[]{:S(2)}) collective-permute-start(f32[64,32,128]{2,1,0:T(8,128)} %get-tuple-element.49), channel_id=1, source_target_pairs={{0,1},{1,0},{2,3},{3,2},{4,5},{5,4},{6,7},{7,6},{8,9},{9,8},{10,11... | collective-permute-start | bytes 3145736 | tf_op jit(solution)/shard_map/ppermute | solution.py:307
  21.4 3.7 %copy-start.9 = (f32[256,1024,1]{0,2,1:T(1,128)S(1)}, f32[256,1024,1]{0,2,1:T(1,128)}, u32[]{:S(2)}) copy-start(f32[256,1024,1]{0,2,1:T(1,128)} %get-tuple-element.47) | copy-start | bytes 3145732
  36.5 3.7 %copy-start.7 = (f32[64,32,128]{2,1,0:T(8,128)}, f32[64,32,128]{2,1,0:T(8,128)S(1)}, u32[]{:S(2)}) copy-start(f32[64,32,128]{2,1,0:T(8,128)S(1)} %collective-permute-done.above_ref.below_ref) | copy-start | bytes 3145732
  36.5 32.2 %collective-permute-start.1 = (f32[64,32,128]{2,1,0:T(8,128)}, f32[64,32,128]{2,1,0:T(8,128)S(1)}, u32[]{:S(2)}, u32[]{:S(2)}) collective-permute-start(f32[64,32,128]{2,1,0:T(8,128)} %get-tuple-element.21), channel_id=1, source_target_pairs={{0,1},{1,0},{2,3},{3,2},{4,5},{5,4},{6,7},{7,6},{8,9},{9,8},{10,11... | collective-permute-start | bytes 3145736 | tf_op jit(solution)/shard_map/ppermute | solution.py:307
  66.5 27.4 %collective-permute-start.2 = (f32[64,32,128]{2,1,0:T(8,128)}, f32[64,32,128]{2,1,0:T(8,128)}, u32[]{:S(2)}, u32[]{:S(2)}) collective-permute-start(f32[64,32,128]{2,1,0:T(8,128)} %get-tuple-element.27), channel_id=1, source_target_pairs={{0,1},{1,0},{2,3},{3,2},{4,5},{5,4},{6,7},{7,6},{8,9},{9,8},{10,11... | collective-permute-start | bytes 3145736 | tf_op jit(solution)/shard_map/ppermute | solution.py:342
  68.7 1.3 copy-start.8
  78.9 4.9 %copy-start.3 = (f32[1024,1024]{0,1:T(8,128)S(1)}, f32[1024,1024]{0,1:T(8,128)}, u32[]{:S(2)}) copy-start(f32[1024,1024]{0,1:T(8,128)} %bitcast_multiply_fusion.1) | copy-start | bytes 12582916
  78.9 4.9 %copy-start.4 = (f32[1024,256]{1,0:T(8,128)S(1)}, f32[1024,256]{1,0:T(8,128)}, u32[]{:S(2)}) copy-start(f32[1024,256]{1,0:T(8,128)} %rev.6) | copy-start | bytes 3145732
  78.9 4.9 %copy-start.10 = (f32[256,1024,1]{1,0,2:T(8,128)S(1)}, f32[256,1024,1]{1,0,2:T(8,128)}, u32[]{:S(2)}) copy-start(f32[256,1024,1]{1,0,2:T(8,128)} %copy.32) | copy-start | bytes 3145732
  83.9 2.2 %copy-start.2 = (f32[1024,1024]{0,1:T(8,128)S(1)}, f32[1024,1024]{0,1:T(8,128)}, u32[]{:S(2)}) copy-start(f32[1024,1024]{0,1:T(8,128)} %bitcast_multiply_fusion) | copy-start | bytes 12582916
  86.1 1.9 %copy-start.5 = (f32[256,1024]{1,0:T(8,128)}, f32[256,1024]{1,0:T(8,128)S(1)}, u32[]{:S(2)}) copy-start(f32[256,1024]{1,0:T(8,128)S(1)} %fusion.8) | copy-start | bytes 3145732
  93.9 55.0 %all-to-all-start.1 = ((f32[16,128,256]{2,1,0:T(8,128)}), f32[16,128,256]{2,1,0:T(8,128)}, u32[]{:S(2)}, u32[]{:S(2)}) async-start(f32[16,128,256]{2,1,0:T(8,128)} %bitcast.12), calls=%async_computation.1 | async-start | bytes 4194304 | tf_op jit(solution)/shard_map/all_to_all | solution.py:378
  101.2 25.3 %copy-start.6 = (f32[256,1024]{1,0:T(8,128)S(1)}, f32[256,1024]{1,0:T(8,128)}, u32[]{:S(2)}) copy-start(f32[256,1024]{1,0:T(8,128)} %copy-done.5) | copy-start | bytes 3145732
  125.3 30.6 %collective-permute-start.3 = (f32[64,32,128]{2,1,0:T(8,128)}, f32[64,32,128]{2,1,0:T(8,128)S(1)}, u32[]{:S(2)}, u32[]{:S(2)}) collective-permute-start(f32[64,32,128]{2,1,0:T(8,128)} %get-tuple-element.32), channel_id=1, source_target_pairs={{0,1},{1,0},{2,3},{3,2},{4,5},{5,4},{6,7},{7,6},{8,9},{9,8},{10,11... | collective-permute-start | bytes 3145736 | tf_op jit(solution)/shard_map/ppermute | solution.py:342
  153.1 2.8 %copy-start.1 = (f32[128,32,128]{2,1,0:T(8,128)S(1)}, f32[128,32,128]{2,1,0:T(8,128)}, u32[]{:S(2)}) copy-start(f32[128,32,128]{2,1,0:T(8,128)} %own_ref.3) | copy-start | bytes 6291460
